TPU v7x, 256 devices: a whole 4x4x8 slice. The times are simulated.
256 devices in a mesh: rows: 64 (over z, y, core), cols: 4 (over x).
Axes of the slice: x: 4, y: 4, z: 8, core: 2. Of those that a mesh axis runs over, the one named last changes fastest.
Arguments:
- images: bfloat16 [512, 360, 128], P('rows'), may hold values from -8 to 8
- partners: int32 [64, 8], P('rows'), may hold values from 0 to 7, each once within a row
- counts: int32 [64], P('rows'), may hold values from 1 to 8
- start: float32 [64, 24], P('rows'), may hold values from -6 to 6
Outputs:
- first_vec: float32 [64, 24], P('rows')
- second_vec: float32 [64, 24], P('rows')
Inputs may be any that keep to these rules, and one draw needn't show every extreme that they name: Each row of partners lists every code of 0 to 7 once; only its first counts[I] entries are pairs.
All inputs are finite; a program needn't handle non-finite values.
Results may differ from a plain program's by a relative error of at most 0.0003.
Values may be sent and summed in bfloat16 or wider, within the bound.
No kernel may reach another device: no remote copies, remote signals or barrier semaphores. Data moves between devices by JAX's collectives and lax.ppermute only.
A program may use at most 64 MiB of HBM per device.

v0:
```python
import math

import jax
import jax.numpy as jnp
from jax import lax
from jax.sharding import PartitionSpec as P

score_gain = 0.4
norm_eps = 1e-06


def shifted(block, axis, distance):
    devices = range(lax.axis_size(axis))
    route = [((i - distance) % len(devices), i) for i in devices]
    return lax.ppermute(block, axis, route)


def line_table(lines):
    angle = 2.0 * math.pi * jnp.arange(lines).astype(jnp.float32) / lines
    return jnp.stack([jnp.cos(angle), jnp.sin(angle), jnp.cos(2.0 * angle)], axis=1)


def pair_tile(own, other, table):
    count, lines, radii = own.shape
    others = other.shape[0]
    flat = other.reshape(others * lines, radii)

    def one_image(lines_a):
        scores = (
            lax.dot_general(
                lines_a, flat, (((1,), (1,)), ((), ())), preferred_element_type=jnp.float32
            )
            * score_gain
        )
        shaped = scores.reshape(lines, others, lines)
        top = jnp.max(shaped, axis=(0, 2))
        weights = jnp.exp(shaped - top[None, :, None])
        total = jnp.sum(weights, axis=(0, 2))
        left = jnp.einsum("lp,lbk->pbk", table, weights, precision=lax.Precision.HIGHEST)
        rel = jnp.einsum("pbk,kq->pbq", left, table, precision=lax.Precision.HIGHEST)
        return rel / total[None, :, None]

    stacked = lax.map(one_image, own)
    return jnp.transpose(stacked, (1, 0, 3, 2)).reshape(3 * count, 3 * others)


def block_offset(code, halo):
    return code - halo if code < halo else code - halo + 1


def body(images, partners, counts, start):
    count, lines, radii = images.shape
    width = 3 * count
    slots = partners.shape[1]
    halo = slots // 2
    ncols = lax.axis_size("cols")
    nblk = lax.axis_size("rows")
    slot_dev = slots // ncols
    column = lax.axis_index("cols")
    table = line_table(lines)
    fetched = []
    for code in range(2 * halo):
        fetched.append(shifted(images, "rows", -block_offset(code, halo)))
    band = jnp.stack(fetched)
    steps = jnp.arange(slot_dev)
    slot_ids = column * slot_dev + steps
    codes = partners[0][slot_ids]
    valid = slot_ids < counts[0]

    def slot_tile(index):
        other = lax.dynamic_index_in_dim(band, codes[index], 0, keepdims=False)
        return lax.cond(
            valid[index],
            lambda: pair_tile(images, other, table),
            lambda: jnp.zeros((width, width), jnp.float32),
        )

    tiles = lax.map(slot_tile, jnp.arange(slot_ids.shape[0]))

    def neighbours(vector):
        pieces = []
        for code in range(2 * halo):
            pieces.append(shifted(vector, "rows", -block_offset(code, halo))[0])
        return jnp.stack(pieces)[codes]

    def apply(vector):
        picked = neighbours(vector)
        products = jnp.einsum("svw,sw->sv", tiles, picked, precision=lax.Precision.HIGHEST)
        partial_value = jnp.sum(jnp.where(valid[:, None], products, 0.0), axis=0)
        return lax.psum(partial_value, "cols").reshape(1, width)

    entries = float(width * nblk)

    def normalize(raw):
        squares = lax.psum(jnp.sum(raw * raw), "rows")
        return raw / jnp.sqrt(squares / entries + norm_eps)

    first_vec = normalize(apply(start))
    second_vec = normalize(apply(first_vec))
    return (first_vec, second_vec)


def solution(mesh):
    in_specs = (P("rows", None, None), P("rows", None), P("rows"), P("rows", None))
    out_specs = (P("rows", None), P("rows", None))
    return jax.shard_map(body, mesh=mesh, in_specs=in_specs, out_specs=out_specs, check_vma=False)
```

profile of v0, /device:TPU:1, one launch (start us, length us, event | category | flops | bytes accessed | tf_op | source)
XLA Modules:
  0.0 764.3 jit_solution(13916237557707644937)
XLA Ops:
  0.6 3.8 collective-permute-start
  11.7 46.1 %collective-permute-done.10 = f32[1,24]{1,0:T(1,128)S(1)} collective-permute-done((f32[1,24]{1,0:T(1,128)}, f32[1,24]{1,0:T(1,128)S(1)}, u32[]{:S(2)}, u32[]{:S(2)}) %collective-permute-start.10) | collective-permute-done | bytes 128 | tf_op jit(solution)/shard_map/ppermute | solution.py:15
  66.5 3.8 collective-permute-start.9
  71.7 3.7 collective-permute-start.3
  77.1 3.4 collective-permute-start.5
  84.3 29.7 %collective-permute-done.4 = bf16[8,360,128]{2,1,0:T(8,128)(2,1)} collective-permute-done((bf16[8,360,128]{2,1,0:T(8,128)(2,1)}, bf16[8,360,128]{2,1,0:T(8,128)(2,1)}, u32[]{:S(2)}, u32[]{:S(2)}) %collective-permute-start.4) | collective-permute-done | bytes 737312 | tf_op jit(solution)/shard_map/ppermute | solution.py:15
  116.7 19.9 %collective-permute-done.6 = bf16[8,360,128]{2,1,0:T(8,128)(2,1)S(1)} collective-permute-done((bf16[8,360,128]{2,1,0:T(8,128)(2,1)}, bf16[8,360,128]{2,1,0:T(8,128)(2,1)S(1)}, u32[]{:S(2)}, u32[]{:S(2)}) %collective-permute-start.6) | collective-permute-done | bytes 737312 | tf_op jit(solution)/shard_map/ppermute | solution.py:15
  136.6 15.7 %collective-permute-done.7 = bf16[8,360,128]{2,1,0:T(8,128)(2,1)S(1)} collective-permute-done((bf16[8,360,128]{2,1,0:T(8,128)(2,1)}, bf16[8,360,128]{2,1,0:T(8,128)(2,1)S(1)}, u32[]{:S(2)}, u32[]{:S(2)}) %collective-permute-start.7) | collective-permute-done | bytes 737312 | tf_op jit(solution)/shard_map/ppermute | solution.py:15
  155.0 162.7 %while.26 = (s32[]{:T(128)}, f32[2,24,24]{2,1,0:T(8,128)S(1)}, s32[2]{0:T(128)S(1)}, pred[2]{0:T(512)(128)(4,1)S(1)}, s32[2]{0:T(128)S(1)}, /*index=5*/bf16[8,8,...) while((s32[]{:T(128)}, f32[2,24,24]{2,1,0:T(8,128)S(1)}, ...), condition=%wide.region_9.10_spmd, body=%wide.region_0.9_spmd.sunk | while | flops 308240704 | bytes 23313940 | solution.py:78
  158.9 154.9 %conditional.2 = (f32[1,24,24]{2,1,0:T(8,128)S(1)}) conditional(s32[]{:T(128)} %bitcast.73, () %tuple.53, (s32[2]{0:T(128)S(1)}, s32[]{:T(128)}, bf16[8,8,360,128]{3,2,1,0:T(8,128)(2,1)}, bf16[8,360,128]{2,1,0:T(8,128)(2,1)}, f32[360,3]{0,1:T(4,128)S(1)}) %tuple.54), branch_computations={%region_1.1_spmd, %region_2.8_spmd} | conditional | flops 308240704 | bytes 23289154 | solution.py:72
  162.8 150.8 %while.25 = (s32[]{:T(128)}, f32[8,3,8,3]{2,3,1,0:T(4,128)S(1)}, bf16[8,360,128]{2,1,0:T(8,128)(2,1)}, bf16[2880,128]{1,0:T(8,128)(2,1)S(1)}, f32[360,3]{0,1:T(4,128)S(1)}, /*index=5*/s32[]{:T(128)}, f32[]{:T(128)}, f32[]{:T(128)}) while((s32[]{:T(128)}, f32[8,3,8,3]{2,3,1,0:T(4,128)S(1)}, bf16[8,360,128]{2,1,0:T(8,128)(2,1)}, ...), condition=%wide.region_8.7_spmd, body=%wide.region_3.6_spmd.sunk | while | flops 308240704 | bytes 21805248 | solution.py:43
  162.8 3.7 fusion.40
  166.6 6.0 reshape.120
  172.8 5.3 fusion.41
  178.3 2.8 exponential_reduce_fusion.2
  181.7 3.8 fusion.40
  185.4 6.0 reshape.120
  191.6 5.3 fusion.41
  197.1 2.8 exponential_reduce_fusion.2
  200.5 3.8 fusion.40
  204.3 6.0 reshape.120
  210.5 5.3 fusion.41
  216.0 2.8 exponential_reduce_fusion.2
  219.4 3.8 fusion.40
  223.1 6.0 reshape.120
  229.4 5.3 fusion.41
  234.9 2.8 exponential_reduce_fusion.2
  238.2 3.8 fusion.40
  242.0 6.0 reshape.120
  248.2 5.3 fusion.41
  253.7 2.8 exponential_reduce_fusion.2
  257.1 3.7 fusion.40
  260.8 6.0 reshape.120
  267.0 5.3 fusion.41
  272.5 2.8 exponential_reduce_fusion.2
  275.9 3.8 fusion.40
  279.7 6.0 reshape.120
  285.9 5.3 fusion.41
  291.4 2.8 exponential_reduce_fusion.2
  294.8 3.8 fusion.40
  298.5 6.0 reshape.120
  304.7 5.3 fusion.41
  317.9 6.0 psum.28
  324.5 287.6 %psum.29 = f32[]{:T(128)} all-reduce(f32[]{:T(128)} %multiply_reduce_fusion.1), channel_id=1, replica_groups=mesh['rows'=64,'cols'=4] {'rows'}, use_global_device_ids=true, to_apply=%region_13.14 | all-reduce | flops 1 | bytes 8 | tf_op jit(solution)/shard_map/psum | solution.py:95
  613.9 5.0 collective-permute-done.16
  621.8 4.4 collective-permute-start.23
  627.9 7.7 %psum.30 = f32[24]{0:T(128)S(1)} all-reduce(f32[24]{0:T(128)S(1)} %select_reduce_fusion), channel_id=1, replica_groups=mesh['rows'=64,'cols'=4] {'cols'}, use_global_device_ids=true, to_apply=%region_15.16 | all-reduce | flops 24 | bytes 192 | tf_op jit(solution)/shard_map/psum | solution.py:90
  636.2 127.0 %psum.31 = f32[]{:T(128)} all-reduce(f32[]{:T(128)} %multiply_reduce_fusion), channel_id=1, replica_groups=mesh['rows'=64,'cols'=4] {'rows'}, use_global_device_ids=true, to_apply=%region_17.18 | all-reduce | flops 1 | bytes 8 | tf_op jit(solution)/shard_map/psum | solution.py:95
  (149 shorter events, 49.6 us)
Async XLA Ops:
  0.6 9.6 %copy-start = (s32[1,8]{1,0:T(1,128)S(1)}, s32[1,8]{1,0:T(1,128)}, u32[]{:S(2)}) copy-start(s32[1,8]{1,0:T(1,128)} %param.11) | copy-start | bytes 100
  0.6 76.5 %collective-permute-start = (bf16[8,360,128]{2,1,0:T(8,128)(2,1)}, bf16[8,360,128]{2,1,0:T(8,128)(2,1)S(1)}, u32[]{:S(2)}, u32[]{:S(2)}) collective-permute-start(bf16[8,360,128]{2,1,0:T(8,128)(2,1)} %param.10), channel_id=1, source_target_pairs={{240,0},{244,4},{248,8},{252,12},{0,16},{4,20},{8,24},{12,28},{16,... | collective-permute-start | bytes 2211848 | tf_op jit(solution)/shard_map/ppermute | solution.py:15
  4.5 76.1 %collective-permute-start.1 = (bf16[8,360,128]{2,1,0:T(8,128)(2,1)}, bf16[8,360,128]{2,1,0:T(8,128)(2,1)S(1)}, u32[]{:S(2)}, u32[]{:S(2)}) collective-permute-start(bf16[8,360,128]{2,1,0:T(8,128)(2,1)} %param.10), channel_id=1, source_target_pairs={{244,0},{248,4},{252,8},{0,12},{4,16},{8,20},{12,24},{16,28},{20,3... | collective-permute-start | bytes 2211848 | tf_op jit(solution)/shard_map/ppermute | solution.py:15
  6.7 74.0 %collective-permute-start.2 = (bf16[8,360,128]{2,1,0:T(8,128)(2,1)}, bf16[8,360,128]{2,1,0:T(8,128)(2,1)S(1)}, u32[]{:S(2)}, u32[]{:S(2)}) collective-permute-start(bf16[8,360,128]{2,1,0:T(8,128)(2,1)} %param.10), channel_id=1, source_target_pairs={{248,0},{252,4},{0,8},{4,12},{8,16},{12,20},{16,24},{20,28},{24,32... | collective-permute-start | bytes 2211848 | tf_op jit(solution)/shard_map/ppermute | solution.py:15
  8.0 49.8 %collective-permute-start.10 = (f32[1,24]{1,0:T(1,128)}, f32[1,24]{1,0:T(1,128)S(1)}, u32[]{:S(2)}, u32[]{:S(2)}) collective-permute-start(f32[1,24]{1,0:T(1,128)} %param.13), channel_id=1, source_target_pairs={{248,0},{252,4},{0,8},{4,12},{8,16},{12,20},{16,24},{20,28},{24,32... | collective-permute-start | bytes 296 | tf_op jit(solution)/shard_map/ppermute | solution.py:15
  9.3 49.9 %collective-permute-start.11 = (f32[1,24]{1,0:T(1,128)}, f32[1,24]{1,0:T(1,128)S(1)}, u32[]{:S(2)}, u32[]{:S(2)}) collective-permute-start(f32[1,24]{1,0:T(1,128)} %param.13), channel_id=1, source_target_pairs={{252,0},{0,4},{4,8},{8,12},{12,16},{16,20},{20,24},{24,28},{28,32}... | collective-permute-start | bytes 296 | tf_op jit(solution)/shard_map/ppermute | solution.py:15
  11.7 140.7 %copy-start.2 = (s32[1024]{0:T(1024)}, s32[1024]{0:T(1024)S(1)}, u32[]{:S(2)}) copy-start(s32[1024]{0:T(1024)S(1)} %pad_clamp_fusion) | copy-start | bytes 12292
  57.8 3.1 collective-permute-start.12
  59.2 3.2 collective-permute-start.13
  60.9 4.6 collective-permute-start.14
  62.4 4.1 collective-permute-start.15
  65.6 6.2 collective-permute-start.8
  66.5 9.5 %collective-permute-start.9 = (f32[1,24]{1,0:T(1,128)}, f32[1,24]{1,0:T(1,128)S(1)}, u32[]{:S(2)}, u32[]{:S(2)}) collective-permute-start(f32[1,24]{1,0:T(1,128)} %param.13), channel_id=1, source_target_pairs={{244,0},{248,4},{252,8},{0,12},{4,16},{8,20},{12,24},{16,28},{20,3... | collective-permute-start | bytes 296 | tf_op jit(solution)/shard_map/ppermute | solution.py:15
  71.7 12.4 %collective-permute-start.3 = (bf16[8,360,128]{2,1,0:T(8,128)(2,1)}, bf16[8,360,128]{2,1,0:T(8,128)(2,1)S(1)}, u32[]{:S(2)}, u32[]{:S(2)}) collective-permute-start(bf16[8,360,128]{2,1,0:T(8,128)(2,1)} %param.10), channel_id=1, source_target_pairs={{252,0},{0,4},{4,8},{8,12},{12,16},{16,20},{20,24},{24,28},{28,32}... | collective-permute-start | bytes 2211848 | tf_op jit(solution)/shard_map/ppermute | solution.py:15
  76.0 38.0 %collective-permute-start.4 = (bf16[8,360,128]{2,1,0:T(8,128)(2,1)}, bf16[8,360,128]{2,1,0:T(8,128)(2,1)}, u32[]{:S(2)}, u32[]{:S(2)}) collective-permute-start(bf16[8,360,128]{2,1,0:T(8,128)(2,1)} %param.10), channel_id=1, source_target_pairs={{4,0},{8,4},{12,8},{16,12},{20,16},{24,20},{28,24},{32,28},{36,32}... | collective-permute-start | bytes 2211848 | tf_op jit(solution)/shard_map/ppermute | solution.py:15
  77.1 39.5 %collective-permute-start.5 = (bf16[8,360,128]{2,1,0:T(8,128)(2,1)}, bf16[8,360,128]{2,1,0:T(8,128)(2,1)S(1)}, u32[]{:S(2)}, u32[]{:S(2)}) collective-permute-start(bf16[8,360,128]{2,1,0:T(8,128)(2,1)} %param.10), channel_id=1, source_target_pairs={{8,0},{12,4},{16,8},{20,12},{24,16},{28,20},{32,24},{36,28},{40,32... | collective-permute-start | bytes 2211848 | tf_op jit(solution)/shard_map/ppermute | solution.py:15
  80.5 56.0 %collective-permute-start.6 = (bf16[8,360,128]{2,1,0:T(8,128)(2,1)}, bf16[8,360,128]{2,1,0:T(8,128)(2,1)S(1)}, u32[]{:S(2)}, u32[]{:S(2)}) collective-permute-start(bf16[8,360,128]{2,1,0:T(8,128)(2,1)} %param.10), channel_id=1, source_target_pairs={{12,0},{16,4},{20,8},{24,12},{28,16},{32,20},{36,24},{40,28},{44,3... | collective-permute-start | bytes 2211848 | tf_op jit(solution)/shard_map/ppermute | solution.py:15
  80.7 71.6 %collective-permute-start.7 = (bf16[8,360,128]{2,1,0:T(8,128)(2,1)}, bf16[8,360,128]{2,1,0:T(8,128)(2,1)S(1)}, u32[]{:S(2)}, u32[]{:S(2)}) collective-permute-start(bf16[8,360,128]{2,1,0:T(8,128)(2,1)} %param.10), channel_id=1, source_target_pairs={{16,0},{20,4},{24,8},{28,12},{32,16},{36,20},{40,24},{44,28},{48,3... | collective-permute-start | bytes 2211848 | tf_op jit(solution)/shard_map/ppermute | solution.py:15
  152.4 2.5 copy-start.1
  155.0 162.7 %copy-start.3 = (f32[2,24]{1,0:T(2,128)S(1)}, f32[2,24]{1,0:T(2,128)}, u32[]{:S(2)}) copy-start(f32[2,24]{1,0:T(2,128)} %gather_fusion.1) | copy-start | bytes 580
  612.8 151.5 %copy-start.4 = (f32[1,24]{1,0:T(1,128)}, f32[1,24]{1,0:T(1,128)S(1)}, u32[]{:S(2)}) copy-start(f32[1,24]{1,0:T(1,128)S(1)} %divide_bitcast_fusion.1) | copy-start | bytes 292
  612.8 6.1 collective-permute-start.16
  612.9 6.4 collective-permute-start.17
  613.0 8.8 %collective-permute-start.18 = (f32[1,24]{1,0:T(1,128)S(1)}, f32[1,24]{1,0:T(1,128)S(1)}, u32[]{:S(2)}, u32[]{:S(2)}) collective-permute-start(f32[1,24]{1,0:T(1,128)S(1)} %divide_bitcast_fusion.1), channel_id=1, source_target_pairs={{248,0},{252,4},{0,8},{4,12},{8,16},{12,20},{16,24},{20,28},{24,32... | collective-permute-start | bytes 296 | tf_op jit(solution)/shard_map/ppermute | solution.py:15
  613.1 13.1 %collective-permute-start.19 = (f32[1,24]{1,0:T(1,128)S(1)}, f32[1,24]{1,0:T(1,128)S(1)}, u32[]{:S(2)}, u32[]{:S(2)}) collective-permute-start(f32[1,24]{1,0:T(1,128)S(1)} %divide_bitcast_fusion.1), channel_id=1, source_target_pairs={{252,0},{0,4},{4,8},{8,12},{12,16},{16,20},{20,24},{24,28},{28,32}... | collective-permute-start | bytes 296 | tf_op jit(solution)/shard_map/ppermute | solution.py:15
  613.2 13.0 %collective-permute-start.20 = (f32[1,24]{1,0:T(1,128)S(1)}, f32[1,24]{1,0:T(1,128)S(1)}, u32[]{:S(2)}, u32[]{:S(2)}) collective-permute-start(f32[1,24]{1,0:T(1,128)S(1)} %divide_bitcast_fusion.1), channel_id=1, source_target_pairs={{4,0},{8,4},{12,8},{16,12},{20,16},{24,20},{28,24},{32,28},{36,32}... | collective-permute-start | bytes 296 | tf_op jit(solution)/shard_map/ppermute | solution.py:15
  618.9 7.3 collective-permute-start.21
  619.3 6.9 collective-permute-start.22
  621.8 5.1 collective-permute-start.23
where the time goes:
time: 768 us; the launch traced here: 764 us
  blocking collectives  428 us (56%)
  waiting for transfers between devices  125 us (16%)
  matrix products  75.7 us (10%)
  local copies, waits for them, and re-layouts  62.1 us (8%)
  starting transfers between devices  36.7 us (5%)
  other arithmetic  26.4 us (3%)
  loops' own time  7.83 us (1%)
    psum x2, blocking collectives, normalize(): squares = lax.psum(jnp.sum(raw * raw), 'rows')  415 us
    ppermute x24, waiting for transfers between devices, shifted(): return lax.ppermute(block, axis, route)  125 us
    reshape x8, local copies, waits for them, and re-layouts, one_image(): shaped = scores.reshape(lines, others, lines)  48.2 us
    dot_general x8, matrix products, one_image(): jnp.einsum('lp,lbk->pbk', table, weights, precision=lax.Precision.HIGHEST)  42.7 us
    ppermute x24, starting transfers between devices, shifted(): return lax.ppermute(block, axis, route)  36.7 us
    dot_general x8, matrix products, one_image(): lax.dot_general(lines_a, flat, (((1,), (1,)), ((), ())), preferred_elemen...  30 us
    reduce_sum x16, other arithmetic, one_image(): total = jnp.sum(weights, axis=(0, 2))  23.3 us
  transfers between devices with their start and end apart: 24, of which 14 were waited for; matrix products, arithmetic and copies ran while one was open for 0% of the time, Pallas kernels for 0%

commit v1 on v0

v1 whole, which is shorter than its diff:
```python
import math

import jax
import jax.numpy as jnp
from jax import lax
from jax.experimental import pallas as pl
from jax.experimental.pallas import tpu as pltpu
from jax.sharding import PartitionSpec as P

score_gain = 0.4
norm_eps = 1e-06
HIGH = lax.Precision.HIGHEST


def line_table(lines):
    angle = 2.0 * math.pi * jnp.arange(lines).astype(jnp.float32) / lines
    return jnp.stack([jnp.cos(angle), jnp.sin(angle), jnp.cos(2.0 * angle)], axis=1)


def tile_kernel(a_ref, b_ref, w_ref, o_ref):
    n = a_ref.shape[0]

    def body(i, carry):
        a = i // n
        b = i % n
        s = lax.dot_general(
            b_ref[b], a_ref[a], (((1,), (1,)), ((), ())), preferred_element_type=jnp.float32
        )
        s = s * score_gain
        top = jnp.max(s, axis=0, keepdims=True)
        e = jnp.exp(s - top)
        o_ref[a, b, 0:1, :] = top
        o_ref[a, b, 1:2, :] = jnp.sum(e, axis=0, keepdims=True)
        o_ref[a, b, 2:3, :] = jnp.sum(e * w_ref[0], axis=0, keepdims=True)
        o_ref[a, b, 3:4, :] = jnp.sum(e * w_ref[1], axis=0, keepdims=True)
        o_ref[a, b, 4:5, :] = jnp.sum(e * w_ref[2], axis=0, keepdims=True)
        return carry

    lax.fori_loop(0, n * n, body, 0)


def pair_tile(own, other, table):
    count, lines, radii = own.shape
    padded = ((lines + 127) // 128) * 128
    own_p = jnp.pad(own, ((0, 0), (0, padded - lines), (0, 0)))
    wide = jnp.broadcast_to(jnp.transpose(table)[:, :, None], (3, lines, padded))
    stats = pl.pallas_call(
        tile_kernel,
        out_shape=jax.ShapeDtypeStruct((count, count, 8, padded), jnp.float32),
        in_specs=[pl.BlockSpec(memory_space=pltpu.VMEM)] * 3,
        out_specs=pl.BlockSpec(memory_space=pltpu.VMEM),
        compiler_params=pltpu.CompilerParams(vmem_limit_bytes=48 * 1024 * 1024),
    )(own_p, other, wide)
    stats = stats[:, :, :, :lines]
    top = stats[:, :, 0, :]
    peak = jnp.max(top, axis=2, keepdims=True)
    scale = jnp.exp(top - peak)
    total = jnp.sum(scale * stats[:, :, 1, :], axis=2)
    sums = stats[:, :, 2:5, :] * scale[:, :, None, :]
    rel = jnp.einsum("lp,abql->abpq", table, sums, precision=HIGH)
    rel = rel / total[:, :, None, None]
    return jnp.transpose(rel, (2, 0, 3, 1)).reshape(3 * count, 3 * count)


def body(images, partners, counts, start):
    count, lines, radii = images.shape
    width = 3 * count
    slots = partners.shape[1]
    halo = slots // 2
    ncols = lax.axis_size("cols")
    nblk = lax.axis_size("rows")
    row = lax.axis_index("rows")
    column = lax.axis_index("cols")
    step = column + 1
    table = line_table(lines)

    axes = ("rows", "cols")
    route = []
    for i in range(nblk):
        for c in range(ncols):
            route.append((((i + c + 1) % nblk) * ncols + c, i * ncols + c))
    fetch = lambda v: lax.ppermute(v, axes, route)
    other = fetch(images)
    other_partners = fetch(partners)
    other_counts = fetch(counts)
    other_start = fetch(start)

    tile = pair_tile(images, other, table)

    slot_ids = jnp.arange(slots)
    plus = jnp.any((partners[0] == step + halo - 1) & (slot_ids < counts[0]))
    minus = jnp.any((other_partners[0] == halo - step) & (slot_ids < other_counts[0]))
    partner_row = (row + step) % nblk
    rows_ids = jnp.arange(nblk)
    at_own = (rows_ids == row)[:, None]
    at_other = (rows_ids == partner_row)[:, None]

    def spread(x_own, x_other):
        forward = jnp.where(plus, jnp.dot(tile, x_other, precision=HIGH), 0.0)
        backward = jnp.where(minus, jnp.dot(tile.T, x_own, precision=HIGH), 0.0)
        part = jnp.where(at_own, forward[None, :], 0.0) + jnp.where(at_other, backward[None, :], 0.0)
        return lax.psum(part, axes)

    entries = float(width * nblk)

    def normalize(raw):
        return raw / jnp.sqrt(jnp.sum(raw * raw) / entries + norm_eps)

    first_all = normalize(spread(start[0], other_start[0]))
    first_own = lax.dynamic_index_in_dim(first_all, row, 0, keepdims=True)
    first_other = lax.dynamic_index_in_dim(first_all, partner_row, 0, keepdims=False)
    second_all = normalize(spread(first_own[0], first_other))
    second_own = lax.dynamic_index_in_dim(second_all, row, 0, keepdims=True)
    return (first_own, second_own)


def solution(mesh):
    in_specs = (P("rows", None, None), P("rows", None), P("rows"), P("rows", None))
    out_specs = (P("rows", None), P("rows", None))
    return jax.shard_map(body, mesh=mesh, in_specs=in_specs, out_specs=out_specs, check_vma=False)
```

time: 768 us -> 220 us (0.29)
  blocking collectives: 428 us -> 162 us
  waiting for transfers between devices: 125 us -> 0.01 us
  matrix products: 75.7 us -> 5.63 us
  local copies, waits for them, and re-layouts: 62.1 us -> 1.53 us
  Pallas kernels: 0 us -> 31.9 us
  starting transfers between devices: 36.7 us -> 10.2 us
  other arithmetic: 26.4 us -> 5.36 us
  loops' own time: 7.83 us -> 0 us
    psum x4 -> x2, blocking collectives: 428 us -> 162 us  [spread(): return lax.psum(part, axes)]
    ppermute x24 -> x4, waiting for transfers between devices: 125 us -> 0.01 us  [body(): fetch = lambda v: lax.ppermute(v, axes, route)]
    dot_general x26 -> x5, matrix products: 75.7 us -> 5.63 us  [the longest x1 2.68 us: pair_tile(): rel = jnp.einsum('lp,abql->abpq', table, sums, precision=HIGH)]
    reshape x8 -> x1, local copies, waits for them, and re-layouts: 48.2 us -> 0.09 us  [pair_tile(): return jnp.transpose(rel, (2, 0, 3, 1)).reshape(3 * count, 3 * count)]
    pallas_call x0 -> x1, Pallas kernels: none -> 31.9 us  [pair_tile(): pl.pallas_call(tile_kernel, out_shape=jax.ShapeDtypeStruct((count, count,...]
    ppermute x24 -> x4, starting transfers between devices: 36.7 us -> 10.2 us  [body(): fetch = lambda v: lax.ppermute(v, axes, route)]
    reduce_sum x20 -> x3, other arithmetic: 24.7 us -> 1.38 us  [the longest x2 1.21 us: normalize(): return raw / jnp.sqrt(jnp.sum(raw * raw) / entries + norm_eps)]
    another operation x4 -> x0, loops' own time: 7.83 us -> none  [the longest x1 5.3 us: body(): tiles = lax.map(slot_tile, jnp.arange(slot_ids.shape[0]))]
  transfers between devices with their start and end apart: 24 -> 4, of which waited for: 14 -> 0; matrix products, arithmetic and copies ran while one was open for 0% -> 4% of each run, Pallas kernels for 0% -> 15%
where the time goes in v1:
time: 220 us
  blocking collectives  162 us (74%)
  Pallas kernels  31.9 us (14%)
  starting transfers between devices  10.2 us (5%)
  matrix products  5.63 us (3%)
  other arithmetic  5.36 us (2%)
  between operations  2.82 us (1%)
    psum x2, blocking collectives, spread(): return lax.psum(part, axes)  162 us
    pallas_call x1, Pallas kernels, pair_tile(): pl.pallas_call(tile_kernel, out_shape=jax.ShapeDtypeStruct((count, count,...  31.9 us
    ppermute x4, starting transfers between devices, body(): fetch = lambda v: lax.ppermute(v, axes, route)  10.2 us
  transfers between devices with their start and end apart: 4, of which 0 were waited for; matrix products, arithmetic and copies ran while one was open for 4% of the time, Pallas kernels for 15%

profile of v1, /device:TPU:1, one launch (start us, length us, event | category | flops | bytes accessed | tf_op | source)
XLA Modules:
  0.0 219.6 jit_solution(1735947739061263379)
XLA Ops:
  0.6 3.3 %collective-permute-start = (bf16[8,360,128]{2,1,0:T(8,128)(2,1)}, bf16[8,360,128]{2,1,0:T(8,128)(2,1)S(1)}, u32[]{:S(2)}, u32[]{:S(2)}) collective-permute-start(bf16[8,360,128]{2,1,0:T(8,128)(2,1)} %param.4), channel_id=1, source_target_pairs={{4,0},{9,1},{14,2},{19,3},{8,4},{13,5},{18,6},{23,7},{12,8},{17,9}... | collective-permute-start | bytes 2211848 | tf_op jit(solution)/shard_map/ppermute | solution.py:82
  3.9 6.0 %collective-permute-start.2 = (s32[1,8]{1,0:T(1,128)}, s32[1,8]{1,0:T(1,128)S(1)}, u32[]{:S(2)}, u32[]{:S(2)}) collective-permute-start(s32[1,8]{1,0:T(1,128)} %param.5), channel_id=1, source_target_pairs={{4,0},{9,1},{14,2},{19,3},{8,4},{13,5},{18,6},{23,7},{12,8},{17,9}... | collective-permute-start | bytes 104 | tf_op jit(solution)/shard_map/ppermute | solution.py:82
  9.9 0.7 collective-permute-start.3
  10.6 0.2 collective-permute-start.1
  11.5 1.2 pad.4.a_ref
  12.7 0.1 fusion.15
  12.7 0.1 multiply_cosine_fusion
  12.8 1.3 fusion.13
  14.1 0.0 collective-permute-done.3
  14.2 0.0 collective-permute-done.2
  14.2 1.3 fusion.12
  15.5 0.0 collective-permute-done.b_ref
  15.5 0.2 broadcast_in_dim.72.w_ref
  15.7 31.9 %shard_map.59 = f32[8,8,8,384]{3,2,1,0:T(8,128)S(1)} custom-call(bf16[8,384,128]{2,1,0:T(8,128)(2,1)S(1)} %pad.4.a_ref, bf16[8,360,128]{2,1,0:T(8,128)(2,1)S(1)} %collective-permute-done.b_ref, f32[3,360,384]{2,1,0:T(8,128)S(1)} %broadcast_in_dim.72.w_ref), custom_call_target="tpu_custom_call" | custom-call | tf_op jit(solution)/shard_map/pallas_call | solution.py:47
  47.6 0.0 copy-start
  47.7 0.3 fusion.23
  47.9 0.1 exponential_bitcast_fusion
  48.0 0.1 slice_multiply_fusion
  48.1 0.2 fusion.6
  48.3 2.7 %fusion = f32[3,8,3,8]{3,0,2,1:T(4,128)S(1)} fusion(f32[8,8,3,360]{3,2,1,0:T(4,128)S(1)} %slice_multiply_fusion, f32[8,8]{1,0:T(8,128)S(1)} %fusion.6, f32[360,1]{0,1:T(1,128)S(1)} %get-tuple-element.5, f32[360,1]{0,1:T(1,128)S(1)} %get-tuple-element.6, f32[360,1]{0,1:T(1,128)S(1)} %fusion.15), kind=kOutput, calls=%fused_computation.1 | convolution fusion | flops 2491056 | bytes 283360 | tf_op jit(solution)/shard_map/lp,abql->abpq/dot_general | solution.py:60
  51.0 0.1 reshape.50
  51.1 0.0 copy-done
  51.1 0.8 fusion.2
  51.9 0.0 collective-permute-done.1
  51.9 0.7 fusion.1
  52.6 0.1 select_add_fusion.1
  52.7 89.2 %psum.14 = f32[64,24]{1,0:T(8,128)S(1)} all-reduce(f32[64,24]{1,0:T(8,128)S(1)} %select_add_fusion.1), channel_id=1, replica_groups=mesh['rows'=64,'cols'=4] {'rows','cols'}, use_global_device_ids=true, to_apply=%region_4.5 | all-reduce | flops 1536 | bytes 12288 | tf_op jit(solution)/shard_map/psum | solution.py:102
  141.9 0.6 multiply_reduce_fusion.1
  143.3 0.0 copy-start.1
  143.3 0.8 fusion.4
  144.1 0.7 fusion.3
  144.8 0.1 select_add_fusion
  144.9 72.9 %psum.15 = f32[64,24]{1,0:T(8,128)S(1)} all-reduce(f32[64,24]{1,0:T(8,128)S(1)} %select_add_fusion), channel_id=1, replica_groups=mesh['rows'=64,'cols'=4] {'rows','cols'}, use_global_device_ids=true, to_apply=%region_6.7 | all-reduce | flops 1536 | bytes 12288 | tf_op jit(solution)/shard_map/psum | solution.py:102
  217.8 0.6 multiply_reduce_fusion
  219.1 0.5 fusion.18
  219.6 0.0 copy-done.1
  (5 shorter events, 0.1 us)
Async XLA Ops:
  0.6 14.9 %collective-permute-start = (bf16[8,360,128]{2,1,0:T(8,128)(2,1)}, bf16[8,360,128]{2,1,0:T(8,128)(2,1)S(1)}, u32[]{:S(2)}, u32[]{:S(2)}) collective-permute-start(bf16[8,360,128]{2,1,0:T(8,128)(2,1)} %param.4), channel_id=1, source_target_pairs={{4,0},{9,1},{14,2},{19,3},{8,4},{13,5},{18,6},{23,7},{12,8},{17,9}... | collective-permute-start | bytes 2211848 | tf_op jit(solution)/shard_map/ppermute | solution.py:82
  3.9 10.3 %collective-permute-start.2 = (s32[1,8]{1,0:T(1,128)}, s32[1,8]{1,0:T(1,128)S(1)}, u32[]{:S(2)}, u32[]{:S(2)}) collective-permute-start(s32[1,8]{1,0:T(1,128)} %param.5), channel_id=1, source_target_pairs={{4,0},{9,1},{14,2},{19,3},{8,4},{13,5},{18,6},{23,7},{12,8},{17,9}... | collective-permute-start | bytes 104 | tf_op jit(solution)/shard_map/ppermute | solution.py:82
  9.9 4.2 %collective-permute-start.3 = (s32[1]{0:T(128)}, s32[1]{0:T(128)}, u32[]{:S(2)}, u32[]{:S(2)}) collective-permute-start(s32[1]{0:T(128)} %param.6), channel_id=1, source_target_pairs={{4,0},{9,1},{14,2},{19,3},{8,4},{13,5},{18,6},{23,7},{12,8},{17,9}... | collective-permute-start | bytes 20 | tf_op jit(solution)/shard_map/ppermute | solution.py:82
  10.6 41.3 %collective-permute-start.1 = (f32[1,24]{1,0:T(1,128)}, f32[1,24]{1,0:T(1,128)S(1)}, u32[]{:S(2)}, u32[]{:S(2)}) collective-permute-start(f32[1,24]{1,0:T(1,128)} %param.7), channel_id=1, source_target_pairs={{4,0},{9,1},{14,2},{19,3},{8,4},{13,5},{18,6},{23,7},{12,8},{17,9}... | collective-permute-start | bytes 296 | tf_op jit(solution)/shard_map/ppermute | solution.py:82
  47.6 3.5 %copy-start = (f32[1,24]{1,0:T(1,128)S(1)}, f32[1,24]{1,0:T(1,128)}, u32[]{:S(2)}) copy-start(f32[1,24]{1,0:T(1,128)} %param.7) | copy-start | bytes 292
  143.3 76.3 %copy-start.1 = (f32[1,24]{1,0:T(1,128)}, f32[1,24]{1,0:T(1,128)S(1)}, u32[]{:S(2)}) copy-start(f32[1,24]{1,0:T(1,128)S(1)} %constant_dynamic-slice_fusion.2) | copy-start | bytes 292

commit v2 on v1

--- a/solution.py
+++ b/solution.py
@@ -62,6 +62,15 @@
     return jnp.transpose(rel, (2, 0, 3, 1)).reshape(3 * count, 3 * count)
 
 
+def butterfly_sum(value, axes, size):
+    bit = 1
+    while bit < size:
+        route = [(i, i ^ bit) for i in range(size)]
+        value = value + lax.ppermute(value, axes, route)
+        bit *= 2
+    return value
+
+
 def body(images, partners, counts, start):
     count, lines, radii = images.shape
     width = 3 * count
@@ -99,7 +108,7 @@
         forward = jnp.where(plus, jnp.dot(tile, x_other, precision=HIGH), 0.0)
         backward = jnp.where(minus, jnp.dot(tile.T, x_own, precision=HIGH), 0.0)
         part = jnp.where(at_own, forward[None, :], 0.0) + jnp.where(at_other, backward[None, :], 0.0)
-        return lax.psum(part, axes)
+        return butterfly_sum(part, axes, nblk * ncols)
 
     entries = float(width * nblk)
 

time: 220 us -> 143 us (0.65)
  the two profiles are of different devices: /device:TPU:1 before, /device:TPU:4 now
where the time goes in v2:
time: 143 us
  waiting for transfers between devices  70.9 us (50%)
  Pallas kernels  31.9 us (22%)
  starting transfers between devices  24.4 us (17%)
  matrix products  5.78 us (4%)
  other arithmetic  5.72 us (4%)
  between operations  2.92 us (2%)
  local copies, waits for them, and re-layouts  1.53 us (1%)
    ppermute x16, waiting for transfers between devices, butterfly_sum(): value = value + lax.ppermute(value, axes, route)  61.1 us
    pallas_call x1, Pallas kernels, pair_tile(): pl.pallas_call(tile_kernel, out_shape=jax.ShapeDtypeStruct((count, count,...  31.9 us
    ppermute x16, starting transfers between devices, butterfly_sum(): value = value + lax.ppermute(value, axes, route)  12.5 us
    ppermute x4, starting transfers between devices, body(): fetch = lambda v: lax.ppermute(v, axes, route)  11.9 us
    ppermute x4, waiting for transfers between devices, body(): fetch = lambda v: lax.ppermute(v, axes, route)  9.72 us
  transfers between devices with their start and end apart: 20, of which 17 were waited for; matrix products, arithmetic and copies ran while one was open for 6% of the time, Pallas kernels for 22%

profile of v2, /device:TPU:4, one launch (start us, length us, event | category | flops | bytes accessed | tf_op | source)
XLA Modules:
  0.0 143.2 jit_solution(6450836113612613439)
XLA Ops:
  0.6 8.0 %collective-permute-start = (bf16[8,360,128]{2,1,0:T(8,128)(2,1)}, bf16[8,360,128]{2,1,0:T(8,128)(2,1)S(1)}, u32[]{:S(2)}, u32[]{:S(2)}) collective-permute-start(bf16[8,360,128]{2,1,0:T(8,128)(2,1)} %param.4), channel_id=1, source_target_pairs={{4,0},{9,1},{14,2},{19,3},{8,4},{13,5},{18,6},{23,7},{12,8},{17,9}... | collective-permute-start | bytes 2211848 | tf_op jit(solution)/shard_map/ppermute | solution.py:91
  8.6 0.7 collective-permute-start.2
  9.4 2.2 %collective-permute-start.3 = (s32[1]{0:T(128)}, s32[1]{0:T(128)}, u32[]{:S(2)}, u32[]{:S(2)}) collective-permute-start(s32[1]{0:T(128)} %param.6), channel_id=1, source_target_pairs={{4,0},{9,1},{14,2},{19,3},{8,4},{13,5},{18,6},{23,7},{12,8},{17,9}... | collective-permute-start | bytes 20 | tf_op jit(solution)/shard_map/ppermute | solution.py:91
  11.5 1.0 collective-permute-start.1
  13.2 1.2 pad.4.a_ref
  14.5 0.1 multiply_cosine_fusion
  14.6 1.3 fusion.15
  15.9 9.7 %collective-permute-done.3 = s32[1]{0:T(128)} collective-permute-done((s32[1]{0:T(128)}, s32[1]{0:T(128)}, u32[]{:S(2)}, u32[]{:S(2)}) %collective-permute-start.3) | collective-permute-done | bytes 36 | tf_op jit(solution)/shard_map/ppermute | solution.py:91
  25.7 1.3 fusion.14
  26.9 0.2 broadcast_in_dim.72.w_ref
  27.1 31.9 %shard_map.59 = f32[8,8,8,384]{3,2,1,0:T(8,128)S(1)} custom-call(bf16[8,384,128]{2,1,0:T(8,128)(2,1)S(1)} %pad.4.a_ref, bf16[8,360,128]{2,1,0:T(8,128)(2,1)S(1)} %collective-permute-done.b_ref, f32[3,360,384]{2,1,0:T(8,128)S(1)} %broadcast_in_dim.72.w_ref), custom_call_target="tpu_custom_call" | custom-call | tf_op jit(solution)/shard_map/pallas_call | solution.py:47
  59.1 0.3 fusion.25
  59.4 0.1 slice_multiply_fusion
  59.6 0.2 fusion.6
  59.7 2.7 %fusion = f32[3,8,3,8]{3,0,2,1:T(4,128)S(1)} fusion(f32[8,8,3,360]{3,2,1,0:T(4,128)S(1)} %slice_multiply_fusion, f32[8,8]{1,0:T(8,128)S(1)} %fusion.6, f32[360,1]{0,1:T(1,128)S(1)} %get-tuple-element.9, f32[360,1]{0,1:T(1,128)S(1)} %get-tuple-element.10, f32[360,1]{0,1:T(1,128)S(1)} %fusion.17), kind=kOutput, calls=%fused_computation.1 | convolution fusion | flops 2491056 | bytes 283360 | tf_op jit(solution)/shard_map/lp,abql->abpq/dot_general | solution.py:60
  62.5 0.8 fusion.2
  63.3 0.8 fusion.1
  64.1 0.1 select_add_fusion.1
  64.2 0.9 collective-permute-start.4
  65.1 3.1 %collective-permute-done.4 = f32[64,24]{1,0:T(8,128)S(1)} collective-permute-done((f32[64,24]{1,0:T(8,128)S(1)}, f32[64,24]{1,0:T(8,128)S(1)}, u32[]{:S(2)}, u32[]{:S(2)}) %collective-permute-start.4) | collective-permute-done | bytes 6176 | tf_op jit(solution)/shard_map/ppermute | solution.py:69
  68.3 0.1 collective-permute-start.5
  68.4 5.4 %collective-permute-done.5 = f32[64,24]{1,0:T(8,128)S(1)} collective-permute-done((f32[64,24]{1,0:T(8,128)S(1)}, f32[64,24]{1,0:T(8,128)S(1)}, u32[]{:S(2)}, u32[]{:S(2)}) %collective-permute-start.5) | collective-permute-done | bytes 6176 | tf_op jit(solution)/shard_map/ppermute | solution.py:69
  73.9 0.1 collective-permute-start.6
  74.0 1.2 collective-permute-done.6
  75.2 3.9 %collective-permute-done.7 = f32[64,24]{1,0:T(8,128)S(1)} collective-permute-done((f32[64,24]{1,0:T(8,128)S(1)}, f32[64,24]{1,0:T(8,128)S(1)}, u32[]{:S(2)}, u32[]{:S(2)}) %collective-permute-start.7) | collective-permute-done | bytes 6176 | tf_op jit(solution)/shard_map/ppermute | solution.py:69
  79.1 5.4 %collective-permute-done.8 = f32[64,24]{1,0:T(8,128)S(1)} collective-permute-done((f32[64,24]{1,0:T(8,128)S(1)}, f32[64,24]{1,0:T(8,128)S(1)}, u32[]{:S(2)}, u32[]{:S(2)}) %collective-permute-start.8) | collective-permute-done | bytes 6176 | tf_op jit(solution)/shard_map/ppermute | solution.py:69
  84.5 3.9 %collective-permute-done.9 = f32[64,24]{1,0:T(8,128)S(1)} collective-permute-done((f32[64,24]{1,0:T(8,128)S(1)}, f32[64,24]{1,0:T(8,128)S(1)}, u32[]{:S(2)}, u32[]{:S(2)}) %collective-permute-start.9) | collective-permute-done | bytes 6176 | tf_op jit(solution)/shard_map/ppermute | solution.py:69
  88.5 4.8 %collective-permute-done.10 = f32[64,24]{1,0:T(8,128)S(1)} collective-permute-done((f32[64,24]{1,0:T(8,128)S(1)}, f32[64,24]{1,0:T(8,128)S(1)}, u32[]{:S(2)}, u32[]{:S(2)}) %collective-permute-start.10) | collective-permute-done | bytes 6176 | tf_op jit(solution)/shard_map/ppermute | solution.py:69
  93.3 3.5 %collective-permute-start.11 = (f32[64,24]{1,0:T(8,128)S(1)}, f32[64,24]{1,0:T(8,128)S(1)}, u32[]{:S(2)}, u32[]{:S(2)}) collective-permute-start(f32[64,24]{1,0:T(8,128)S(1)} %add.97), channel_id=1, source_target_pairs={{0,128},{1,129},{2,130},{3,131},{4,132},{5,133},{6,134},{7,135},{8... | collective-permute-start | bytes 18440 | tf_op jit(solution)/shard_map/ppermute | solution.py:69
  96.8 4.3 %collective-permute-done.11 = f32[64,24]{1,0:T(8,128)S(1)} collective-permute-done((f32[64,24]{1,0:T(8,128)S(1)}, f32[64,24]{1,0:T(8,128)S(1)}, u32[]{:S(2)}, u32[]{:S(2)}) %collective-permute-start.11) | collective-permute-done | bytes 6176 | tf_op jit(solution)/shard_map/ppermute | solution.py:69
  101.1 0.6 multiply_reduce_fusion.1
  102.5 0.8 fusion.4
  103.2 0.8 fusion.3
  104.0 0.1 select_add_fusion
  104.1 0.9 collective-permute-start.12
  105.0 3.1 %collective-permute-done.12 = f32[64,24]{1,0:T(8,128)S(1)} collective-permute-done((f32[64,24]{1,0:T(8,128)S(1)}, f32[64,24]{1,0:T(8,128)S(1)}, u32[]{:S(2)}, u32[]{:S(2)}) %collective-permute-start.12) | collective-permute-done | bytes 6176 | tf_op jit(solution)/shard_map/ppermute | solution.py:69
  108.3 5.4 %collective-permute-done.13 = f32[64,24]{1,0:T(8,128)S(1)} collective-permute-done((f32[64,24]{1,0:T(8,128)S(1)}, f32[64,24]{1,0:T(8,128)S(1)}, u32[]{:S(2)}, u32[]{:S(2)}) %collective-permute-start.13) | collective-permute-done | bytes 6176 | tf_op jit(solution)/shard_map/ppermute | solution.py:69
  113.9 1.2 collective-permute-done.14
  115.1 3.9 %collective-permute-done.15 = f32[64,24]{1,0:T(8,128)S(1)} collective-permute-done((f32[64,24]{1,0:T(8,128)S(1)}, f32[64,24]{1,0:T(8,128)S(1)}, u32[]{:S(2)}, u32[]{:S(2)}) %collective-permute-start.15) | collective-permute-done | bytes 6176 | tf_op jit(solution)/shard_map/ppermute | solution.py:69
  119.0 1.8 %collective-permute-start.16 = (f32[64,24]{1,0:T(8,128)S(1)}, f32[64,24]{1,0:T(8,128)S(1)}, u32[]{:S(2)}, u32[]{:S(2)}) collective-permute-start(f32[64,24]{1,0:T(8,128)S(1)} %add.106), channel_id=1, source_target_pairs={{0,16},{1,17},{2,18},{3,19},{4,20},{5,21},{6,22},{7,23},{8,24},{9,... | collective-permute-start | bytes 18440 | tf_op jit(solution)/shard_map/ppermute | solution.py:69
  120.8 3.6 %collective-permute-done.16 = f32[64,24]{1,0:T(8,128)S(1)} collective-permute-done((f32[64,24]{1,0:T(8,128)S(1)}, f32[64,24]{1,0:T(8,128)S(1)}, u32[]{:S(2)}, u32[]{:S(2)}) %collective-permute-start.16) | collective-permute-done | bytes 6176 | tf_op jit(solution)/shard_map/ppermute | solution.py:69
  124.5 0.3 collective-permute-start.17
  124.8 3.6 %collective-permute-done.17 = f32[64,24]{1,0:T(8,128)S(1)} collective-permute-done((f32[64,24]{1,0:T(8,128)S(1)}, f32[64,24]{1,0:T(8,128)S(1)}, u32[]{:S(2)}, u32[]{:S(2)}) %collective-permute-start.17) | collective-permute-done | bytes 6176 | tf_op jit(solution)/shard_map/ppermute | solution.py:69
  128.5 5.1 %collective-permute-done.18 = f32[64,24]{1,0:T(8,128)S(1)} collective-permute-done((f32[64,24]{1,0:T(8,128)S(1)}, f32[64,24]{1,0:T(8,128)S(1)}, u32[]{:S(2)}, u32[]{:S(2)}) %collective-permute-start.18) | collective-permute-done | bytes 6176 | tf_op jit(solution)/shard_map/ppermute | solution.py:69
  133.5 4.6 %collective-permute-start.19 = (f32[64,24]{1,0:T(8,128)S(1)}, f32[64,24]{1,0:T(8,128)S(1)}, u32[]{:S(2)}, u32[]{:S(2)}) collective-permute-start(f32[64,24]{1,0:T(8,128)S(1)} %add.109), channel_id=1, source_target_pairs={{0,128},{1,129},{2,130},{3,131},{4,132},{5,133},{6,134},{7,135},{8... | collective-permute-start | bytes 18440 | tf_op jit(solution)/shard_map/ppermute | solution.py:69
  138.1 3.2 %collective-permute-done.19 = f32[64,24]{1,0:T(8,128)S(1)} collective-permute-done((f32[64,24]{1,0:T(8,128)S(1)}, f32[64,24]{1,0:T(8,128)S(1)}, u32[]{:S(2)}, u32[]{:S(2)}) %collective-permute-start.19) | collective-permute-done | bytes 6176 | tf_op jit(solution)/shard_map/ppermute | solution.py:69
  141.3 0.6 multiply_reduce_fusion
  142.7 0.5 fusion.20
  (37 shorter events, 1.0 us)
Async XLA Ops:
  0.6 26.3 %collective-permute-start = (bf16[8,360,128]{2,1,0:T(8,128)(2,1)}, bf16[8,360,128]{2,1,0:T(8,128)(2,1)S(1)}, u32[]{:S(2)}, u32[]{:S(2)}) collective-permute-start(bf16[8,360,128]{2,1,0:T(8,128)(2,1)} %param.4), channel_id=1, source_target_pairs={{4,0},{9,1},{14,2},{19,3},{8,4},{13,5},{18,6},{23,7},{12,8},{17,9}... | collective-permute-start | bytes 2211848 | tf_op jit(solution)/shard_map/ppermute | solution.py:91
  8.6 17.0 %collective-permute-start.2 = (s32[1,8]{1,0:T(1,128)}, s32[1,8]{1,0:T(1,128)S(1)}, u32[]{:S(2)}, u32[]{:S(2)}) collective-permute-start(s32[1,8]{1,0:T(1,128)} %param.5), channel_id=1, source_target_pairs={{4,0},{9,1},{14,2},{19,3},{8,4},{13,5},{18,6},{23,7},{12,8},{17,9}... | collective-permute-start | bytes 104 | tf_op jit(solution)/shard_map/ppermute | solution.py:91
  9.4 16.3 %collective-permute-start.3 = (s32[1]{0:T(128)}, s32[1]{0:T(128)}, u32[]{:S(2)}, u32[]{:S(2)}) collective-permute-start(s32[1]{0:T(128)} %param.6), channel_id=1, source_target_pairs={{4,0},{9,1},{14,2},{19,3},{8,4},{13,5},{18,6},{23,7},{12,8},{17,9}... | collective-permute-start | bytes 20 | tf_op jit(solution)/shard_map/ppermute | solution.py:91
  11.5 51.8 %collective-permute-start.1 = (f32[1,24]{1,0:T(1,128)}, f32[1,24]{1,0:T(1,128)S(1)}, u32[]{:S(2)}, u32[]{:S(2)}) collective-permute-start(f32[1,24]{1,0:T(1,128)} %param.7), channel_id=1, source_target_pairs={{4,0},{9,1},{14,2},{19,3},{8,4},{13,5},{18,6},{23,7},{12,8},{17,9}... | collective-permute-start | bytes 296 | tf_op jit(solution)/shard_map/ppermute | solution.py:91
  59.1 3.5 %copy-start = (f32[1,24]{1,0:T(1,128)S(1)}, f32[1,24]{1,0:T(1,128)}, u32[]{:S(2)}) copy-start(f32[1,24]{1,0:T(1,128)} %param.7) | copy-start | bytes 292
  64.2 4.0 %collective-permute-start.4 = (f32[64,24]{1,0:T(8,128)S(1)}, f32[64,24]{1,0:T(8,128)S(1)}, u32[]{:S(2)}, u32[]{:S(2)}) collective-permute-start(f32[64,24]{1,0:T(8,128)S(1)} %select_add_fusion.1), channel_id=1, source_target_pairs={{0,1},{1,0},{2,3},{3,2},{4,5},{5,4},{6,7},{7,6},{8,9},{9,8},{10,11... | collective-permute-start | bytes 18440 | tf_op jit(solution)/shard_map/ppermute | solution.py:69
  68.3 5.5 %collective-permute-start.5 = (f32[64,24]{1,0:T(8,128)S(1)}, f32[64,24]{1,0:T(8,128)S(1)}, u32[]{:S(2)}, u32[]{:S(2)}) collective-permute-start(f32[64,24]{1,0:T(8,128)S(1)} %fusion.11), channel_id=1, source_target_pairs={{0,2},{1,3},{2,0},{3,1},{4,6},{5,7},{6,4},{7,5},{8,10},{9,11},{10,... | collective-permute-start | bytes 18440 | tf_op jit(solution)/shard_map/ppermute | solution.py:69
  73.9 1.3 collective-permute-start.6
  75.2 3.9 %collective-permute-start.7 = (f32[64,24]{1,0:T(8,128)S(1)}, f32[64,24]{1,0:T(8,128)S(1)}, u32[]{:S(2)}, u32[]{:S(2)}) collective-permute-start(f32[64,24]{1,0:T(8,128)S(1)} %add.93), channel_id=1, source_target_pairs={{0,8},{1,9},{2,10},{3,11},{4,12},{5,13},{6,14},{7,15},{8,0},{9,1},... | collective-permute-start | bytes 18440 | tf_op jit(solution)/shard_map/ppermute | solution.py:69
  79.1 5.4 %collective-permute-start.8 = (f32[64,24]{1,0:T(8,128)S(1)}, f32[64,24]{1,0:T(8,128)S(1)}, u32[]{:S(2)}, u32[]{:S(2)}) collective-permute-start(f32[64,24]{1,0:T(8,128)S(1)} %add.94), channel_id=1, source_target_pairs={{0,16},{1,17},{2,18},{3,19},{4,20},{5,21},{6,22},{7,23},{8,24},{9,... | collective-permute-start | bytes 18440 | tf_op jit(solution)/shard_map/ppermute | solution.py:69
  84.5 3.9 %collective-permute-start.9 = (f32[64,24]{1,0:T(8,128)S(1)}, f32[64,24]{1,0:T(8,128)S(1)}, u32[]{:S(2)}, u32[]{:S(2)}) collective-permute-start(f32[64,24]{1,0:T(8,128)S(1)} %add.95), channel_id=1, source_target_pairs={{0,32},{1,33},{2,34},{3,35},{4,36},{5,37},{6,38},{7,39},{8,40},{9,... | collective-permute-start | bytes 18440 | tf_op jit(solution)/shard_map/ppermute | solution.py:69
  88.5 4.8 %collective-permute-start.10 = (f32[64,24]{1,0:T(8,128)S(1)}, f32[64,24]{1,0:T(8,128)S(1)}, u32[]{:S(2)}, u32[]{:S(2)}) collective-permute-start(f32[64,24]{1,0:T(8,128)S(1)} %add.96), channel_id=1, source_target_pairs={{0,64},{1,65},{2,66},{3,67},{4,68},{5,69},{6,70},{7,71},{8,72},{9,... | collective-permute-start | bytes 18440 | tf_op jit(solution)/shard_map/ppermute | solution.py:69
  93.3 7.8 %collective-permute-start.11 = (f32[64,24]{1,0:T(8,128)S(1)}, f32[64,24]{1,0:T(8,128)S(1)}, u32[]{:S(2)}, u32[]{:S(2)}) collective-permute-start(f32[64,24]{1,0:T(8,128)S(1)} %add.97), channel_id=1, source_target_pairs={{0,128},{1,129},{2,130},{3,131},{4,132},{5,133},{6,134},{7,135},{8... | collective-permute-start | bytes 18440 | tf_op jit(solution)/shard_map/ppermute | solution.py:69
  102.5 40.7 %copy-start.1 = (f32[1,24]{1,0:T(1,128)}, f32[1,24]{1,0:T(1,128)S(1)}, u32[]{:S(2)}) copy-start(f32[1,24]{1,0:T(1,128)S(1)} %constant_dynamic-slice_fusion.2) | copy-start | bytes 292
  104.1 4.0 %collective-permute-start.12 = (f32[64,24]{1,0:T(8,128)S(1)}, f32[64,24]{1,0:T(8,128)S(1)}, u32[]{:S(2)}, u32[]{:S(2)}) collective-permute-start(f32[64,24]{1,0:T(8,128)S(1)} %select_add_fusion), channel_id=1, source_target_pairs={{0,1},{1,0},{2,3},{3,2},{4,5},{5,4},{6,7},{7,6},{8,9},{9,8},{10,11... | collective-permute-start | bytes 18440 | tf_op jit(solution)/shard_map/ppermute | solution.py:69
  108.2 5.5 %collective-permute-start.13 = (f32[64,24]{1,0:T(8,128)S(1)}, f32[64,24]{1,0:T(8,128)S(1)}, u32[]{:S(2)}, u32[]{:S(2)}) collective-permute-start(f32[64,24]{1,0:T(8,128)S(1)} %fusion.12), channel_id=1, source_target_pairs={{0,2},{1,3},{2,0},{3,1},{4,6},{5,7},{6,4},{7,5},{8,10},{9,11},{10,... | collective-permute-start | bytes 18440 | tf_op jit(solution)/shard_map/ppermute | solution.py:69
  113.8 1.3 collective-permute-start.14
  115.1 3.9 %collective-permute-start.15 = (f32[64,24]{1,0:T(8,128)S(1)}, f32[64,24]{1,0:T(8,128)S(1)}, u32[]{:S(2)}, u32[]{:S(2)}) collective-permute-start(f32[64,24]{1,0:T(8,128)S(1)} %add.105), channel_id=1, source_target_pairs={{0,8},{1,9},{2,10},{3,11},{4,12},{5,13},{6,14},{7,15},{8,0},{9,1},... | collective-permute-start | bytes 18440 | tf_op jit(solution)/shard_map/ppermute | solution.py:69
  119.0 5.4 %collective-permute-start.16 = (f32[64,24]{1,0:T(8,128)S(1)}, f32[64,24]{1,0:T(8,128)S(1)}, u32[]{:S(2)}, u32[]{:S(2)}) collective-permute-start(f32[64,24]{1,0:T(8,128)S(1)} %add.106), channel_id=1, source_target_pairs={{0,16},{1,17},{2,18},{3,19},{4,20},{5,21},{6,22},{7,23},{8,24},{9,... | collective-permute-start | bytes 18440 | tf_op jit(solution)/shard_map/ppermute | solution.py:69
  124.5 3.9 %collective-permute-start.17 = (f32[64,24]{1,0:T(8,128)S(1)}, f32[64,24]{1,0:T(8,128)S(1)}, u32[]{:S(2)}, u32[]{:S(2)}) collective-permute-start(f32[64,24]{1,0:T(8,128)S(1)} %add.107), channel_id=1, source_target_pairs={{0,32},{1,33},{2,34},{3,35},{4,36},{5,37},{6,38},{7,39},{8,40},{9,... | collective-permute-start | bytes 18440 | tf_op jit(solution)/shard_map/ppermute | solution.py:69
  128.4 5.1 %collective-permute-start.18 = (f32[64,24]{1,0:T(8,128)S(1)}, f32[64,24]{1,0:T(8,128)S(1)}, u32[]{:S(2)}, u32[]{:S(2)}) collective-permute-start(f32[64,24]{1,0:T(8,128)S(1)} %add.108), channel_id=1, source_target_pairs={{0,64},{1,65},{2,66},{3,67},{4,68},{5,69},{6,70},{7,71},{8,72},{9,... | collective-permute-start | bytes 18440 | tf_op jit(solution)/shard_map/ppermute | solution.py:69
  133.5 7.8 %collective-permute-start.19 = (f32[64,24]{1,0:T(8,128)S(1)}, f32[64,24]{1,0:T(8,128)S(1)}, u32[]{:S(2)}, u32[]{:S(2)}) collective-permute-start(f32[64,24]{1,0:T(8,128)S(1)} %add.109), channel_id=1, source_target_pairs={{0,128},{1,129},{2,130},{3,131},{4,132},{5,133},{6,134},{7,135},{8... | collective-permute-start | bytes 18440 | tf_op jit(solution)/shard_map/ppermute | solution.py:69

commit v3 on v2

--- a/solution.py
+++ b/solution.py
@@ -17,40 +17,69 @@
     return jnp.stack([jnp.cos(angle), jnp.sin(angle), jnp.cos(2.0 * angle)], axis=1)
 
 
-def tile_kernel(a_ref, b_ref, w_ref, o_ref):
+def tile_kernel(a_ref, b_ref, w_ref, o_ref, s_ref):
     n = a_ref.shape[0]
+    lines = w_ref.shape[1]
+    width = a_ref.shape[1]
+    groups = width // 128
+    strips = lines // 8
 
-    def body(i, carry):
-        a = i // n
-        b = i % n
-        s = lax.dot_general(
-            b_ref[b], a_ref[a], (((1,), (1,)), ((), ())), preferred_element_type=jnp.float32
+    def per_image(a, carry):
+        s_ref[...] = (
+            lax.dot_general(
+                b_ref[...], a_ref[a], (((1,), (1,)), ((), ())), preferred_element_type=jnp.float32
+            )
+            * score_gain
         )
-        s = s * score_gain
-        top = jnp.max(s, axis=0, keepdims=True)
-        e = jnp.exp(s - top)
-        o_ref[a, b, 0:1, :] = top
-        o_ref[a, b, 1:2, :] = jnp.sum(e, axis=0, keepdims=True)
-        o_ref[a, b, 2:3, :] = jnp.sum(e * w_ref[0], axis=0, keepdims=True)
-        o_ref[a, b, 3:4, :] = jnp.sum(e * w_ref[1], axis=0, keepdims=True)
-        o_ref[a, b, 4:5, :] = jnp.sum(e * w_ref[2], axis=0, keepdims=True)
+
+        def per_partner(b, carry2):
+            base = b * lines
+
+            def col_max(r, m):
+                start = pl.multiple_of(base + r * 8, 8)
+                return jnp.maximum(m, s_ref[pl.ds(start, 8), :])
+
+            m8 = lax.fori_loop(0, strips, col_max, jnp.full((8, width), -jnp.inf, jnp.float32))
+            top = jnp.max(m8, axis=0, keepdims=True)
+            top8 = jnp.broadcast_to(top, (8, width))
+
+            def accumulate(r, acc):
+                start = pl.multiple_of(base + r * 8, 8)
+                e = jnp.exp(s_ref[pl.ds(start, 8), :] - top8)
+                row = pl.multiple_of(r * 8, 8)
+                out = [acc[0] + e]
+                for q in range(3):
+                    wq = w_ref[q, pl.ds(row, 8), :]
+                    wide = jnp.concatenate([wq] * groups, axis=1)
+                    out.append(acc[q + 1] + e * wide)
+                return tuple(out)
+
+            zero = jnp.zeros((8, width), jnp.float32)
+            acc = lax.fori_loop(0, strips, accumulate, (zero, zero, zero, zero))
+            o_ref[a, b, 0:1, :] = top
+            for j in range(4):
+                o_ref[a, b, j + 1 : j + 2, :] = jnp.sum(acc[j], axis=0, keepdims=True)
+            return carry2
+
+        lax.fori_loop(0, n, per_partner, 0)
         return carry
 
-    lax.fori_loop(0, n * n, body, 0)
+    lax.fori_loop(0, n, per_image, 0)
 
 
 def pair_tile(own, other, table):
     count, lines, radii = own.shape
     padded = ((lines + 127) // 128) * 128
     own_p = jnp.pad(own, ((0, 0), (0, padded - lines), (0, 0)))
-    wide = jnp.broadcast_to(jnp.transpose(table)[:, :, None], (3, lines, padded))
+    wide = jnp.broadcast_to(jnp.transpose(table)[:, :, None], (3, lines, 128))
     stats = pl.pallas_call(
         tile_kernel,
         out_shape=jax.ShapeDtypeStruct((count, count, 8, padded), jnp.float32),
         in_specs=[pl.BlockSpec(memory_space=pltpu.VMEM)] * 3,
         out_specs=pl.BlockSpec(memory_space=pltpu.VMEM),
+        scratch_shapes=[pltpu.VMEM((count * lines, padded), jnp.float32)],
         compiler_params=pltpu.CompilerParams(vmem_limit_bytes=48 * 1024 * 1024),
-    )(own_p, other, wide)
+    )(own_p, other.reshape(count * lines, radii), wide)
     stats = stats[:, :, :, :lines]
     top = stats[:, :, 0, :]
     peak = jnp.max(top, axis=2, keepdims=True)

time: 143 us -> 178 us (1.24)
  Pallas kernels: 31.9 us -> 66.5 us
    pallas_call x1, Pallas kernels: 31.9 us -> 66.5 us  [pair_tile(): pl.pallas_call(tile_kernel, out_shape=jax.ShapeDtypeStruct((count, count,...]
  transfers between devices with their start and end apart: 20 -> 20, of which waited for: 17 -> 17; matrix products, arithmetic and copies ran while one was open for 6% -> 4% of each run, Pallas kernels for 22% -> 37%
where the time goes in v3:
time: 178 us
  waiting for transfers between devices  71.2 us (40%)
  Pallas kernels  66.5 us (37%)
  starting transfers between devices  23.9 us (13%)
  matrix products  5.75 us (3%)
  other arithmetic  5.1 us (3%)
  between operations  2.92 us (2%)
  local copies, waits for them, and re-layouts  2.73 us (2%)
    pallas_call x1, Pallas kernels, pair_tile(): pl.pallas_call(tile_kernel, out_shape=jax.ShapeDtypeStruct((count, count,...  66.5 us
    ppermute x16, waiting for transfers between devices, butterfly_sum(): value = value + lax.ppermute(value, axes, route)  61.5 us
    ppermute x16, starting transfers between devices, butterfly_sum(): value = value + lax.ppermute(value, axes, route)  12 us
    ppermute x4, starting transfers between devices, body(): fetch = lambda v: lax.ppermute(v, axes, route)  11.9 us
    ppermute x4, waiting for transfers between devices, body(): fetch = lambda v: lax.ppermute(v, axes, route)  9.69 us
  transfers between devices with their start and end apart: 20, of which 17 were waited for; matrix products, arithmetic and copies ran while one was open for 4% of the time, Pallas kernels for 37%

profile of v3, /device:TPU:4, one launch (start us, length us, event | category | flops | bytes accessed | tf_op | source)
XLA Modules:
  0.0 178.2 jit_solution(1980993770772546760)
XLA Ops:
  0.6 8.0 %collective-permute-start = (bf16[8,360,128]{2,1,0:T(8,128)(2,1)}, bf16[8,360,128]{2,1,0:T(8,128)(2,1)S(1)}, u32[]{:S(2)}, u32[]{:S(2)}) collective-permute-start(bf16[8,360,128]{2,1,0:T(8,128)(2,1)} %param.4), channel_id=1, source_target_pairs={{4,0},{9,1},{14,2},{19,3},{8,4},{13,5},{18,6},{23,7},{12,8},{17,9}... | collective-permute-start | bytes 2211848 | tf_op jit(solution)/shard_map/ppermute | solution.py:120
  8.6 0.7 collective-permute-start.2
  9.4 2.2 %collective-permute-start.3 = (s32[1]{0:T(128)}, s32[1]{0:T(128)}, u32[]{:S(2)}, u32[]{:S(2)}) collective-permute-start(s32[1]{0:T(128)} %param.6), channel_id=1, source_target_pairs={{4,0},{9,1},{14,2},{19,3},{8,4},{13,5},{18,6},{23,7},{12,8},{17,9}... | collective-permute-start | bytes 20 | tf_op jit(solution)/shard_map/ppermute | solution.py:120
  11.5 1.0 collective-permute-start.1
  13.2 1.2 pad.4.a_ref
  14.5 0.1 multiply_cosine_fusion
  14.6 0.6 copy-done.2
  15.3 0.7 fusion.15
  16.0 9.7 %collective-permute-done.3 = s32[1]{0:T(128)} collective-permute-done((s32[1]{0:T(128)}, s32[1]{0:T(128)}, u32[]{:S(2)}, u32[]{:S(2)}) %collective-permute-start.3) | collective-permute-done | bytes 36 | tf_op jit(solution)/shard_map/ppermute | solution.py:120
  25.7 1.3 fusion.14
  26.9 0.2 broadcast_in_dim.72.w_ref
  27.1 66.5 %shard_map.59 = f32[8,8,8,384]{3,2,1,0:T(8,128)S(1)} custom-call(bf16[8,384,128]{2,1,0:T(8,128)(2,1)S(1)} %pad.4.a_ref, bf16[2880,128]{1,0:T(8,128)(2,1)S(1)} %bitcast.72, f32[3,360,128]{2,1,0:T(8,128)S(1)} %broadcast_in_dim.72.w_ref), custom_call_target="tpu_custom_call" | custom-call | tf_op jit(solution)/shard_map/pallas_call | solution.py:75
  93.7 0.3 fusion.25
  94.0 0.1 slice_multiply_fusion
  94.2 0.2 fusion.6
  94.3 2.7 %fusion = f32[3,8,3,8]{3,0,2,1:T(4,128)S(1)} fusion(f32[8,8,3,360]{3,2,1,0:T(4,128)S(1)} %slice_multiply_fusion, f32[8,8]{1,0:T(8,128)S(1)} %fusion.6, f32[360,1]{0,1:T(1,128)S(1)} %get-tuple-element.9, f32[360,1]{0,1:T(1,128)S(1)} %get-tuple-element.10, f32[360,1]{0,1:T(1,128)S(1)} %fusion.17), kind=kOutput, calls=%fused_computation.1 | convolution fusion | flops 2491056 | bytes 283360 | tf_op jit(solution)/shard_map/lp,abql->abpq/dot_general | solution.py:89
  97.1 0.6 copy-done
  97.7 0.8 fusion.2
  98.5 0.8 fusion.1
  99.2 0.1 select_add_fusion.1
  99.3 0.9 collective-permute-start.4
  100.3 3.1 %collective-permute-done.4 = f32[64,24]{1,0:T(8,128)S(1)} collective-permute-done((f32[64,24]{1,0:T(8,128)S(1)}, f32[64,24]{1,0:T(8,128)S(1)}, u32[]{:S(2)}, u32[]{:S(2)}) %collective-permute-start.4) | collective-permute-done | bytes 6176 | tf_op jit(solution)/shard_map/ppermute | solution.py:98
  103.5 5.4 %collective-permute-done.5 = f32[64,24]{1,0:T(8,128)S(1)} collective-permute-done((f32[64,24]{1,0:T(8,128)S(1)}, f32[64,24]{1,0:T(8,128)S(1)}, u32[]{:S(2)}, u32[]{:S(2)}) %collective-permute-start.5) | collective-permute-done | bytes 6176 | tf_op jit(solution)/shard_map/ppermute | solution.py:98
  109.1 1.2 collective-permute-done.6
  110.3 3.9 %collective-permute-done.7 = f32[64,24]{1,0:T(8,128)S(1)} collective-permute-done((f32[64,24]{1,0:T(8,128)S(1)}, f32[64,24]{1,0:T(8,128)S(1)}, u32[]{:S(2)}, u32[]{:S(2)}) %collective-permute-start.7) | collective-permute-done | bytes 6176 | tf_op jit(solution)/shard_map/ppermute | solution.py:98
  114.3 5.4 %collective-permute-done.8 = f32[64,24]{1,0:T(8,128)S(1)} collective-permute-done((f32[64,24]{1,0:T(8,128)S(1)}, f32[64,24]{1,0:T(8,128)S(1)}, u32[]{:S(2)}, u32[]{:S(2)}) %collective-permute-start.8) | collective-permute-done | bytes 6176 | tf_op jit(solution)/shard_map/ppermute | solution.py:98
  119.7 3.9 %collective-permute-done.9 = f32[64,24]{1,0:T(8,128)S(1)} collective-permute-done((f32[64,24]{1,0:T(8,128)S(1)}, f32[64,24]{1,0:T(8,128)S(1)}, u32[]{:S(2)}, u32[]{:S(2)}) %collective-permute-start.9) | collective-permute-done | bytes 6176 | tf_op jit(solution)/shard_map/ppermute | solution.py:98
  123.6 4.8 %collective-permute-done.10 = f32[64,24]{1,0:T(8,128)S(1)} collective-permute-done((f32[64,24]{1,0:T(8,128)S(1)}, f32[64,24]{1,0:T(8,128)S(1)}, u32[]{:S(2)}, u32[]{:S(2)}) %collective-permute-start.10) | collective-permute-done | bytes 6176 | tf_op jit(solution)/shard_map/ppermute | solution.py:98
  128.4 3.6 %collective-permute-start.11 = (f32[64,24]{1,0:T(8,128)S(1)}, f32[64,24]{1,0:T(8,128)S(1)}, u32[]{:S(2)}, u32[]{:S(2)}) collective-permute-start(f32[64,24]{1,0:T(8,128)S(1)} %add.97), channel_id=1, source_target_pairs={{0,128},{1,129},{2,130},{3,131},{4,132},{5,133},{6,134},{7,135},{8... | collective-permute-start | bytes 18440 | tf_op jit(solution)/shard_map/ppermute | solution.py:98
  132.0 4.2 %collective-permute-done.11 = f32[64,24]{1,0:T(8,128)S(1)} collective-permute-done((f32[64,24]{1,0:T(8,128)S(1)}, f32[64,24]{1,0:T(8,128)S(1)}, u32[]{:S(2)}, u32[]{:S(2)}) %collective-permute-start.11) | collective-permute-done | bytes 6176 | tf_op jit(solution)/shard_map/ppermute | solution.py:98
  136.2 0.6 multiply_reduce_fusion.1
  137.6 0.8 fusion.4
  138.4 0.8 fusion.3
  139.2 0.9 collective-permute-start.12
  140.2 3.1 %collective-permute-done.12 = f32[64,24]{1,0:T(8,128)S(1)} collective-permute-done((f32[64,24]{1,0:T(8,128)S(1)}, f32[64,24]{1,0:T(8,128)S(1)}, u32[]{:S(2)}, u32[]{:S(2)}) %collective-permute-start.12) | collective-permute-done | bytes 6176 | tf_op jit(solution)/shard_map/ppermute | solution.py:98
  143.4 5.4 %collective-permute-done.13 = f32[64,24]{1,0:T(8,128)S(1)} collective-permute-done((f32[64,24]{1,0:T(8,128)S(1)}, f32[64,24]{1,0:T(8,128)S(1)}, u32[]{:S(2)}, u32[]{:S(2)}) %collective-permute-start.13) | collective-permute-done | bytes 6176 | tf_op jit(solution)/shard_map/ppermute | solution.py:98
  148.9 0.3 collective-permute-start.14
  149.2 1.2 collective-permute-done.14
  150.5 3.8 %collective-permute-done.15 = f32[64,24]{1,0:T(8,128)S(1)} collective-permute-done((f32[64,24]{1,0:T(8,128)S(1)}, f32[64,24]{1,0:T(8,128)S(1)}, u32[]{:S(2)}, u32[]{:S(2)}) %collective-permute-start.15) | collective-permute-done | bytes 6176 | tf_op jit(solution)/shard_map/ppermute | solution.py:98
  154.3 1.6 collective-permute-start.16
  155.9 3.8 %collective-permute-done.16 = f32[64,24]{1,0:T(8,128)S(1)} collective-permute-done((f32[64,24]{1,0:T(8,128)S(1)}, f32[64,24]{1,0:T(8,128)S(1)}, u32[]{:S(2)}, u32[]{:S(2)}) %collective-permute-start.16) | collective-permute-done | bytes 6176 | tf_op jit(solution)/shard_map/ppermute | solution.py:98
  159.8 3.8 %collective-permute-done.17 = f32[64,24]{1,0:T(8,128)S(1)} collective-permute-done((f32[64,24]{1,0:T(8,128)S(1)}, f32[64,24]{1,0:T(8,128)S(1)}, u32[]{:S(2)}, u32[]{:S(2)}) %collective-permute-start.17) | collective-permute-done | bytes 6176 | tf_op jit(solution)/shard_map/ppermute | solution.py:98
  163.7 0.3 collective-permute-start.18
  163.9 4.6 %collective-permute-done.18 = f32[64,24]{1,0:T(8,128)S(1)} collective-permute-done((f32[64,24]{1,0:T(8,128)S(1)}, f32[64,24]{1,0:T(8,128)S(1)}, u32[]{:S(2)}, u32[]{:S(2)}) %collective-permute-start.18) | collective-permute-done | bytes 6176 | tf_op jit(solution)/shard_map/ppermute | solution.py:98
  168.5 4.0 %collective-permute-start.19 = (f32[64,24]{1,0:T(8,128)S(1)}, f32[64,24]{1,0:T(8,128)S(1)}, u32[]{:S(2)}, u32[]{:S(2)}) collective-permute-start(f32[64,24]{1,0:T(8,128)S(1)} %add.109), channel_id=1, source_target_pairs={{0,128},{1,129},{2,130},{3,131},{4,132},{5,133},{6,134},{7,135},{8... | collective-permute-start | bytes 18440 | tf_op jit(solution)/shard_map/ppermute | solution.py:98
  172.5 3.9 %collective-permute-done.19 = f32[64,24]{1,0:T(8,128)S(1)} collective-permute-done((f32[64,24]{1,0:T(8,128)S(1)}, f32[64,24]{1,0:T(8,128)S(1)}, u32[]{:S(2)}, u32[]{:S(2)}) %collective-permute-start.19) | collective-permute-done | bytes 6176 | tf_op jit(solution)/shard_map/ppermute | solution.py:98
  176.3 0.6 multiply_reduce_fusion
  177.6 0.5 fusion.20
  (39 shorter events, 1.3 us)
Async XLA Ops:
  0.6 26.3 %collective-permute-start = (bf16[8,360,128]{2,1,0:T(8,128)(2,1)}, bf16[8,360,128]{2,1,0:T(8,128)(2,1)S(1)}, u32[]{:S(2)}, u32[]{:S(2)}) collective-permute-start(bf16[8,360,128]{2,1,0:T(8,128)(2,1)} %param.4), channel_id=1, source_target_pairs={{4,0},{9,1},{14,2},{19,3},{8,4},{13,5},{18,6},{23,7},{12,8},{17,9}... | collective-permute-start | bytes 2211848 | tf_op jit(solution)/shard_map/ppermute | solution.py:120
  8.6 17.0 %collective-permute-start.2 = (s32[1,8]{1,0:T(1,128)}, s32[1,8]{1,0:T(1,128)S(1)}, u32[]{:S(2)}, u32[]{:S(2)}) collective-permute-start(s32[1,8]{1,0:T(1,128)} %param.5), channel_id=1, source_target_pairs={{4,0},{9,1},{14,2},{19,3},{8,4},{13,5},{18,6},{23,7},{12,8},{17,9}... | collective-permute-start | bytes 104 | tf_op jit(solution)/shard_map/ppermute | solution.py:120
  9.4 16.3 %collective-permute-start.3 = (s32[1]{0:T(128)}, s32[1]{0:T(128)}, u32[]{:S(2)}, u32[]{:S(2)}) collective-permute-start(s32[1]{0:T(128)} %param.6), channel_id=1, source_target_pairs={{4,0},{9,1},{14,2},{19,3},{8,4},{13,5},{18,6},{23,7},{12,8},{17,9}... | collective-permute-start | bytes 20 | tf_op jit(solution)/shard_map/ppermute | solution.py:120
  11.5 86.9 %collective-permute-start.1 = (f32[1,24]{1,0:T(1,128)}, f32[1,24]{1,0:T(1,128)S(1)}, u32[]{:S(2)}, u32[]{:S(2)}) collective-permute-start(f32[1,24]{1,0:T(1,128)} %param.7), channel_id=1, source_target_pairs={{4,0},{9,1},{14,2},{19,3},{8,4},{13,5},{18,6},{23,7},{12,8},{17,9}... | collective-permute-start | bytes 296 | tf_op jit(solution)/shard_map/ppermute | solution.py:120
  14.6 0.7 copy-start.2
  97.0 0.7 copy-start
  99.3 4.0 %collective-permute-start.4 = (f32[64,24]{1,0:T(8,128)S(1)}, f32[64,24]{1,0:T(8,128)S(1)}, u32[]{:S(2)}, u32[]{:S(2)}) collective-permute-start(f32[64,24]{1,0:T(8,128)S(1)} %select_add_fusion.1), channel_id=1, source_target_pairs={{0,1},{1,0},{2,3},{3,2},{4,5},{5,4},{6,7},{7,6},{8,9},{9,8},{10,11... | collective-permute-start | bytes 18440 | tf_op jit(solution)/shard_map/ppermute | solution.py:98
  103.4 5.5 %collective-permute-start.5 = (f32[64,24]{1,0:T(8,128)S(1)}, f32[64,24]{1,0:T(8,128)S(1)}, u32[]{:S(2)}, u32[]{:S(2)}) collective-permute-start(f32[64,24]{1,0:T(8,128)S(1)} %fusion.11), channel_id=1, source_target_pairs={{0,2},{1,3},{2,0},{3,1},{4,6},{5,7},{6,4},{7,5},{8,10},{9,11},{10,... | collective-permute-start | bytes 18440 | tf_op jit(solution)/shard_map/ppermute | solution.py:98
  109.0 1.3 collective-permute-start.6
  110.3 3.9 %collective-permute-start.7 = (f32[64,24]{1,0:T(8,128)S(1)}, f32[64,24]{1,0:T(8,128)S(1)}, u32[]{:S(2)}, u32[]{:S(2)}) collective-permute-start(f32[64,24]{1,0:T(8,128)S(1)} %add.93), channel_id=1, source_target_pairs={{0,8},{1,9},{2,10},{3,11},{4,12},{5,13},{6,14},{7,15},{8,0},{9,1},... | collective-permute-start | bytes 18440 | tf_op jit(solution)/shard_map/ppermute | solution.py:98
  114.3 5.4 %collective-permute-start.8 = (f32[64,24]{1,0:T(8,128)S(1)}, f32[64,24]{1,0:T(8,128)S(1)}, u32[]{:S(2)}, u32[]{:S(2)}) collective-permute-start(f32[64,24]{1,0:T(8,128)S(1)} %add.94), channel_id=1, source_target_pairs={{0,16},{1,17},{2,18},{3,19},{4,20},{5,21},{6,22},{7,23},{8,24},{9,... | collective-permute-start | bytes 18440 | tf_op jit(solution)/shard_map/ppermute | solution.py:98
  119.7 3.9 %collective-permute-start.9 = (f32[64,24]{1,0:T(8,128)S(1)}, f32[64,24]{1,0:T(8,128)S(1)}, u32[]{:S(2)}, u32[]{:S(2)}) collective-permute-start(f32[64,24]{1,0:T(8,128)S(1)} %add.95), channel_id=1, source_target_pairs={{0,32},{1,33},{2,34},{3,35},{4,36},{5,37},{6,38},{7,39},{8,40},{9,... | collective-permute-start | bytes 18440 | tf_op jit(solution)/shard_map/ppermute | solution.py:98
  123.6 4.8 %collective-permute-start.10 = (f32[64,24]{1,0:T(8,128)S(1)}, f32[64,24]{1,0:T(8,128)S(1)}, u32[]{:S(2)}, u32[]{:S(2)}) collective-permute-start(f32[64,24]{1,0:T(8,128)S(1)} %add.96), channel_id=1, source_target_pairs={{0,64},{1,65},{2,66},{3,67},{4,68},{5,69},{6,70},{7,71},{8,72},{9,... | collective-permute-start | bytes 18440 | tf_op jit(solution)/shard_map/ppermute | solution.py:98
  128.4 7.8 %collective-permute-start.11 = (f32[64,24]{1,0:T(8,128)S(1)}, f32[64,24]{1,0:T(8,128)S(1)}, u32[]{:S(2)}, u32[]{:S(2)}) collective-permute-start(f32[64,24]{1,0:T(8,128)S(1)} %add.97), channel_id=1, source_target_pairs={{0,128},{1,129},{2,130},{3,131},{4,132},{5,133},{6,134},{7,135},{8... | collective-permute-start | bytes 18440 | tf_op jit(solution)/shard_map/ppermute | solution.py:98
  137.6 0.8 copy-start.1
  139.2 4.0 %collective-permute-start.12 = (f32[64,24]{1,0:T(8,128)S(1)}, f32[64,24]{1,0:T(8,128)S(1)}, u32[]{:S(2)}, u32[]{:S(2)}) collective-permute-start(f32[64,24]{1,0:T(8,128)S(1)} %select_add_fusion), channel_id=1, source_target_pairs={{0,1},{1,0},{2,3},{3,2},{4,5},{5,4},{6,7},{7,6},{8,9},{9,8},{10,11... | collective-permute-start | bytes 18440 | tf_op jit(solution)/shard_map/ppermute | solution.py:98
  143.3 5.5 %collective-permute-start.13 = (f32[64,24]{1,0:T(8,128)S(1)}, f32[64,24]{1,0:T(8,128)S(1)}, u32[]{:S(2)}, u32[]{:S(2)}) collective-permute-start(f32[64,24]{1,0:T(8,128)S(1)} %fusion.12), channel_id=1, source_target_pairs={{0,2},{1,3},{2,0},{3,1},{4,6},{5,7},{6,4},{7,5},{8,10},{9,11},{10,... | collective-permute-start | bytes 18440 | tf_op jit(solution)/shard_map/ppermute | solution.py:98
  148.9 1.5 collective-permute-start.14
  150.4 3.9 %collective-permute-start.15 = (f32[64,24]{1,0:T(8,128)S(1)}, f32[64,24]{1,0:T(8,128)S(1)}, u32[]{:S(2)}, u32[]{:S(2)}) collective-permute-start(f32[64,24]{1,0:T(8,128)S(1)} %add.105), channel_id=1, source_target_pairs={{0,8},{1,9},{2,10},{3,11},{4,12},{5,13},{6,14},{7,15},{8,0},{9,1},... | collective-permute-start | bytes 18440 | tf_op jit(solution)/shard_map/ppermute | solution.py:98
  154.3 5.4 %collective-permute-start.16 = (f32[64,24]{1,0:T(8,128)S(1)}, f32[64,24]{1,0:T(8,128)S(1)}, u32[]{:S(2)}, u32[]{:S(2)}) collective-permute-start(f32[64,24]{1,0:T(8,128)S(1)} %add.106), channel_id=1, source_target_pairs={{0,16},{1,17},{2,18},{3,19},{4,20},{5,21},{6,22},{7,23},{8,24},{9,... | collective-permute-start | bytes 18440 | tf_op jit(solution)/shard_map/ppermute | solution.py:98
  159.8 3.9 %collective-permute-start.17 = (f32[64,24]{1,0:T(8,128)S(1)}, f32[64,24]{1,0:T(8,128)S(1)}, u32[]{:S(2)}, u32[]{:S(2)}) collective-permute-start(f32[64,24]{1,0:T(8,128)S(1)} %add.107), channel_id=1, source_target_pairs={{0,32},{1,33},{2,34},{3,35},{4,36},{5,37},{6,38},{7,39},{8,40},{9,... | collective-permute-start | bytes 18440 | tf_op jit(solution)/shard_map/ppermute | solution.py:98
  163.7 4.8 %collective-permute-start.18 = (f32[64,24]{1,0:T(8,128)S(1)}, f32[64,24]{1,0:T(8,128)S(1)}, u32[]{:S(2)}, u32[]{:S(2)}) collective-permute-start(f32[64,24]{1,0:T(8,128)S(1)} %add.108), channel_id=1, source_target_pairs={{0,64},{1,65},{2,66},{3,67},{4,68},{5,69},{6,70},{7,71},{8,72},{9,... | collective-permute-start | bytes 18440 | tf_op jit(solution)/shard_map/ppermute | solution.py:98
  168.5 7.8 %collective-permute-start.19 = (f32[64,24]{1,0:T(8,128)S(1)}, f32[64,24]{1,0:T(8,128)S(1)}, u32[]{:S(2)}, u32[]{:S(2)}) collective-permute-start(f32[64,24]{1,0:T(8,128)S(1)} %add.109), channel_id=1, source_target_pairs={{0,128},{1,129},{2,130},{3,131},{4,132},{5,133},{6,134},{7,135},{8... | collective-permute-start | bytes 18440 | tf_op jit(solution)/shard_map/ppermute | solution.py:98

commit v4 on v3

--- a/solution.py
+++ b/solution.py
@@ -39,7 +39,7 @@
                 start = pl.multiple_of(base + r * 8, 8)
                 return jnp.maximum(m, s_ref[pl.ds(start, 8), :])
 
-            m8 = lax.fori_loop(0, strips, col_max, jnp.full((8, width), -jnp.inf, jnp.float32))
+            m8 = lax.fori_loop(0, strips, col_max, jnp.full((8, width), -jnp.inf, jnp.float32), unroll=True)
             top = jnp.max(m8, axis=0, keepdims=True)
             top8 = jnp.broadcast_to(top, (8, width))
 
@@ -55,7 +55,7 @@
                 return tuple(out)
 
             zero = jnp.zeros((8, width), jnp.float32)
-            acc = lax.fori_loop(0, strips, accumulate, (zero, zero, zero, zero))
+            acc = lax.fori_loop(0, strips, accumulate, (zero, zero, zero, zero), unroll=True)
             o_ref[a, b, 0:1, :] = top
             for j in range(4):
                 o_ref[a, b, j + 1 : j + 2, :] = jnp.sum(acc[j], axis=0, keepdims=True)
@@ -91,12 +91,10 @@
     return jnp.transpose(rel, (2, 0, 3, 1)).reshape(3 * count, 3 * count)
 
 
-def butterfly_sum(value, axes, size):
-    bit = 1
-    while bit < size:
+def butterfly_sum(value, axes, size, bits):
+    for bit in bits:
         route = [(i, i ^ bit) for i in range(size)]
         value = value + lax.ppermute(value, axes, route)
-        bit *= 2
     return value
 
 
@@ -107,9 +105,8 @@
     halo = slots // 2
     ncols = lax.axis_size("cols")
     nblk = lax.axis_size("rows")
-    row = lax.axis_index("rows")
-    column = lax.axis_index("cols")
-    step = column + 1
+    size = nblk * ncols
+    step = lax.axis_index("cols") + 1
     table = line_table(lines)
 
     axes = ("rows", "cols")
@@ -117,6 +114,7 @@
     for i in range(nblk):
         for c in range(ncols):
             route.append((((i + c + 1) % nblk) * ncols + c, i * ncols + c))
+    back = [(dst, src) for src, dst in route]
     fetch = lambda v: lax.ppermute(v, axes, route)
     other = fetch(images)
     other_partners = fetch(partners)
@@ -128,28 +126,25 @@
     slot_ids = jnp.arange(slots)
     plus = jnp.any((partners[0] == step + halo - 1) & (slot_ids < counts[0]))
     minus = jnp.any((other_partners[0] == halo - step) & (slot_ids < other_counts[0]))
-    partner_row = (row + step) % nblk
-    rows_ids = jnp.arange(nblk)
-    at_own = (rows_ids == row)[:, None]
-    at_other = (rows_ids == partner_row)[:, None]
+    col_bits = [1 << b for b in range(ncols.bit_length() - 1)]
+    row_bits = [ncols << b for b in range(nblk.bit_length() - 1)]
 
-    def spread(x_own, x_other):
+    def apply(x_own, x_other):
         forward = jnp.where(plus, jnp.dot(tile, x_other, precision=HIGH), 0.0)
         backward = jnp.where(minus, jnp.dot(tile.T, x_own, precision=HIGH), 0.0)
-        part = jnp.where(at_own, forward[None, :], 0.0) + jnp.where(at_other, backward[None, :], 0.0)
-        return butterfly_sum(part, axes, nblk * ncols)
+        part = forward + lax.ppermute(backward, axes, back)
+        return butterfly_sum(part, axes, size, col_bits)
 
+    y1 = apply(start[0], other_start[0])
+    z = apply(y1, fetch(y1))
+    squares = jnp.stack([jnp.sum(y1 * y1), jnp.sum(z * z)])
+    squares = butterfly_sum(squares, axes, size, row_bits)
     entries = float(width * nblk)
-
-    def normalize(raw):
-        return raw / jnp.sqrt(jnp.sum(raw * raw) / entries + norm_eps)
-
-    first_all = normalize(spread(start[0], other_start[0]))
-    first_own = lax.dynamic_index_in_dim(first_all, row, 0, keepdims=True)
-    first_other = lax.dynamic_index_in_dim(first_all, partner_row, 0, keepdims=False)
-    second_all = normalize(spread(first_own[0], first_other))
-    second_own = lax.dynamic_index_in_dim(second_all, row, 0, keepdims=True)
-    return (first_own, second_own)
+    s1 = jnp.sqrt(squares[0] / entries + norm_eps)
+    first_vec = y1 / s1
+    second_raw = z / s1
+    s2 = jnp.sqrt(squares[1] / (s1 * s1) / entries + norm_eps)
+    return (first_vec[None, :], (second_raw / s2)[None, :])
 
 
 def solution(mesh):

time: 178 us -> 123 us (0.69)
  the two profiles are of different devices: /device:TPU:4 before, /device:TPU:6 now
where the time goes in v4:
time: 123 us
  waiting for transfers between devices  54.5 us (44%)
  starting transfers between devices  24.4 us (20%)
  Pallas kernels  22.8 us (19%)
  other arithmetic  9.33 us (8%)
  matrix products  5.78 us (5%)
  local copies, waits for them, and re-layouts  3.3 us (3%)
  between operations  2.81 us (2%)
    ppermute x10, waiting for transfers between devices, butterfly_sum(): value = value + lax.ppermute(value, axes, route)  36.8 us
    pallas_call x1, Pallas kernels, pair_tile(): pl.pallas_call(tile_kernel, out_shape=jax.ShapeDtypeStruct((count, count,...  22.8 us
    ppermute x5, starting transfers between devices, body(): fetch = lambda v: lax.ppermute(v, axes, route)  18.5 us
    ppermute x2, waiting for transfers between devices, apply(): part = forward + lax.ppermute(backward, axes, back)  9.23 us
    ppermute x5, waiting for transfers between devices, body(): fetch = lambda v: lax.ppermute(v, axes, route)  8.47 us
    ppermute x10, starting transfers between devices, butterfly_sum(): value = value + lax.ppermute(value, axes, route)  5.89 us
    add x8, other arithmetic, butterfly_sum(): value = value + lax.ppermute(value, axes, route)  2.84 us
    dot_general x1, matrix products, pair_tile(): rel = jnp.einsum('lp,abql->abpq', table, sums, precision=HIGH)  2.68 us
  transfers between devices with their start and end apart: 17, of which 13 were waited for; matrix products, arithmetic and copies ran while one was open for 6% of the time, Pallas kernels for 19%

profile of v4, /device:TPU:6, one launch (start us, length us, event | category | flops | bytes accessed | tf_op | source)
XLA Modules:
  0.0 122.9 jit_solution(5838395857052945399)
XLA Ops:
  0.6 8.6 %collective-permute-start = (bf16[8,360,128]{2,1,0:T(8,128)(2,1)}, bf16[8,360,128]{2,1,0:T(8,128)(2,1)S(1)}, u32[]{:S(2)}, u32[]{:S(2)}) collective-permute-start(bf16[8,360,128]{2,1,0:T(8,128)(2,1)} %param.4), channel_id=1, source_target_pairs={{4,0},{9,1},{14,2},{19,3},{8,4},{13,5},{18,6},{23,7},{12,8},{17,9}... | collective-permute-start | bytes 2211848 | tf_op jit(solution)/shard_map/ppermute | solution.py:118
  9.2 0.3 collective-permute-start.3
  9.5 3.6 %collective-permute-start.2 = (s32[1,8]{1,0:T(1,128)}, s32[1,8]{1,0:T(1,128)S(1)}, u32[]{:S(2)}, u32[]{:S(2)}) collective-permute-start(s32[1,8]{1,0:T(1,128)} %param.5), channel_id=1, source_target_pairs={{4,0},{9,1},{14,2},{19,3},{8,4},{13,5},{18,6},{23,7},{12,8},{17,9}... | collective-permute-start | bytes 104 | tf_op jit(solution)/shard_map/ppermute | solution.py:118
  13.2 0.3 collective-permute-start.1
  14.2 1.2 pad.4.a_ref
  15.4 0.1 multiply_cosine_fusion
  15.5 0.6 copy-done.1
  16.2 0.6 fusion.15
  16.8 8.5 %collective-permute-done.3 = s32[1]{0:T(128)} collective-permute-done((s32[1]{0:T(128)}, s32[1]{0:T(128)}, u32[]{:S(2)}, u32[]{:S(2)}) %collective-permute-start.3) | collective-permute-done | bytes 36 | tf_op jit(solution)/shard_map/ppermute | solution.py:118
  25.3 1.3 %fusion.14 = pred[]{:T(512)} fusion(s32[1,8]{1,0:T(1,128)S(1)} %collective-permute-done.2, s32[]{:T(128)} %bitcast.13, s32[]{:T(128)S(6)} %sub.24), kind=kLoop, calls=%fused_computation.25 | loop fusion | flops 31 | bytes 41 | tf_op jit(solution)/shard_map/reduce_or | solution.py:128
  26.6 0.2 broadcast_in_dim.22.w_ref
  26.8 22.8 %shard_map.59 = f32[8,8,8,384]{3,2,1,0:T(8,128)S(1)} custom-call(bf16[8,384,128]{2,1,0:T(8,128)(2,1)S(1)} %pad.4.a_ref, bf16[2880,128]{1,0:T(8,128)(2,1)S(1)} %bitcast.82, f32[3,360,128]{2,1,0:T(8,128)S(1)} %broadcast_in_dim.22.w_ref), custom_call_target="tpu_custom_call" | custom-call | tf_op jit(solution)/shard_map/pallas_call | solution.py:75
  49.6 0.3 fusion.23
  49.9 0.2 fusion.8
  50.1 0.1 slice_multiply_fusion
  50.2 2.7 %fusion = f32[3,8,3,8]{3,0,2,1:T(4,128)S(1)} fusion(f32[8,8,3,360]{3,2,1,0:T(4,128)S(1)} %slice_multiply_fusion, f32[8,8]{1,0:T(8,128)S(1)} %fusion.8, f32[360,1]{0,1:T(1,128)S(1)} %get-tuple-element.11, f32[360,1]{0,1:T(1,128)S(1)} %get-tuple-element.12, f32[360,1]{0,1:T(1,128)S(1)} %fusion.17), kind=kOutput, calls=%fused_computation.1 | convolution fusion | flops 2491056 | bytes 283360 | tf_op jit(solution)/shard_map/lp,abql->abpq/dot_general | solution.py:89
  53.1 0.6 copy-done
  53.6 0.8 fusion.3
  54.4 7.7 %collective-permute-done.4 = f32[24]{0:T(128)S(1)} collective-permute-done((f32[24]{0:T(128)S(1)}, f32[24]{0:T(128)S(1)}, u32[]{:S(2)}, u32[]{:S(2)}) %collective-permute-start.4) | collective-permute-done | bytes 128 | tf_op jit(solution)/shard_map/ppermute | solution.py:135
  62.1 0.8 fusion.2
  62.9 0.4 collective-permute-start.5
  63.2 3.2 %collective-permute-done.5 = f32[24]{0:T(128)S(1)} collective-permute-done((f32[24]{0:T(128)S(1)}, f32[24]{0:T(128)S(1)}, u32[]{:S(2)}, u32[]{:S(2)}) %collective-permute-start.5) | collective-permute-done | bytes 128 | tf_op jit(solution)/shard_map/ppermute | solution.py:97
  66.5 0.9 collective-permute-start.6
  67.4 4.1 %collective-permute-done.6 = f32[24]{0:T(128)S(1)} collective-permute-done((f32[24]{0:T(128)S(1)}, f32[24]{0:T(128)S(1)}, u32[]{:S(2)}, u32[]{:S(2)}) %collective-permute-start.6) | collective-permute-done | bytes 128 | tf_op jit(solution)/shard_map/ppermute | solution.py:97
  71.5 0.7 multiply_reduce_fusion.1
  72.2 0.8 fusion.6
  73.0 5.6 %collective-permute-start.7 = (f32[24]{0:T(128)S(1)}, f32[24]{0:T(128)S(1)}, u32[]{:S(2)}, u32[]{:S(2)}) collective-permute-start(f32[24]{0:T(128)S(1)} %get-tuple-element.3), channel_id=1, source_target_pairs={{4,0},{9,1},{14,2},{19,3},{8,4},{13,5},{18,6},{23,7},{12,8},{17,9}... | collective-permute-start | bytes 296 | tf_op jit(solution)/shard_map/ppermute | solution.py:118
  78.6 1.5 %collective-permute-done.8 = f32[24]{0:T(128)S(1)} collective-permute-done((f32[24]{0:T(128)S(1)}, f32[24]{0:T(128)S(1)}, u32[]{:S(2)}, u32[]{:S(2)}) %collective-permute-start.8) | collective-permute-done | bytes 128 | tf_op jit(solution)/shard_map/ppermute | solution.py:135
  80.2 0.8 fusion.5
  81.0 3.6 %collective-permute-done.9 = f32[24]{0:T(128)S(1)} collective-permute-done((f32[24]{0:T(128)S(1)}, f32[24]{0:T(128)S(1)}, u32[]{:S(2)}, u32[]{:S(2)}) %collective-permute-start.9) | collective-permute-done | bytes 128 | tf_op jit(solution)/shard_map/ppermute | solution.py:97
  84.5 0.6 collective-permute-start.10
  85.2 4.4 %collective-permute-done.10 = f32[24]{0:T(128)S(1)} collective-permute-done((f32[24]{0:T(128)S(1)}, f32[24]{0:T(128)S(1)}, u32[]{:S(2)}, u32[]{:S(2)}) %collective-permute-start.10) | collective-permute-done | bytes 128 | tf_op jit(solution)/shard_map/ppermute | solution.py:97
  89.6 0.6 multiply_reduce_fusion
  90.2 1.4 %pad_maximum_fusion.2 = f32[2]{0:T(128)S(1)} fusion(f32[1]{0:T(128)} %bitcast.23, f32[1]{0:T(128)} %bitcast.18), kind=kLoop, calls=%fused_computation.32 | loop fusion | flops 2 | bytes 16 | tf_op jit(solution)/shard_map/stack | solution.py:140
  91.7 1.1 collective-permute-done.11
  92.8 1.4 %fusion.27 = f32[2]{0:T(128)S(1)} fusion(f32[2]{0:T(128)S(1)} %collective-permute-done.11, f32[1]{0:T(128)} %bitcast.23, f32[1]{0:T(128)} %bitcast.18), kind=kLoop, calls=%fused_computation.45 | loop fusion | flops 4 | bytes 24 | tf_op jit(solution)/shard_map/add | solution.py:97
  94.2 0.7 collective-permute-start.12
  94.9 2.9 %collective-permute-done.12 = f32[2]{0:T(128)S(1)} collective-permute-done((f32[2]{0:T(128)S(1)}, f32[2]{0:T(128)S(1)}, u32[]{:S(2)}, u32[]{:S(2)}) %collective-permute-start.12) | collective-permute-done | bytes 40 | tf_op jit(solution)/shard_map/ppermute | solution.py:97
  97.8 1.4 %fusion.28 = f32[2]{0:T(128)S(1)} fusion(f32[2]{0:T(128)S(1)} %collective-permute-done.12, f32[2]{0:T(128)S(1)} %collective-permute-done.11, f32[1]{0:T(128)} %bitcast.23, f32[1]{0:T(128)} %bitcast.18), kind=kLoop, calls=%fused_computation.46 | loop fusion | flops 6 | bytes 32 | tf_op jit(solution)/shard_map/add | solution.py:97
  99.3 5.1 %collective-permute-done.13 = f32[2]{0:T(128)S(1)} collective-permute-done((f32[2]{0:T(128)S(1)}, f32[2]{0:T(128)S(1)}, u32[]{:S(2)}, u32[]{:S(2)}) %collective-permute-start.13) | collective-permute-done | bytes 40 | tf_op jit(solution)/shard_map/ppermute | solution.py:97
  104.3 3.6 %collective-permute-done.14 = f32[2]{0:T(128)S(1)} collective-permute-done((f32[2]{0:T(128)S(1)}, f32[2]{0:T(128)S(1)}, u32[]{:S(2)}, u32[]{:S(2)}) %collective-permute-start.14) | collective-permute-done | bytes 40 | tf_op jit(solution)/shard_map/ppermute | solution.py:97
  107.9 0.9 collective-permute-start.15
  108.8 3.5 %collective-permute-done.15 = f32[2]{0:T(128)S(1)} collective-permute-done((f32[2]{0:T(128)S(1)}, f32[2]{0:T(128)S(1)}, u32[]{:S(2)}, u32[]{:S(2)}) %collective-permute-start.15) | collective-permute-done | bytes 40 | tf_op jit(solution)/shard_map/ppermute | solution.py:97
  112.4 2.2 %collective-permute-start.16 = (f32[2]{0:T(128)S(1)}, f32[2]{0:T(128)S(1)}, u32[]{:S(2)}, u32[]{:S(2)}) collective-permute-start(f32[2]{0:T(128)S(1)} %add.65), channel_id=1, source_target_pairs={{0,128},{1,129},{2,130},{3,131},{4,132},{5,133},{6,134},{7,135},{8... | collective-permute-start | bytes 32 | tf_op jit(solution)/shard_map/ppermute | solution.py:97
  114.6 5.2 %collective-permute-done.16 = f32[2]{0:T(128)S(1)} collective-permute-done((f32[2]{0:T(128)S(1)}, f32[2]{0:T(128)S(1)}, u32[]{:S(2)}, u32[]{:S(2)}) %collective-permute-start.16) | collective-permute-done | bytes 40 | tf_op jit(solution)/shard_map/ppermute | solution.py:97
  119.9 0.6 fusion.24
  121.1 0.5 divide_bitcast_fusion.1
  122.4 0.5 divide_bitcast_fusion
  (23 shorter events, 0.4 us)
Async XLA Ops:
  0.6 26.0 %collective-permute-start = (bf16[8,360,128]{2,1,0:T(8,128)(2,1)}, bf16[8,360,128]{2,1,0:T(8,128)(2,1)S(1)}, u32[]{:S(2)}, u32[]{:S(2)}) collective-permute-start(bf16[8,360,128]{2,1,0:T(8,128)(2,1)} %param.4), channel_id=1, source_target_pairs={{4,0},{9,1},{14,2},{19,3},{8,4},{13,5},{18,6},{23,7},{12,8},{17,9}... | collective-permute-start | bytes 2211848 | tf_op jit(solution)/shard_map/ppermute | solution.py:118
  9.2 16.1 %collective-permute-start.3 = (s32[1]{0:T(128)}, s32[1]{0:T(128)}, u32[]{:S(2)}, u32[]{:S(2)}) collective-permute-start(s32[1]{0:T(128)} %param.6), channel_id=1, source_target_pairs={{4,0},{9,1},{14,2},{19,3},{8,4},{13,5},{18,6},{23,7},{12,8},{17,9}... | collective-permute-start | bytes 20 | tf_op jit(solution)/shard_map/ppermute | solution.py:118
  9.5 15.7 %collective-permute-start.2 = (s32[1,8]{1,0:T(1,128)}, s32[1,8]{1,0:T(1,128)S(1)}, u32[]{:S(2)}, u32[]{:S(2)}) collective-permute-start(s32[1,8]{1,0:T(1,128)} %param.5), channel_id=1, source_target_pairs={{4,0},{9,1},{14,2},{19,3},{8,4},{13,5},{18,6},{23,7},{12,8},{17,9}... | collective-permute-start | bytes 104 | tf_op jit(solution)/shard_map/ppermute | solution.py:118
  13.2 41.2 %collective-permute-start.1 = (f32[1,24]{1,0:T(1,128)}, f32[1,24]{1,0:T(1,128)S(1)}, u32[]{:S(2)}, u32[]{:S(2)}) collective-permute-start(f32[1,24]{1,0:T(1,128)} %param.7), channel_id=1, source_target_pairs={{4,0},{9,1},{14,2},{19,3},{8,4},{13,5},{18,6},{23,7},{12,8},{17,9}... | collective-permute-start | bytes 296 | tf_op jit(solution)/shard_map/ppermute | solution.py:118
  15.5 0.7 copy-start.1
  53.0 0.7 copy-start
  54.4 7.7 %collective-permute-start.4 = (f32[24]{0:T(128)S(1)}, f32[24]{0:T(128)S(1)}, u32[]{:S(2)}, u32[]{:S(2)}) collective-permute-start(f32[24]{0:T(128)S(1)} %fusion.3), channel_id=1, source_target_pairs={{0,4},{1,9},{2,14},{3,19},{4,8},{5,13},{6,18},{7,23},{8,12},{9,17}... | collective-permute-start | bytes 296 | tf_op jit(solution)/shard_map/ppermute | solution.py:135
  62.9 3.6 %collective-permute-start.5 = (f32[24]{0:T(128)S(1)}, f32[24]{0:T(128)S(1)}, u32[]{:S(2)}, u32[]{:S(2)}) collective-permute-start(f32[24]{0:T(128)S(1)} %fusion.2), channel_id=1, source_target_pairs={{0,1},{1,0},{2,3},{3,2},{4,5},{5,4},{6,7},{7,6},{8,9},{9,8},{10,11... | collective-permute-start | bytes 296 | tf_op jit(solution)/shard_map/ppermute | solution.py:97
  66.5 5.1 %collective-permute-start.6 = (f32[24]{0:T(128)S(1)}, f32[24]{0:T(128)S(1)}, u32[]{:S(2)}, u32[]{:S(2)}) collective-permute-start(f32[24]{0:T(128)S(1)} %add.56), channel_id=1, source_target_pairs={{0,2},{1,3},{2,0},{3,1},{4,6},{5,7},{6,4},{7,5},{8,10},{9,11},{10,... | collective-permute-start | bytes 296 | tf_op jit(solution)/shard_map/ppermute | solution.py:97
  73.0 7.2 %collective-permute-start.8 = (f32[24]{0:T(128)S(1)}, f32[24]{0:T(128)S(1)}, u32[]{:S(2)}, u32[]{:S(2)}) collective-permute-start(f32[24]{0:T(128)S(1)} %fusion.6), channel_id=1, source_target_pairs={{0,4},{1,9},{2,14},{3,19},{4,8},{5,13},{6,18},{7,23},{8,12},{9,17}... | collective-permute-start | bytes 296 | tf_op jit(solution)/shard_map/ppermute | solution.py:135
  73.0 7.2 %collective-permute-start.7 = (f32[24]{0:T(128)S(1)}, f32[24]{0:T(128)S(1)}, u32[]{:S(2)}, u32[]{:S(2)}) collective-permute-start(f32[24]{0:T(128)S(1)} %get-tuple-element.3), channel_id=1, source_target_pairs={{4,0},{9,1},{14,2},{19,3},{8,4},{13,5},{18,6},{23,7},{12,8},{17,9}... | collective-permute-start | bytes 296 | tf_op jit(solution)/shard_map/ppermute | solution.py:118
  81.0 3.6 %collective-permute-start.9 = (f32[24]{0:T(128)S(1)}, f32[24]{0:T(128)S(1)}, u32[]{:S(2)}, u32[]{:S(2)}) collective-permute-start(f32[24]{0:T(128)S(1)} %fusion.5), channel_id=1, source_target_pairs={{0,1},{1,0},{2,3},{3,2},{4,5},{5,4},{6,7},{7,6},{8,9},{9,8},{10,11... | collective-permute-start | bytes 296 | tf_op jit(solution)/shard_map/ppermute | solution.py:97
  84.5 5.1 %collective-permute-start.10 = (f32[24]{0:T(128)S(1)}, f32[24]{0:T(128)S(1)}, u32[]{:S(2)}, u32[]{:S(2)}) collective-permute-start(f32[24]{0:T(128)S(1)} %add.59), channel_id=1, source_target_pairs={{0,2},{1,3},{2,0},{3,1},{4,6},{5,7},{6,4},{7,5},{8,10},{9,11},{10,... | collective-permute-start | bytes 296 | tf_op jit(solution)/shard_map/ppermute | solution.py:97
  91.6 1.2 collective-permute-start.11
  94.2 3.6 %collective-permute-start.12 = (f32[2]{0:T(128)S(1)}, f32[2]{0:T(128)S(1)}, u32[]{:S(2)}, u32[]{:S(2)}) collective-permute-start(f32[2]{0:T(128)S(1)} %fusion.27), channel_id=1, source_target_pairs={{0,8},{1,9},{2,10},{3,11},{4,12},{5,13},{6,14},{7,15},{8,0},{9,1},... | collective-permute-start | bytes 32 | tf_op jit(solution)/shard_map/ppermute | solution.py:97
  99.2 5.1 %collective-permute-start.13 = (f32[2]{0:T(128)S(1)}, f32[2]{0:T(128)S(1)}, u32[]{:S(2)}, u32[]{:S(2)}) collective-permute-start(f32[2]{0:T(128)S(1)} %fusion.28), channel_id=1, source_target_pairs={{0,16},{1,17},{2,18},{3,19},{4,20},{5,21},{6,22},{7,23},{8,24},{9,... | collective-permute-start | bytes 32 | tf_op jit(solution)/shard_map/ppermute | solution.py:97
  104.3 3.6 %collective-permute-start.14 = (f32[2]{0:T(128)S(1)}, f32[2]{0:T(128)S(1)}, u32[]{:S(2)}, u32[]{:S(2)}) collective-permute-start(f32[2]{0:T(128)S(1)} %add.63), channel_id=1, source_target_pairs={{0,32},{1,33},{2,34},{3,35},{4,36},{5,37},{6,38},{7,39},{8,40},{9,... | collective-permute-start | bytes 32 | tf_op jit(solution)/shard_map/ppermute | solution.py:97
  107.9 4.5 %collective-permute-start.15 = (f32[2]{0:T(128)S(1)}, f32[2]{0:T(128)S(1)}, u32[]{:S(2)}, u32[]{:S(2)}) collective-permute-start(f32[2]{0:T(128)S(1)} %add.64), channel_id=1, source_target_pairs={{0,64},{1,65},{2,66},{3,67},{4,68},{5,69},{6,70},{7,71},{8,72},{9,... | collective-permute-start | bytes 32 | tf_op jit(solution)/shard_map/ppermute | solution.py:97
  112.4 7.5 %collective-permute-start.16 = (f32[2]{0:T(128)S(1)}, f32[2]{0:T(128)S(1)}, u32[]{:S(2)}, u32[]{:S(2)}) collective-permute-start(f32[2]{0:T(128)S(1)} %add.65), channel_id=1, source_target_pairs={{0,128},{1,129},{2,130},{3,131},{4,132},{5,133},{6,134},{7,135},{8... | collective-permute-start | bytes 32 | tf_op jit(solution)/shard_map/ppermute | solution.py:97

commit v5 on v4

--- a/solution.py
+++ b/solution.py
@@ -20,6 +20,7 @@
 def tile_kernel(a_ref, b_ref, w_ref, o_ref, s_ref):
     n = a_ref.shape[0]
     lines = w_ref.shape[1]
+    nb = b_ref.shape[0] // lines
     width = a_ref.shape[1]
     groups = width // 128
     strips = lines // 8
@@ -61,25 +62,35 @@
                 o_ref[a, b, j + 1 : j + 2, :] = jnp.sum(acc[j], axis=0, keepdims=True)
             return carry2
 
-        lax.fori_loop(0, n, per_partner, 0)
+        lax.fori_loop(0, nb, per_partner, 0)
         return carry
 
     lax.fori_loop(0, n, per_image, 0)
 
 
-def pair_tile(own, other, table):
+def pair_stats(own_p, other, wide):
+    count, padded, radii = own_p.shape
+    part, lines, _ = other.shape
+    flops = 2 * count * part * lines * padded * radii + 12 * count * part * lines * padded
+    return pl.pallas_call(
+        tile_kernel,
+        out_shape=jax.ShapeDtypeStruct((count, part, 8, padded), jnp.float32),
+        in_specs=[pl.BlockSpec(memory_space=pltpu.VMEM)] * 3,
+        out_specs=pl.BlockSpec(memory_space=pltpu.VMEM),
+        scratch_shapes=[pltpu.VMEM((part * lines, padded), jnp.float32)],
+        compiler_params=pltpu.CompilerParams(vmem_limit_bytes=48 * 1024 * 1024),
+        cost_estimate=pl.CostEstimate(
+            flops=flops, transcendentals=count * part * lines * padded, bytes_accessed=2 * 1024 * 1024
+        ),
+    )(own_p, other.reshape(part * lines, radii), wide)
+
+
+def pair_tile(own, others, table):
     count, lines, radii = own.shape
     padded = ((lines + 127) // 128) * 128
     own_p = jnp.pad(own, ((0, 0), (0, padded - lines), (0, 0)))
     wide = jnp.broadcast_to(jnp.transpose(table)[:, :, None], (3, lines, 128))
-    stats = pl.pallas_call(
-        tile_kernel,
-        out_shape=jax.ShapeDtypeStruct((count, count, 8, padded), jnp.float32),
-        in_specs=[pl.BlockSpec(memory_space=pltpu.VMEM)] * 3,
-        out_specs=pl.BlockSpec(memory_space=pltpu.VMEM),
-        scratch_shapes=[pltpu.VMEM((count * lines, padded), jnp.float32)],
-        compiler_params=pltpu.CompilerParams(vmem_limit_bytes=48 * 1024 * 1024),
-    )(own_p, other.reshape(count * lines, radii), wide)
+    stats = jnp.concatenate([pair_stats(own_p, other, wide) for other in others], axis=1)
     stats = stats[:, :, :, :lines]
     top = stats[:, :, 0, :]
     peak = jnp.max(top, axis=2, keepdims=True)
@@ -116,12 +127,13 @@
             route.append((((i + c + 1) % nblk) * ncols + c, i * ncols + c))
     back = [(dst, src) for src, dst in route]
     fetch = lambda v: lax.ppermute(v, axes, route)
-    other = fetch(images)
+    half = count // 2
+    others = [fetch(images[:half]), fetch(images[half:])]
     other_partners = fetch(partners)
     other_counts = fetch(counts)
     other_start = fetch(start)
 
-    tile = pair_tile(images, other, table)
+    tile = pair_tile(images, others, table)
 
     slot_ids = jnp.arange(slots)
     plus = jnp.any((partners[0] == step + halo - 1) & (slot_ids < counts[0]))

time: 123 us -> 125 us (1.016)
  starting transfers between devices: 24.4 us -> 28.3 us
  waiting for transfers between devices: 54.5 us -> 52.3 us
  Pallas kernels: 22.8 us -> 24.2 us
    ppermute x5 -> x6, starting transfers between devices: 18.5 us -> 22.2 us  [body(): fetch = lambda v: lax.ppermute(v, axes, route)]
    ppermute x5 -> x6, waiting for transfers between devices: 8.47 us -> 6.31 us  [body(): fetch = lambda v: lax.ppermute(v, axes, route)]
    pallas_call x1 -> x2, Pallas kernels: 22.8 us -> 24.2 us  [pair_stats(): pl.pallas_call(tile_kernel, out_shape=jax.ShapeDtypeStruct((count, part,...]
  transfers between devices with their start and end apart: 17 -> 18, of which waited for: 13 -> 13; matrix products, arithmetic and copies ran while one was open for 6% -> 5% of each run, Pallas kernels for 19% -> 19%
where the time goes in v5:
time: 125 us
  waiting for transfers between devices  52.3 us (42%)
  starting transfers between devices  28.3 us (23%)
  Pallas kernels  24.2 us (19%)
  other arithmetic  9.07 us (7%)
  matrix products  5.78 us (5%)
  between operations  2.84 us (2%)
  local copies, waits for them, and re-layouts  2.2 us (2%)
    ppermute x10, waiting for transfers between devices, butterfly_sum(): value = value + lax.ppermute(value, axes, route)  36.8 us
    pallas_call x2, Pallas kernels, pair_stats(): pl.pallas_call(tile_kernel, out_shape=jax.ShapeDtypeStruct((count, part,...  24.2 us
    ppermute x6, starting transfers between devices, body(): fetch = lambda v: lax.ppermute(v, axes, route)  22.2 us
    ppermute x2, waiting for transfers between devices, apply(): part = forward + lax.ppermute(backward, axes, back)  9.23 us
    ppermute x6, waiting for transfers between devices, body(): fetch = lambda v: lax.ppermute(v, axes, route)  6.31 us
    ppermute x10, starting transfers between devices, butterfly_sum(): value = value + lax.ppermute(value, axes, route)  6.09 us
    add x8, other arithmetic, butterfly_sum(): value = value + lax.ppermute(value, axes, route)  2.71 us
    dot_general x1, matrix products, pair_tile(): rel = jnp.einsum('lp,abql->abpq', table, sums, precision=HIGH)  2.68 us
  transfers between devices with their start and end apart: 18, of which 13 were waited for; matrix products, arithmetic and copies ran while one was open for 5% of the time, Pallas kernels for 19%

profile of v5, /device:TPU:6, one launch (start us, length us, event | category | flops | bytes accessed | tf_op | source)
XLA Modules:
  0.0 124.7 jit_solution(10709114303878652021)
XLA Ops:
  0.6 1.2 fusion.28
  1.9 8.6 %collective-permute-start.1 = (bf16[4,360,128]{2,1,0:T(8,128)(2,1)S(1)}, bf16[4,360,128]{2,1,0:T(8,128)(2,1)S(1)}, u32[]{:S(2)}, u32[]{:S(2)}) collective-permute-start(bf16[4,360,128]{2,1,0:T(8,128)(2,1)S(1)} %get-tuple-element.9), channel_id=1, source_target_pairs={{4,0},{9,1},{14,2},{19,3},{8,4},{13,5},{18,6},{23,7},{12,8},{17,9}... | collective-permute-start | bytes 1105928 | tf_op jit(solution)/shard_map/ppermute | solution.py:129
  10.4 0.3 collective-permute-start
  10.8 3.6 %collective-permute-start.4 = (s32[1]{0:T(128)}, s32[1]{0:T(128)}, u32[]{:S(2)}, u32[]{:S(2)}) collective-permute-start(s32[1]{0:T(128)} %param.6), channel_id=1, source_target_pairs={{4,0},{9,1},{14,2},{19,3},{8,4},{13,5},{18,6},{23,7},{12,8},{17,9}... | collective-permute-start | bytes 20 | tf_op jit(solution)/shard_map/ppermute | solution.py:129
  14.4 0.3 collective-permute-start.3
  14.8 3.6 %collective-permute-start.2 = (f32[1,24]{1,0:T(1,128)S(1)}, f32[1,24]{1,0:T(1,128)S(1)}, u32[]{:S(2)}, u32[]{:S(2)}) collective-permute-start(f32[1,24]{1,0:T(1,128)S(1)} %copy-done.1), channel_id=1, source_target_pairs={{4,0},{9,1},{14,2},{19,3},{8,4},{13,5},{18,6},{23,7},{12,8},{17,9}... | collective-permute-start | bytes 296 | tf_op jit(solution)/shard_map/ppermute | solution.py:129
  19.1 0.6 fusion.18
  20.0 6.3 %collective-permute-done.4 = s32[1]{0:T(128)} collective-permute-done((s32[1]{0:T(128)}, s32[1]{0:T(128)}, u32[]{:S(2)}, u32[]{:S(2)}) %collective-permute-start.4) | collective-permute-done | bytes 36 | tf_op jit(solution)/shard_map/ppermute | solution.py:129
  26.3 1.3 %fusion.17 = pred[]{:T(512)} fusion(s32[1,8]{1,0:T(1,128)S(1)} %collective-permute-done.3, s32[]{:T(128)} %bitcast.14, s32[]{:T(128)S(6)} %sub.24), kind=kLoop, calls=%fused_computation.32 | loop fusion | flops 31 | bytes 41 | tf_op jit(solution)/shard_map/reduce_or | solution.py:140
  27.5 0.2 broadcast_in_dim.22.w_ref
  27.7 12.1 %shard_map.60 = f32[8,4,8,384]{3,2,1,0:T(8,128)S(1)} custom-call(bf16[8,384,128]{2,1,0:T(8,128)(2,1)S(1)} %pad.4.a_ref, bf16[1440,128]{1,0:T(8,128)(2,1)S(1)} %bitcast.84, f32[3,360,128]{2,1,0:T(8,128)S(1)} %broadcast_in_dim.22.w_ref), custom_call_target="tpu_custom_call" | custom-call | flops 1185546240 | bytes 2097152 | tf_op jit(solution)/shard_map/pallas_call | solution.py:75
  39.9 12.1 %shard_map.59 = f32[8,4,8,384]{3,2,1,0:T(8,128)S(1)} custom-call(bf16[8,384,128]{2,1,0:T(8,128)(2,1)S(1)} %pad.4.a_ref, bf16[1440,128]{1,0:T(8,128)(2,1)S(1)} %bitcast.83, f32[3,360,128]{2,1,0:T(8,128)S(1)} %broadcast_in_dim.22.w_ref), custom_call_target="tpu_custom_call" | custom-call | flops 1185546240 | bytes 2097152 | tf_op jit(solution)/shard_map/pallas_call | solution.py:75
  52.0 0.3 fusion.26
  52.4 0.2 fusion.11
  52.5 0.1 fusion.8
  52.7 2.7 %fusion = f32[3,8,3,8]{3,0,2,1:T(4,128)S(1)} fusion(f32[8,8,3,360]{3,2,1,0:T(4,128)S(1)} %fusion.8, f32[8,8]{1,0:T(8,128)S(1)} %fusion.11, f32[360,1]{0,1:T(1,128)S(1)} %get-tuple-element.13, f32[360,1]{0,1:T(1,128)S(1)} %get-tuple-element.14, f32[360,1]{0,1:T(1,128)S(1)} %fusion.20), kind=kOutput, calls=%fused_computation.1 | convolution fusion | flops 2491056 | bytes 283360 | tf_op jit(solution)/shard_map/lp,abql->abpq/dot_general | solution.py:100
  55.5 0.8 fusion.3
  56.3 7.7 %collective-permute-done.5 = f32[24]{0:T(128)S(1)} collective-permute-done((f32[24]{0:T(128)S(1)}, f32[24]{0:T(128)S(1)}, u32[]{:S(2)}, u32[]{:S(2)}) %collective-permute-start.5) | collective-permute-done | bytes 128 | tf_op jit(solution)/shard_map/ppermute | solution.py:147
  63.9 0.8 fusion.2
  64.7 0.4 collective-permute-start.6
  65.1 3.2 %collective-permute-done.6 = f32[24]{0:T(128)S(1)} collective-permute-done((f32[24]{0:T(128)S(1)}, f32[24]{0:T(128)S(1)}, u32[]{:S(2)}, u32[]{:S(2)}) %collective-permute-start.6) | collective-permute-done | bytes 128 | tf_op jit(solution)/shard_map/ppermute | solution.py:108
  68.3 0.9 collective-permute-start.7
  69.3 4.1 %collective-permute-done.7 = f32[24]{0:T(128)S(1)} collective-permute-done((f32[24]{0:T(128)S(1)}, f32[24]{0:T(128)S(1)}, u32[]{:S(2)}, u32[]{:S(2)}) %collective-permute-start.7) | collective-permute-done | bytes 128 | tf_op jit(solution)/shard_map/ppermute | solution.py:108
  73.4 0.7 multiply_reduce_fusion.1
  74.0 0.8 fusion.6
  74.8 5.6 %collective-permute-start.8 = (f32[24]{0:T(128)S(1)}, f32[24]{0:T(128)S(1)}, u32[]{:S(2)}, u32[]{:S(2)}) collective-permute-start(f32[24]{0:T(128)S(1)} %get-tuple-element.3), channel_id=1, source_target_pairs={{4,0},{9,1},{14,2},{19,3},{8,4},{13,5},{18,6},{23,7},{12,8},{17,9}... | collective-permute-start | bytes 296 | tf_op jit(solution)/shard_map/ppermute | solution.py:129
  80.5 1.5 %collective-permute-done.9 = f32[24]{0:T(128)S(1)} collective-permute-done((f32[24]{0:T(128)S(1)}, f32[24]{0:T(128)S(1)}, u32[]{:S(2)}, u32[]{:S(2)}) %collective-permute-start.9) | collective-permute-done | bytes 128 | tf_op jit(solution)/shard_map/ppermute | solution.py:147
  82.0 0.8 fusion.5
  82.8 3.6 %collective-permute-done.10 = f32[24]{0:T(128)S(1)} collective-permute-done((f32[24]{0:T(128)S(1)}, f32[24]{0:T(128)S(1)}, u32[]{:S(2)}, u32[]{:S(2)}) %collective-permute-start.10) | collective-permute-done | bytes 128 | tf_op jit(solution)/shard_map/ppermute | solution.py:108
  86.4 0.7 collective-permute-start.11
  87.0 4.4 %collective-permute-done.11 = f32[24]{0:T(128)S(1)} collective-permute-done((f32[24]{0:T(128)S(1)}, f32[24]{0:T(128)S(1)}, u32[]{:S(2)}, u32[]{:S(2)}) %collective-permute-start.11) | collective-permute-done | bytes 128 | tf_op jit(solution)/shard_map/ppermute | solution.py:108
  91.4 0.6 multiply_reduce_fusion
  92.0 1.3 %pad_maximum_fusion.3 = f32[2]{0:T(128)S(1)} fusion(f32[1]{0:T(128)} %bitcast.24, f32[1]{0:T(128)} %bitcast.19), kind=kLoop, calls=%fused_computation.39 | loop fusion | flops 2 | bytes 16 | tf_op jit(solution)/shard_map/stack | solution.py:152
  93.4 0.2 collective-permute-start.12
  93.6 1.1 collective-permute-done.12
  94.8 1.3 %fusion.32 = f32[2]{0:T(128)S(1)} fusion(f32[2]{0:T(128)S(1)} %collective-permute-done.12, f32[1]{0:T(128)} %bitcast.24, f32[1]{0:T(128)} %bitcast.19), kind=kLoop, calls=%fused_computation.52 | loop fusion | flops 4 | bytes 24 | tf_op jit(solution)/shard_map/add | solution.py:108
  96.1 0.7 collective-permute-start.13
  96.8 2.9 %collective-permute-done.13 = f32[2]{0:T(128)S(1)} collective-permute-done((f32[2]{0:T(128)S(1)}, f32[2]{0:T(128)S(1)}, u32[]{:S(2)}, u32[]{:S(2)}) %collective-permute-start.13) | collective-permute-done | bytes 40 | tf_op jit(solution)/shard_map/ppermute | solution.py:108
  99.7 1.3 %fusion.33 = f32[2]{0:T(128)S(1)} fusion(f32[2]{0:T(128)S(1)} %collective-permute-done.13, f32[2]{0:T(128)S(1)} %collective-permute-done.12, f32[1]{0:T(128)} %bitcast.24, f32[1]{0:T(128)} %bitcast.19), kind=kLoop, calls=%fused_computation.53 | loop fusion | flops 6 | bytes 32 | tf_op jit(solution)/shard_map/add | solution.py:108
  101.1 5.1 %collective-permute-done.14 = f32[2]{0:T(128)S(1)} collective-permute-done((f32[2]{0:T(128)S(1)}, f32[2]{0:T(128)S(1)}, u32[]{:S(2)}, u32[]{:S(2)}) %collective-permute-start.14) | collective-permute-done | bytes 40 | tf_op jit(solution)/shard_map/ppermute | solution.py:108
  106.1 3.6 %collective-permute-done.15 = f32[2]{0:T(128)S(1)} collective-permute-done((f32[2]{0:T(128)S(1)}, f32[2]{0:T(128)S(1)}, u32[]{:S(2)}, u32[]{:S(2)}) %collective-permute-start.15) | collective-permute-done | bytes 40 | tf_op jit(solution)/shard_map/ppermute | solution.py:108
  109.7 0.9 collective-permute-start.16
  110.7 3.5 %collective-permute-done.16 = f32[2]{0:T(128)S(1)} collective-permute-done((f32[2]{0:T(128)S(1)}, f32[2]{0:T(128)S(1)}, u32[]{:S(2)}, u32[]{:S(2)}) %collective-permute-start.16) | collective-permute-done | bytes 40 | tf_op jit(solution)/shard_map/ppermute | solution.py:108
  114.2 2.2 %collective-permute-start.17 = (f32[2]{0:T(128)S(1)}, f32[2]{0:T(128)S(1)}, u32[]{:S(2)}, u32[]{:S(2)}) collective-permute-start(f32[2]{0:T(128)S(1)} %add.65), channel_id=1, source_target_pairs={{0,128},{1,129},{2,130},{3,131},{4,132},{5,133},{6,134},{7,135},{8... | collective-permute-start | bytes 32 | tf_op jit(solution)/shard_map/ppermute | solution.py:108
  116.4 5.2 %collective-permute-done.17 = f32[2]{0:T(128)S(1)} collective-permute-done((f32[2]{0:T(128)S(1)}, f32[2]{0:T(128)S(1)}, u32[]{:S(2)}, u32[]{:S(2)}) %collective-permute-start.17) | collective-permute-done | bytes 40 | tf_op jit(solution)/shard_map/ppermute | solution.py:108
  121.7 0.6 fusion.29
  123.0 0.5 divide_bitcast_fusion.1
  124.2 0.5 divide_bitcast_fusion
  (29 shorter events, 0.5 us)
Async XLA Ops:
  0.6 19.2 %copy-start = (bf16[8,360,128]{2,1,0:T(8,128)(2,1)S(1)}, bf16[8,360,128]{2,1,0:T(8,128)(2,1)}, u32[]{:S(2)}) copy-start(bf16[8,360,128]{2,1,0:T(8,128)(2,1)} %param.4) | copy-start | bytes 2211844
  1.9 12.6 %copy-start.2 = (s32[1,8]{1,0:T(1,128)S(1)}, s32[1,8]{1,0:T(1,128)}, u32[]{:S(2)}) copy-start(s32[1,8]{1,0:T(1,128)} %param.5) | copy-start | bytes 100
  1.9 12.9 %copy-start.1 = (f32[1,24]{1,0:T(1,128)S(1)}, f32[1,24]{1,0:T(1,128)}, u32[]{:S(2)}) copy-start(f32[1,24]{1,0:T(1,128)} %param.7) | copy-start | bytes 292
  1.9 25.6 %collective-permute-start.1 = (bf16[4,360,128]{2,1,0:T(8,128)(2,1)S(1)}, bf16[4,360,128]{2,1,0:T(8,128)(2,1)S(1)}, u32[]{:S(2)}, u32[]{:S(2)}) collective-permute-start(bf16[4,360,128]{2,1,0:T(8,128)(2,1)S(1)} %get-tuple-element.9), channel_id=1, source_target_pairs={{4,0},{9,1},{14,2},{19,3},{8,4},{13,5},{18,6},{23,7},{12,8},{17,9}... | collective-permute-start | bytes 1105928 | tf_op jit(solution)/shard_map/ppermute | solution.py:129
  10.4 29.4 %collective-permute-start = (bf16[4,360,128]{2,1,0:T(8,128)(2,1)S(1)}, bf16[4,360,128]{2,1,0:T(8,128)(2,1)S(1)}, u32[]{:S(2)}, u32[]{:S(2)}) collective-permute-start(bf16[4,360,128]{2,1,0:T(8,128)(2,1)S(1)} %get-tuple-element.10), channel_id=1, source_target_pairs={{4,0},{9,1},{14,2},{19,3},{8,4},{13,5},{18,6},{23,7},{12,8},{17,9}... | collective-permute-start | bytes 1105928 | tf_op jit(solution)/shard_map/ppermute | solution.py:129
  10.8 15.5 %collective-permute-start.4 = (s32[1]{0:T(128)}, s32[1]{0:T(128)}, u32[]{:S(2)}, u32[]{:S(2)}) collective-permute-start(s32[1]{0:T(128)} %param.6), channel_id=1, source_target_pairs={{4,0},{9,1},{14,2},{19,3},{8,4},{13,5},{18,6},{23,7},{12,8},{17,9}... | collective-permute-start | bytes 20 | tf_op jit(solution)/shard_map/ppermute | solution.py:129
  14.4 11.8 %collective-permute-start.3 = (s32[1,8]{1,0:T(1,128)S(1)}, s32[1,8]{1,0:T(1,128)S(1)}, u32[]{:S(2)}, u32[]{:S(2)}) collective-permute-start(s32[1,8]{1,0:T(1,128)S(1)} %copy-done.2), channel_id=1, source_target_pairs={{4,0},{9,1},{14,2},{19,3},{8,4},{13,5},{18,6},{23,7},{12,8},{17,9}... | collective-permute-start | bytes 104 | tf_op jit(solution)/shard_map/ppermute | solution.py:129
  14.8 41.5 %collective-permute-start.2 = (f32[1,24]{1,0:T(1,128)S(1)}, f32[1,24]{1,0:T(1,128)S(1)}, u32[]{:S(2)}, u32[]{:S(2)}) collective-permute-start(f32[1,24]{1,0:T(1,128)S(1)} %copy-done.1), channel_id=1, source_target_pairs={{4,0},{9,1},{14,2},{19,3},{8,4},{13,5},{18,6},{23,7},{12,8},{17,9}... | collective-permute-start | bytes 296 | tf_op jit(solution)/shard_map/ppermute | solution.py:129
  56.2 7.7 %collective-permute-start.5 = (f32[24]{0:T(128)S(1)}, f32[24]{0:T(128)S(1)}, u32[]{:S(2)}, u32[]{:S(2)}) collective-permute-start(f32[24]{0:T(128)S(1)} %fusion.3), channel_id=1, source_target_pairs={{0,4},{1,9},{2,14},{3,19},{4,8},{5,13},{6,18},{7,23},{8,12},{9,17}... | collective-permute-start | bytes 296 | tf_op jit(solution)/shard_map/ppermute | solution.py:147
  64.7 3.6 %collective-permute-start.6 = (f32[24]{0:T(128)S(1)}, f32[24]{0:T(128)S(1)}, u32[]{:S(2)}, u32[]{:S(2)}) collective-permute-start(f32[24]{0:T(128)S(1)} %fusion.2), channel_id=1, source_target_pairs={{0,1},{1,0},{2,3},{3,2},{4,5},{5,4},{6,7},{7,6},{8,9},{9,8},{10,11... | collective-permute-start | bytes 296 | tf_op jit(solution)/shard_map/ppermute | solution.py:108
  68.3 5.1 %collective-permute-start.7 = (f32[24]{0:T(128)S(1)}, f32[24]{0:T(128)S(1)}, u32[]{:S(2)}, u32[]{:S(2)}) collective-permute-start(f32[24]{0:T(128)S(1)} %add.56), channel_id=1, source_target_pairs={{0,2},{1,3},{2,0},{3,1},{4,6},{5,7},{6,4},{7,5},{8,10},{9,11},{10,... | collective-permute-start | bytes 296 | tf_op jit(solution)/shard_map/ppermute | solution.py:108
  74.8 7.2 %collective-permute-start.9 = (f32[24]{0:T(128)S(1)}, f32[24]{0:T(128)S(1)}, u32[]{:S(2)}, u32[]{:S(2)}) collective-permute-start(f32[24]{0:T(128)S(1)} %fusion.6), channel_id=1, source_target_pairs={{0,4},{1,9},{2,14},{3,19},{4,8},{5,13},{6,18},{7,23},{8,12},{9,17}... | collective-permute-start | bytes 296 | tf_op jit(solution)/shard_map/ppermute | solution.py:147
  74.8 7.2 %collective-permute-start.8 = (f32[24]{0:T(128)S(1)}, f32[24]{0:T(128)S(1)}, u32[]{:S(2)}, u32[]{:S(2)}) collective-permute-start(f32[24]{0:T(128)S(1)} %get-tuple-element.3), channel_id=1, source_target_pairs={{4,0},{9,1},{14,2},{19,3},{8,4},{13,5},{18,6},{23,7},{12,8},{17,9}... | collective-permute-start | bytes 296 | tf_op jit(solution)/shard_map/ppermute | solution.py:129
  82.8 3.6 %collective-permute-start.10 = (f32[24]{0:T(128)S(1)}, f32[24]{0:T(128)S(1)}, u32[]{:S(2)}, u32[]{:S(2)}) collective-permute-start(f32[24]{0:T(128)S(1)} %fusion.5), channel_id=1, source_target_pairs={{0,1},{1,0},{2,3},{3,2},{4,5},{5,4},{6,7},{7,6},{8,9},{9,8},{10,11... | collective-permute-start | bytes 296 | tf_op jit(solution)/shard_map/ppermute | solution.py:108
  86.4 5.1 %collective-permute-start.11 = (f32[24]{0:T(128)S(1)}, f32[24]{0:T(128)S(1)}, u32[]{:S(2)}, u32[]{:S(2)}) collective-permute-start(f32[24]{0:T(128)S(1)} %add.59), channel_id=1, source_target_pairs={{0,2},{1,3},{2,0},{3,1},{4,6},{5,7},{6,4},{7,5},{8,10},{9,11},{10,... | collective-permute-start | bytes 296 | tf_op jit(solution)/shard_map/ppermute | solution.py:108
  93.4 1.4 %collective-permute-start.12 = (f32[2]{0:T(128)S(1)}, f32[2]{0:T(128)S(1)}, u32[]{:S(2)}, u32[]{:S(2)}) collective-permute-start(f32[2]{0:T(128)S(1)} %pad_maximum_fusion.3), channel_id=1, source_target_pairs={{0,4},{1,5},{2,6},{3,7},{4,0},{5,1},{6,2},{7,3},{8,12},{9,13},{10,... | collective-permute-start | bytes 32 | tf_op jit(solution)/shard_map/ppermute | solution.py:108
  96.1 3.6 %collective-permute-start.13 = (f32[2]{0:T(128)S(1)}, f32[2]{0:T(128)S(1)}, u32[]{:S(2)}, u32[]{:S(2)}) collective-permute-start(f32[2]{0:T(128)S(1)} %fusion.32), channel_id=1, source_target_pairs={{0,8},{1,9},{2,10},{3,11},{4,12},{5,13},{6,14},{7,15},{8,0},{9,1},... | collective-permute-start | bytes 32 | tf_op jit(solution)/shard_map/ppermute | solution.py:108
  101.0 5.1 %collective-permute-start.14 = (f32[2]{0:T(128)S(1)}, f32[2]{0:T(128)S(1)}, u32[]{:S(2)}, u32[]{:S(2)}) collective-permute-start(f32[2]{0:T(128)S(1)} %fusion.33), channel_id=1, source_target_pairs={{0,16},{1,17},{2,18},{3,19},{4,20},{5,21},{6,22},{7,23},{8,24},{9,... | collective-permute-start | bytes 32 | tf_op jit(solution)/shard_map/ppermute | solution.py:108
  106.1 3.6 %collective-permute-start.15 = (f32[2]{0:T(128)S(1)}, f32[2]{0:T(128)S(1)}, u32[]{:S(2)}, u32[]{:S(2)}) collective-permute-start(f32[2]{0:T(128)S(1)} %add.63), channel_id=1, source_target_pairs={{0,32},{1,33},{2,34},{3,35},{4,36},{5,37},{6,38},{7,39},{8,40},{9,... | collective-permute-start | bytes 32 | tf_op jit(solution)/shard_map/ppermute | solution.py:108
  109.7 4.5 %collective-permute-start.16 = (f32[2]{0:T(128)S(1)}, f32[2]{0:T(128)S(1)}, u32[]{:S(2)}, u32[]{:S(2)}) collective-permute-start(f32[2]{0:T(128)S(1)} %add.64), channel_id=1, source_target_pairs={{0,64},{1,65},{2,66},{3,67},{4,68},{5,69},{6,70},{7,71},{8,72},{9,... | collective-permute-start | bytes 32 | tf_op jit(solution)/shard_map/ppermute | solution.py:108
  114.2 7.5 %collective-permute-start.17 = (f32[2]{0:T(128)S(1)}, f32[2]{0:T(128)S(1)}, u32[]{:S(2)}, u32[]{:S(2)}) collective-permute-start(f32[2]{0:T(128)S(1)} %add.65), channel_id=1, source_target_pairs={{0,128},{1,129},{2,130},{3,131},{4,132},{5,133},{6,134},{7,135},{8... | collective-permute-start | bytes 32 | tf_op jit(solution)/shard_map/ppermute | solution.py:108

commit v6 on v5

--- a/solution.py
+++ b/solution.py
@@ -128,7 +128,9 @@
     back = [(dst, src) for src, dst in route]
     fetch = lambda v: lax.ppermute(v, axes, route)
     half = count // 2
-    others = [fetch(images[:half]), fetch(images[half:])]
+    first_half = fetch(images[:half])
+    second_src, first_half = lax.optimization_barrier((images[half:], first_half))
+    others = [first_half, fetch(second_src)]
     other_partners = fetch(partners)
     other_counts = fetch(counts)
     other_start = fetch(start)

time: 125 us -> 123 us (0.984)
  waiting for transfers between devices: 52.3 us -> 50.2 us
    ppermute x6, waiting for transfers between devices: 6.31 us -> 2.17 us  [body(): fetch = lambda v: lax.ppermute(v, axes, route)]
    ppermute x10, starting transfers between devices: 6.09 us -> 3.54 us  [butterfly_sum(): value = value + lax.ppermute(value, axes, route)]
    ppermute x10, waiting for transfers between devices: 36.8 us -> 39.3 us  [butterfly_sum(): value = value + lax.ppermute(value, axes, route)]
    ppermute x6, starting transfers between devices: 22.2 us -> 24.6 us  [body(): fetch = lambda v: lax.ppermute(v, axes, route)]
  transfers between devices with their start and end apart: 18 -> 18, of which waited for: 13 -> 13; matrix products, arithmetic and copies ran while one was open for 5% -> 5% of each run, Pallas kernels for 19% -> 20%
where the time goes in v6:
time: 123 us
  waiting for transfers between devices  50.2 us (41%)
  starting transfers between devices  28.2 us (23%)
  Pallas kernels  24.2 us (20%)
  other arithmetic  9.07 us (7%)
  matrix products  5.78 us (5%)
  between operations  2.86 us (2%)
  local copies, waits for them, and re-layouts  2.2 us (2%)
    ppermute x10, waiting for transfers between devices, butterfly_sum(): value = value + lax.ppermute(value, axes, route)  39.3 us
    ppermute x6, starting transfers between devices, body(): fetch = lambda v: lax.ppermute(v, axes, route)  24.6 us
    pallas_call x2, Pallas kernels, pair_stats(): pl.pallas_call(tile_kernel, out_shape=jax.ShapeDtypeStruct((count, part,...  24.2 us
    ppermute x2, waiting for transfers between devices, apply(): part = forward + lax.ppermute(backward, axes, back)  8.72 us
    ppermute x10, starting transfers between devices, butterfly_sum(): value = value + lax.ppermute(value, axes, route)  3.54 us
    add x8, other arithmetic, butterfly_sum(): value = value + lax.ppermute(value, axes, route)  2.71 us
    dot_general x1, matrix products, pair_tile(): rel = jnp.einsum('lp,abql->abpq', table, sums, precision=HIGH)  2.68 us
  transfers between devices with their start and end apart: 18, of which 13 were waited for; matrix products, arithmetic and copies ran while one was open for 5% of the time, Pallas kernels for 20%

profile of v6, /device:TPU:6, one launch (start us, length us, event | category | flops | bytes accessed | tf_op | source)
XLA Modules:
  0.0 122.5 jit_solution(12239768897474099674)
XLA Ops:
  0.6 1.2 fusion.28
  1.9 8.6 %collective-permute-start = (bf16[4,360,128]{2,1,0:T(8,128)(2,1)S(1)}, bf16[4,360,128]{2,1,0:T(8,128)(2,1)S(1)}, u32[]{:S(2)}, u32[]{:S(2)}) collective-permute-start(bf16[4,360,128]{2,1,0:T(8,128)(2,1)S(1)} %get-tuple-element.13), channel_id=1, source_target_pairs={{4,0},{9,1},{14,2},{19,3},{8,4},{13,5},{18,6},{23,7},{12,8},{17,9}... | collective-permute-start | bytes 1105928 | tf_op jit(solution)/shard_map/ppermute | solution.py:129
  10.4 0.3 collective-permute-start.4
  10.8 3.6 %collective-permute-start.3 = (s32[1,8]{1,0:T(1,128)S(1)}, s32[1,8]{1,0:T(1,128)S(1)}, u32[]{:S(2)}, u32[]{:S(2)}) collective-permute-start(s32[1,8]{1,0:T(1,128)S(1)} %copy-done.2), channel_id=1, source_target_pairs={{4,0},{9,1},{14,2},{19,3},{8,4},{13,5},{18,6},{23,7},{12,8},{17,9}... | collective-permute-start | bytes 104 | tf_op jit(solution)/shard_map/ppermute | solution.py:129
  14.4 0.3 collective-permute-start.2
  15.4 0.1 multiply_cosine_fusion
  15.5 0.6 fusion.18
  16.2 2.2 %collective-permute-done = bf16[4,360,128]{2,1,0:T(8,128)(2,1)S(1)} collective-permute-done((bf16[4,360,128]{2,1,0:T(8,128)(2,1)S(1)}, bf16[4,360,128]{2,1,0:T(8,128)(2,1)S(1)}, u32[]{:S(2)}, u32[]{:S(2)}) %collective-permute-start) | collective-permute-done | bytes 368672 | tf_op jit(solution)/shard_map/ppermute | solution.py:129
  18.3 6.1 %collective-permute-start.1 = (bf16[4,360,128]{2,1,0:T(8,128)(2,1)S(1)}, bf16[4,360,128]{2,1,0:T(8,128)(2,1)S(1)}, u32[]{:S(2)}, u32[]{:S(2)}) collective-permute-start(bf16[4,360,128]{2,1,0:T(8,128)(2,1)S(1)} %get-tuple-element.5), channel_id=1, source_target_pairs={{4,0},{9,1},{14,2},{19,3},{8,4},{13,5},{18,6},{23,7},{12,8},{17,9}... | collective-permute-start | bytes 1105928 | tf_op jit(solution)/shard_map/ppermute | solution.py:129
  24.6 1.3 %fusion.17 = pred[]{:T(512)} fusion(s32[1,8]{1,0:T(1,128)S(1)} %collective-permute-done.3, s32[]{:T(128)} %bitcast.14, s32[]{:T(128)S(6)} %sub.24), kind=kLoop, calls=%fused_computation.32 | loop fusion | flops 31 | bytes 41 | tf_op jit(solution)/shard_map/reduce_or | solution.py:142
  25.8 0.2 broadcast_in_dim.22.w_ref
  26.1 12.1 %shard_map.59 = f32[8,4,8,384]{3,2,1,0:T(8,128)S(1)} custom-call(bf16[8,384,128]{2,1,0:T(8,128)(2,1)S(1)} %pad.4.a_ref, bf16[1440,128]{1,0:T(8,128)(2,1)S(1)} %bitcast.83, f32[3,360,128]{2,1,0:T(8,128)S(1)} %broadcast_in_dim.22.w_ref), custom_call_target="tpu_custom_call" | custom-call | flops 1185546240 | bytes 2097152 | tf_op jit(solution)/shard_map/pallas_call | solution.py:75
  38.2 12.1 %shard_map.60 = f32[8,4,8,384]{3,2,1,0:T(8,128)S(1)} custom-call(bf16[8,384,128]{2,1,0:T(8,128)(2,1)S(1)} %pad.4.a_ref, bf16[1440,128]{1,0:T(8,128)(2,1)S(1)} %bitcast.84, f32[3,360,128]{2,1,0:T(8,128)S(1)} %broadcast_in_dim.22.w_ref), custom_call_target="tpu_custom_call" | custom-call | flops 1185546240 | bytes 2097152 | tf_op jit(solution)/shard_map/pallas_call | solution.py:75
  50.3 0.3 fusion.26
  50.6 0.1 exponential_bitcast_fusion
  50.7 0.2 fusion.11
  50.9 0.1 fusion.8
  51.0 2.7 %fusion = f32[3,8,3,8]{3,0,2,1:T(4,128)S(1)} fusion(f32[8,8,3,360]{3,2,1,0:T(4,128)S(1)} %fusion.8, f32[8,8]{1,0:T(8,128)S(1)} %fusion.11, f32[360,1]{0,1:T(1,128)S(1)} %get-tuple-element.17, f32[360,1]{0,1:T(1,128)S(1)} %get-tuple-element.18, f32[360,1]{0,1:T(1,128)S(1)} %fusion.20), kind=kOutput, calls=%fused_computation.1 | convolution fusion | flops 2491056 | bytes 283360 | tf_op jit(solution)/shard_map/lp,abql->abpq/dot_general | solution.py:100
  53.8 0.8 fusion.3
  54.6 7.2 %collective-permute-done.5 = f32[24]{0:T(128)S(1)} collective-permute-done((f32[24]{0:T(128)S(1)}, f32[24]{0:T(128)S(1)}, u32[]{:S(2)}, u32[]{:S(2)}) %collective-permute-start.5) | collective-permute-done | bytes 128 | tf_op jit(solution)/shard_map/ppermute | solution.py:149
  61.8 0.8 fusion.2
  62.6 3.6 %collective-permute-done.6 = f32[24]{0:T(128)S(1)} collective-permute-done((f32[24]{0:T(128)S(1)}, f32[24]{0:T(128)S(1)}, u32[]{:S(2)}, u32[]{:S(2)}) %collective-permute-start.6) | collective-permute-done | bytes 128 | tf_op jit(solution)/shard_map/ppermute | solution.py:108
  66.1 0.7 collective-permute-start.7
  66.8 4.4 %collective-permute-done.7 = f32[24]{0:T(128)S(1)} collective-permute-done((f32[24]{0:T(128)S(1)}, f32[24]{0:T(128)S(1)}, u32[]{:S(2)}, u32[]{:S(2)}) %collective-permute-start.7) | collective-permute-done | bytes 128 | tf_op jit(solution)/shard_map/ppermute | solution.py:108
  71.2 0.7 multiply_reduce_fusion.1
  71.9 0.8 fusion.6
  72.6 5.6 %collective-permute-start.8 = (f32[24]{0:T(128)S(1)}, f32[24]{0:T(128)S(1)}, u32[]{:S(2)}, u32[]{:S(2)}) collective-permute-start(f32[24]{0:T(128)S(1)} %get-tuple-element.7), channel_id=1, source_target_pairs={{4,0},{9,1},{14,2},{19,3},{8,4},{13,5},{18,6},{23,7},{12,8},{17,9}... | collective-permute-start | bytes 296 | tf_op jit(solution)/shard_map/ppermute | solution.py:129
  78.3 1.5 %collective-permute-done.9 = f32[24]{0:T(128)S(1)} collective-permute-done((f32[24]{0:T(128)S(1)}, f32[24]{0:T(128)S(1)}, u32[]{:S(2)}, u32[]{:S(2)}) %collective-permute-start.9) | collective-permute-done | bytes 128 | tf_op jit(solution)/shard_map/ppermute | solution.py:149
  79.8 0.8 fusion.5
  80.6 3.6 %collective-permute-done.10 = f32[24]{0:T(128)S(1)} collective-permute-done((f32[24]{0:T(128)S(1)}, f32[24]{0:T(128)S(1)}, u32[]{:S(2)}, u32[]{:S(2)}) %collective-permute-start.10) | collective-permute-done | bytes 128 | tf_op jit(solution)/shard_map/ppermute | solution.py:108
  84.2 0.4 collective-permute-start.11
  84.5 4.7 %collective-permute-done.11 = f32[24]{0:T(128)S(1)} collective-permute-done((f32[24]{0:T(128)S(1)}, f32[24]{0:T(128)S(1)}, u32[]{:S(2)}, u32[]{:S(2)}) %collective-permute-start.11) | collective-permute-done | bytes 128 | tf_op jit(solution)/shard_map/ppermute | solution.py:108
  89.3 0.6 multiply_reduce_fusion
  89.9 1.3 %pad_maximum_fusion.3 = f32[2]{0:T(128)S(1)} fusion(f32[1]{0:T(128)} %bitcast.24, f32[1]{0:T(128)} %bitcast.19), kind=kLoop, calls=%fused_computation.39 | loop fusion | flops 2 | bytes 16 | tf_op jit(solution)/shard_map/stack | solution.py:154
  91.2 0.2 collective-permute-start.12
  91.4 1.1 collective-permute-done.12
  92.6 1.3 %fusion.32 = f32[2]{0:T(128)S(1)} fusion(f32[2]{0:T(128)S(1)} %collective-permute-done.12, f32[1]{0:T(128)} %bitcast.24, f32[1]{0:T(128)} %bitcast.19), kind=kLoop, calls=%fused_computation.52 | loop fusion | flops 4 | bytes 24 | tf_op jit(solution)/shard_map/add | solution.py:108
  93.9 0.7 collective-permute-start.13
  94.6 2.9 %collective-permute-done.13 = f32[2]{0:T(128)S(1)} collective-permute-done((f32[2]{0:T(128)S(1)}, f32[2]{0:T(128)S(1)}, u32[]{:S(2)}, u32[]{:S(2)}) %collective-permute-start.13) | collective-permute-done | bytes 40 | tf_op jit(solution)/shard_map/ppermute | solution.py:108
  97.5 1.3 %fusion.33 = f32[2]{0:T(128)S(1)} fusion(f32[2]{0:T(128)S(1)} %collective-permute-done.13, f32[2]{0:T(128)S(1)} %collective-permute-done.12, f32[1]{0:T(128)} %bitcast.24, f32[1]{0:T(128)} %bitcast.19), kind=kLoop, calls=%fused_computation.53 | loop fusion | flops 6 | bytes 32 | tf_op jit(solution)/shard_map/add | solution.py:108
  98.9 5.1 %collective-permute-done.14 = f32[2]{0:T(128)S(1)} collective-permute-done((f32[2]{0:T(128)S(1)}, f32[2]{0:T(128)S(1)}, u32[]{:S(2)}, u32[]{:S(2)}) %collective-permute-start.14) | collective-permute-done | bytes 40 | tf_op jit(solution)/shard_map/ppermute | solution.py:108
  104.0 3.6 %collective-permute-done.15 = f32[2]{0:T(128)S(1)} collective-permute-done((f32[2]{0:T(128)S(1)}, f32[2]{0:T(128)S(1)}, u32[]{:S(2)}, u32[]{:S(2)}) %collective-permute-start.15) | collective-permute-done | bytes 40 | tf_op jit(solution)/shard_map/ppermute | solution.py:108
  107.5 4.5 %collective-permute-done.16 = f32[2]{0:T(128)S(1)} collective-permute-done((f32[2]{0:T(128)S(1)}, f32[2]{0:T(128)S(1)}, u32[]{:S(2)}, u32[]{:S(2)}) %collective-permute-start.16) | collective-permute-done | bytes 40 | tf_op jit(solution)/shard_map/ppermute | solution.py:108
  112.0 1.6 %collective-permute-start.17 = (f32[2]{0:T(128)S(1)}, f32[2]{0:T(128)S(1)}, u32[]{:S(2)}, u32[]{:S(2)}) collective-permute-start(f32[2]{0:T(128)S(1)} %add.65), channel_id=1, source_target_pairs={{0,128},{1,129},{2,130},{3,131},{4,132},{5,133},{6,134},{7,135},{8... | collective-permute-start | bytes 32 | tf_op jit(solution)/shard_map/ppermute | solution.py:108
  113.6 5.9 %collective-permute-done.17 = f32[2]{0:T(128)S(1)} collective-permute-done((f32[2]{0:T(128)S(1)}, f32[2]{0:T(128)S(1)}, u32[]{:S(2)}, u32[]{:S(2)}) %collective-permute-start.17) | collective-permute-done | bytes 40 | tf_op jit(solution)/shard_map/ppermute | solution.py:108
  119.5 0.6 fusion.29
  120.8 0.5 divide_bitcast_fusion.1
  122.0 0.5 divide_bitcast_fusion
  (29 shorter events, 0.3 us)
Async XLA Ops:
  0.6 23.8 %copy-start = (bf16[8,360,128]{2,1,0:T(8,128)(2,1)S(1)}, bf16[8,360,128]{2,1,0:T(8,128)(2,1)}, u32[]{:S(2)}) copy-start(bf16[8,360,128]{2,1,0:T(8,128)(2,1)} %param.4) | copy-start | bytes 2211844
  1.9 8.9 %copy-start.2 = (s32[1,8]{1,0:T(1,128)S(1)}, s32[1,8]{1,0:T(1,128)}, u32[]{:S(2)}) copy-start(s32[1,8]{1,0:T(1,128)} %param.5) | copy-start | bytes 100
  1.9 12.6 %copy-start.1 = (f32[1,24]{1,0:T(1,128)S(1)}, f32[1,24]{1,0:T(1,128)}, u32[]{:S(2)}) copy-start(f32[1,24]{1,0:T(1,128)} %param.7) | copy-start | bytes 292
  1.9 16.4 %collective-permute-start = (bf16[4,360,128]{2,1,0:T(8,128)(2,1)S(1)}, bf16[4,360,128]{2,1,0:T(8,128)(2,1)S(1)}, u32[]{:S(2)}, u32[]{:S(2)}) collective-permute-start(bf16[4,360,128]{2,1,0:T(8,128)(2,1)S(1)} %get-tuple-element.13), channel_id=1, source_target_pairs={{4,0},{9,1},{14,2},{19,3},{8,4},{13,5},{18,6},{23,7},{12,8},{17,9}... | collective-permute-start | bytes 1105928 | tf_op jit(solution)/shard_map/ppermute | solution.py:129
  10.4 14.1 %collective-permute-start.4 = (s32[1]{0:T(128)}, s32[1]{0:T(128)}, u32[]{:S(2)}, u32[]{:S(2)}) collective-permute-start(s32[1]{0:T(128)} %param.6), channel_id=1, source_target_pairs={{4,0},{9,1},{14,2},{19,3},{8,4},{13,5},{18,6},{23,7},{12,8},{17,9}... | collective-permute-start | bytes 20 | tf_op jit(solution)/shard_map/ppermute | solution.py:129
  10.8 13.8 %collective-permute-start.3 = (s32[1,8]{1,0:T(1,128)S(1)}, s32[1,8]{1,0:T(1,128)S(1)}, u32[]{:S(2)}, u32[]{:S(2)}) collective-permute-start(s32[1,8]{1,0:T(1,128)S(1)} %copy-done.2), channel_id=1, source_target_pairs={{4,0},{9,1},{14,2},{19,3},{8,4},{13,5},{18,6},{23,7},{12,8},{17,9}... | collective-permute-start | bytes 104 | tf_op jit(solution)/shard_map/ppermute | solution.py:129
  14.4 40.2 %collective-permute-start.2 = (f32[1,24]{1,0:T(1,128)S(1)}, f32[1,24]{1,0:T(1,128)S(1)}, u32[]{:S(2)}, u32[]{:S(2)}) collective-permute-start(f32[1,24]{1,0:T(1,128)S(1)} %copy-done.1), channel_id=1, source_target_pairs={{4,0},{9,1},{14,2},{19,3},{8,4},{13,5},{18,6},{23,7},{12,8},{17,9}... | collective-permute-start | bytes 296 | tf_op jit(solution)/shard_map/ppermute | solution.py:129
  18.3 19.9 %collective-permute-start.1 = (bf16[4,360,128]{2,1,0:T(8,128)(2,1)S(1)}, bf16[4,360,128]{2,1,0:T(8,128)(2,1)S(1)}, u32[]{:S(2)}, u32[]{:S(2)}) collective-permute-start(bf16[4,360,128]{2,1,0:T(8,128)(2,1)S(1)} %get-tuple-element.5), channel_id=1, source_target_pairs={{4,0},{9,1},{14,2},{19,3},{8,4},{13,5},{18,6},{23,7},{12,8},{17,9}... | collective-permute-start | bytes 1105928 | tf_op jit(solution)/shard_map/ppermute | solution.py:129
  54.6 7.2 %collective-permute-start.5 = (f32[24]{0:T(128)S(1)}, f32[24]{0:T(128)S(1)}, u32[]{:S(2)}, u32[]{:S(2)}) collective-permute-start(f32[24]{0:T(128)S(1)} %fusion.3), channel_id=1, source_target_pairs={{0,4},{1,9},{2,14},{3,19},{4,8},{5,13},{6,18},{7,23},{8,12},{9,17}... | collective-permute-start | bytes 296 | tf_op jit(solution)/shard_map/ppermute | solution.py:149
  62.5 3.6 %collective-permute-start.6 = (f32[24]{0:T(128)S(1)}, f32[24]{0:T(128)S(1)}, u32[]{:S(2)}, u32[]{:S(2)}) collective-permute-start(f32[24]{0:T(128)S(1)} %fusion.2), channel_id=1, source_target_pairs={{0,1},{1,0},{2,3},{3,2},{4,5},{5,4},{6,7},{7,6},{8,9},{9,8},{10,11... | collective-permute-start | bytes 296 | tf_op jit(solution)/shard_map/ppermute | solution.py:108
  66.1 5.1 %collective-permute-start.7 = (f32[24]{0:T(128)S(1)}, f32[24]{0:T(128)S(1)}, u32[]{:S(2)}, u32[]{:S(2)}) collective-permute-start(f32[24]{0:T(128)S(1)} %add.56), channel_id=1, source_target_pairs={{0,2},{1,3},{2,0},{3,1},{4,6},{5,7},{6,4},{7,5},{8,10},{9,11},{10,... | collective-permute-start | bytes 296 | tf_op jit(solution)/shard_map/ppermute | solution.py:108
  72.6 7.2 %collective-permute-start.9 = (f32[24]{0:T(128)S(1)}, f32[24]{0:T(128)S(1)}, u32[]{:S(2)}, u32[]{:S(2)}) collective-permute-start(f32[24]{0:T(128)S(1)} %fusion.6), channel_id=1, source_target_pairs={{0,4},{1,9},{2,14},{3,19},{4,8},{5,13},{6,18},{7,23},{8,12},{9,17}... | collective-permute-start | bytes 296 | tf_op jit(solution)/shard_map/ppermute | solution.py:149
  72.6 7.2 %collective-permute-start.8 = (f32[24]{0:T(128)S(1)}, f32[24]{0:T(128)S(1)}, u32[]{:S(2)}, u32[]{:S(2)}) collective-permute-start(f32[24]{0:T(128)S(1)} %get-tuple-element.7), channel_id=1, source_target_pairs={{4,0},{9,1},{14,2},{19,3},{8,4},{13,5},{18,6},{23,7},{12,8},{17,9}... | collective-permute-start | bytes 296 | tf_op jit(solution)/shard_map/ppermute | solution.py:129
  80.6 3.6 %collective-permute-start.10 = (f32[24]{0:T(128)S(1)}, f32[24]{0:T(128)S(1)}, u32[]{:S(2)}, u32[]{:S(2)}) collective-permute-start(f32[24]{0:T(128)S(1)} %fusion.5), channel_id=1, source_target_pairs={{0,1},{1,0},{2,3},{3,2},{4,5},{5,4},{6,7},{7,6},{8,9},{9,8},{10,11... | collective-permute-start | bytes 296 | tf_op jit(solution)/shard_map/ppermute | solution.py:108
  84.2 5.1 %collective-permute-start.11 = (f32[24]{0:T(128)S(1)}, f32[24]{0:T(128)S(1)}, u32[]{:S(2)}, u32[]{:S(2)}) collective-permute-start(f32[24]{0:T(128)S(1)} %add.59), channel_id=1, source_target_pairs={{0,2},{1,3},{2,0},{3,1},{4,6},{5,7},{6,4},{7,5},{8,10},{9,11},{10,... | collective-permute-start | bytes 296 | tf_op jit(solution)/shard_map/ppermute | solution.py:108
  91.2 1.4 %collective-permute-start.12 = (f32[2]{0:T(128)S(1)}, f32[2]{0:T(128)S(1)}, u32[]{:S(2)}, u32[]{:S(2)}) collective-permute-start(f32[2]{0:T(128)S(1)} %pad_maximum_fusion.3), channel_id=1, source_target_pairs={{0,4},{1,5},{2,6},{3,7},{4,0},{5,1},{6,2},{7,3},{8,12},{9,13},{10,... | collective-permute-start | bytes 32 | tf_op jit(solution)/shard_map/ppermute | solution.py:108
  93.9 3.6 %collective-permute-start.13 = (f32[2]{0:T(128)S(1)}, f32[2]{0:T(128)S(1)}, u32[]{:S(2)}, u32[]{:S(2)}) collective-permute-start(f32[2]{0:T(128)S(1)} %fusion.32), channel_id=1, source_target_pairs={{0,8},{1,9},{2,10},{3,11},{4,12},{5,13},{6,14},{7,15},{8,0},{9,1},... | collective-permute-start | bytes 32 | tf_op jit(solution)/shard_map/ppermute | solution.py:108
  98.9 5.1 %collective-permute-start.14 = (f32[2]{0:T(128)S(1)}, f32[2]{0:T(128)S(1)}, u32[]{:S(2)}, u32[]{:S(2)}) collective-permute-start(f32[2]{0:T(128)S(1)} %fusion.33), channel_id=1, source_target_pairs={{0,16},{1,17},{2,18},{3,19},{4,20},{5,21},{6,22},{7,23},{8,24},{9,... | collective-permute-start | bytes 32 | tf_op jit(solution)/shard_map/ppermute | solution.py:108
  104.0 3.6 %collective-permute-start.15 = (f32[2]{0:T(128)S(1)}, f32[2]{0:T(128)S(1)}, u32[]{:S(2)}, u32[]{:S(2)}) collective-permute-start(f32[2]{0:T(128)S(1)} %add.63), channel_id=1, source_target_pairs={{0,32},{1,33},{2,34},{3,35},{4,36},{5,37},{6,38},{7,39},{8,40},{9,... | collective-permute-start | bytes 32 | tf_op jit(solution)/shard_map/ppermute | solution.py:108
  107.5 4.5 %collective-permute-start.16 = (f32[2]{0:T(128)S(1)}, f32[2]{0:T(128)S(1)}, u32[]{:S(2)}, u32[]{:S(2)}) collective-permute-start(f32[2]{0:T(128)S(1)} %add.64), channel_id=1, source_target_pairs={{0,64},{1,65},{2,66},{3,67},{4,68},{5,69},{6,70},{7,71},{8,72},{9,... | collective-permute-start | bytes 32 | tf_op jit(solution)/shard_map/ppermute | solution.py:108
  112.0 7.5 %collective-permute-start.17 = (f32[2]{0:T(128)S(1)}, f32[2]{0:T(128)S(1)}, u32[]{:S(2)}, u32[]{:S(2)}) collective-permute-start(f32[2]{0:T(128)S(1)} %add.65), channel_id=1, source_target_pairs={{0,128},{1,129},{2,130},{3,131},{4,132},{5,133},{6,134},{7,135},{8... | collective-permute-start | bytes 32 | tf_op jit(solution)/shard_map/ppermute | solution.py:108

commit v7 on v6

--- a/solution.py
+++ b/solution.py
@@ -131,17 +131,20 @@
     first_half = fetch(images[:half])
     second_src, first_half = lax.optimization_barrier((images[half:], first_half))
     others = [first_half, fetch(second_src)]
-    other_partners = fetch(partners)
-    other_counts = fetch(counts)
-    other_start = fetch(start)
+    packed = jnp.concatenate(
+        [partners[0].astype(jnp.float32), counts.astype(jnp.float32), start[0]]
+    )
+    other_packed = fetch(packed)
+    other_partners = other_packed[:slots]
+    other_counts = other_packed[slots]
+    other_start = other_packed[slots + 1 :]
 
     tile = pair_tile(images, others, table)
 
     slot_ids = jnp.arange(slots)
     plus = jnp.any((partners[0] == step + halo - 1) & (slot_ids < counts[0]))
-    minus = jnp.any((other_partners[0] == halo - step) & (slot_ids < other_counts[0]))
+    minus = jnp.any((other_partners == (halo - step).astype(jnp.float32)) & (slot_ids < other_counts))
     col_bits = [1 << b for b in range(ncols.bit_length() - 1)]
-    row_bits = [ncols << b for b in range(nblk.bit_length() - 1)]
 
     def apply(x_own, x_other):
         forward = jnp.where(plus, jnp.dot(tile, x_other, precision=HIGH), 0.0)
@@ -149,10 +152,10 @@
         part = forward + lax.ppermute(backward, axes, back)
         return butterfly_sum(part, axes, size, col_bits)
 
-    y1 = apply(start[0], other_start[0])
+    y1 = apply(start[0], other_start)
     z = apply(y1, fetch(y1))
     squares = jnp.stack([jnp.sum(y1 * y1), jnp.sum(z * z)])
-    squares = butterfly_sum(squares, axes, size, row_bits)
+    squares = jnp.sum(lax.all_to_all(jnp.broadcast_to(squares, (nblk, 2)), "rows", 0, 0, tiled=True), axis=0)
     entries = float(width * nblk)
     s1 = jnp.sqrt(squares[0] / entries + norm_eps)
     first_vec = y1 / s1

time: 123 us -> 113 us (0.919)
  the two profiles are of different devices: /device:TPU:6 before, /device:TPU:1 now
where the time goes in v7:
time: 113 us; the launch traced here: 112 us
  starting transfers between devices  32.6 us (29%)
  Pallas kernels  24.2 us (21%)
  blocking collectives  22.1 us (20%)
  waiting for transfers between devices  13.5 us (12%)
  other arithmetic  6.61 us (6%)
  matrix products  5.92 us (5%)
  local copies, waits for them, and re-layouts  4.09 us (4%)
  between operations  2.83 us (3%)
    pallas_call x2, Pallas kernels, pair_stats(): pl.pallas_call(tile_kernel, out_shape=jax.ShapeDtypeStruct((count, part,...  24.2 us
    all_to_all x1, blocking collectives, body(): lax.all_to_all(jnp.broadcast_to(squares, (nblk, 2)), 'rows', 0, 0, tiled=...  22.1 us
    ppermute x4, starting transfers between devices, butterfly_sum(): value = value + lax.ppermute(value, axes, route)  17.8 us
    ppermute x4, starting transfers between devices, body(): fetch = lambda v: lax.ppermute(v, axes, route)  12.2 us
    ppermute x2, waiting for transfers between devices, apply(): part = forward + lax.ppermute(backward, axes, back)  5.97 us
    ppermute x4, waiting for transfers between devices, butterfly_sum(): value = value + lax.ppermute(value, axes, route)  5.3 us
    dot_general x1, matrix products, pair_tile(): rel = jnp.einsum('lp,abql->abpq', table, sums, precision=HIGH)  2.68 us
    ppermute x2, starting transfers between devices, apply(): part = forward + lax.ppermute(backward, axes, back)  2.6 us
  transfers between devices with their start and end apart: 10, of which 7 were waited for; matrix products, arithmetic and copies ran while one was open for 3% of the time, Pallas kernels for 11%

profile of v7, /device:TPU:1, one launch (start us, length us, event | category | flops | bytes accessed | tf_op | source)
XLA Modules:
  0.0 111.9 jit_solution(10808769947553454041)
XLA Ops:
  0.6 1.2 %fusion.28 = (bf16[4,360,128]{2,1,0:T(8,128)(2,1)S(1)}, bf16[4,360,128]{2,1,0:T(8,128)(2,1)S(1)}) fusion(bf16[8,360,128]{2,1,0:T(8,128)(2,1)} %param.4), kind=kLoop, calls=%fused_computation.52 | loop fusion | bytes 1474560 | tf_op jit(solution)/shard_map/slice | solution.py:131
  1.9 3.3 %collective-permute-start = (bf16[4,360,128]{2,1,0:T(8,128)(2,1)S(1)}, bf16[4,360,128]{2,1,0:T(8,128)(2,1)S(1)}, u32[]{:S(2)}, u32[]{:S(2)}) collective-permute-start(bf16[4,360,128]{2,1,0:T(8,128)(2,1)S(1)} %get-tuple-element.13), channel_id=1, source_target_pairs={{4,0},{9,1},{14,2},{19,3},{8,4},{13,5},{18,6},{23,7},{12,8},{17,9}... | collective-permute-start | bytes 1105928 | tf_op jit(solution)/shard_map/ppermute | solution.py:129
  5.8 0.0 copy-start.2
  5.8 0.6 copy-done.2
  6.5 0.7 copy-done.1
  7.1 0.1 pad_maximum_fusion.3
  7.2 6.1 %collective-permute-start.2 = (f32[33]{0:T(128)S(1)}, f32[33]{0:T(128)S(1)}, u32[]{:S(2)}, u32[]{:S(2)}) collective-permute-start(f32[33]{0:T(128)S(1)} %pad_maximum_fusion.3), channel_id=1, source_target_pairs={{4,0},{9,1},{14,2},{19,3},{8,4},{13,5},{18,6},{23,7},{12,8},{17,9}... | collective-permute-start | bytes 404 | tf_op jit(solution)/shard_map/ppermute | solution.py:129
  13.2 0.1 multiply_cosine_fusion
  13.3 0.0 collective-permute-done
  13.3 2.9 %collective-permute-start.1 = (bf16[4,360,128]{2,1,0:T(8,128)(2,1)S(1)}, bf16[4,360,128]{2,1,0:T(8,128)(2,1)S(1)}, u32[]{:S(2)}, u32[]{:S(2)}) collective-permute-start(bf16[4,360,128]{2,1,0:T(8,128)(2,1)S(1)} %get-tuple-element.5), channel_id=1, source_target_pairs={{4,0},{9,1},{14,2},{19,3},{8,4},{13,5},{18,6},{23,7},{12,8},{17,9}... | collective-permute-start | bytes 1105928 | tf_op jit(solution)/shard_map/ppermute | solution.py:129
  16.2 0.1 fusion.19
  16.3 0.1 pad.4.a_ref
  16.4 0.0 collective-permute-done.2
  16.4 0.6 slice.41
  17.0 1.4 %and_reduce_fusion = pred[]{:T(512)} fusion(f32[33]{0:T(128)S(1)} %collective-permute-done.2, f32[]{:T(128)} %bitcast.14, f32[]{:T(128)S(6)} %convert_element_type.43), kind=kLoop, calls=%fused_computation.33 | loop fusion | flops 39 | bytes 41 | tf_op jit(solution)/shard_map/reduce_or | solution.py:146
  18.3 0.2 broadcast_in_dim.25.w_ref
  18.5 12.1 %shard_map.59 = f32[8,4,8,384]{3,2,1,0:T(8,128)S(1)} custom-call(bf16[8,384,128]{2,1,0:T(8,128)(2,1)S(1)} %pad.4.a_ref, bf16[1440,128]{1,0:T(8,128)(2,1)S(1)} %bitcast.80, f32[3,360,128]{2,1,0:T(8,128)S(1)} %broadcast_in_dim.25.w_ref), custom_call_target="tpu_custom_call" | custom-call | flops 1185546240 | bytes 2097152 | tf_op jit(solution)/shard_map/pallas_call | solution.py:75
  30.7 12.1 %shard_map.60 = f32[8,4,8,384]{3,2,1,0:T(8,128)S(1)} custom-call(bf16[8,384,128]{2,1,0:T(8,128)(2,1)S(1)} %pad.4.a_ref, bf16[1440,128]{1,0:T(8,128)(2,1)S(1)} %bitcast.81, f32[3,360,128]{2,1,0:T(8,128)S(1)} %broadcast_in_dim.25.w_ref), custom_call_target="tpu_custom_call" | custom-call | flops 1185546240 | bytes 2097152 | tf_op jit(solution)/shard_map/pallas_call | solution.py:75
  42.8 0.3 fusion.26
  43.1 0.1 exponential_bitcast_fusion
  43.2 0.2 fusion.11
  43.3 0.1 fusion.8
  43.5 2.7 %fusion = f32[3,8,3,8]{3,0,2,1:T(4,128)S(1)} fusion(f32[8,8,3,360]{3,2,1,0:T(4,128)S(1)} %fusion.8, f32[8,8]{1,0:T(8,128)S(1)} %fusion.11, f32[360,1]{0,1:T(1,128)S(1)} %get-tuple-element.17, f32[360,1]{0,1:T(1,128)S(1)} %get-tuple-element.18, f32[360,1]{0,1:T(1,128)S(1)} %fusion.19), kind=kOutput, calls=%fused_computation.1 | convolution fusion | flops 2491056 | bytes 283360 | tf_op jit(solution)/shard_map/lp,abql->abpq/dot_general | solution.py:100
  46.2 0.1 reshape.54
  46.3 0.8 fusion.3
  47.1 0.6 fusion.17
  47.8 5.3 %collective-permute-done.3 = f32[24]{0:T(128)S(1)} collective-permute-done((f32[24]{0:T(128)S(1)}, f32[24]{0:T(128)S(1)}, u32[]{:S(2)}, u32[]{:S(2)}) %collective-permute-start.3) | collective-permute-done | bytes 128 | tf_op jit(solution)/shard_map/ppermute | solution.py:152
  53.0 0.8 fusion.2
  53.8 8.4 %collective-permute-start.4 = (f32[24]{0:T(128)S(1)}, f32[24]{0:T(128)S(1)}, u32[]{:S(2)}, u32[]{:S(2)}) collective-permute-start(f32[24]{0:T(128)S(1)} %fusion.2), channel_id=1, source_target_pairs={{0,1},{1,0},{2,3},{3,2},{4,5},{5,4},{6,7},{7,6},{8,9},{9,8},{10,11... | collective-permute-start | bytes 296 | tf_op jit(solution)/shard_map/ppermute | solution.py:108
  62.3 1.0 collective-permute-done.4
  63.2 5.6 %collective-permute-start.5 = (f32[24]{0:T(128)S(1)}, f32[24]{0:T(128)S(1)}, u32[]{:S(2)}, u32[]{:S(2)}) collective-permute-start(f32[24]{0:T(128)S(1)} %add.38), channel_id=1, source_target_pairs={{0,2},{1,3},{2,0},{3,1},{4,6},{5,7},{6,4},{7,5},{8,10},{9,11},{10,... | collective-permute-start | bytes 296 | tf_op jit(solution)/shard_map/ppermute | solution.py:108
  68.9 1.0 collective-permute-done.5
  69.8 0.6 multiply_reduce_fusion.1
  70.4 0.8 fusion.6
  71.2 2.6 %collective-permute-start.7 = (f32[24]{0:T(128)S(1)}, f32[24]{0:T(128)S(1)}, u32[]{:S(2)}, u32[]{:S(2)}) collective-permute-start(f32[24]{0:T(128)S(1)} %fusion.6), channel_id=1, source_target_pairs={{0,4},{1,9},{2,14},{3,19},{4,8},{5,13},{6,18},{7,23},{8,12},{9,17}... | collective-permute-start | bytes 296 | tf_op jit(solution)/shard_map/ppermute | solution.py:152
  73.8 0.7 collective-permute-done.7
  74.6 2.3 %collective-permute-done.6 = f32[24]{0:T(128)S(1)} collective-permute-done((f32[24]{0:T(128)S(1)}, f32[24]{0:T(128)S(1)}, u32[]{:S(2)}, u32[]{:S(2)}) %collective-permute-start.6) | collective-permute-done | bytes 128 | tf_op jit(solution)/shard_map/ppermute | solution.py:129
  76.8 0.8 fusion.5
  77.6 2.4 %collective-permute-done.8 = f32[24]{0:T(128)S(1)} collective-permute-done((f32[24]{0:T(128)S(1)}, f32[24]{0:T(128)S(1)}, u32[]{:S(2)}, u32[]{:S(2)}) %collective-permute-start.8) | collective-permute-done | bytes 128 | tf_op jit(solution)/shard_map/ppermute | solution.py:108
  80.0 3.7 %collective-permute-start.9 = (f32[24]{0:T(128)S(1)}, f32[24]{0:T(128)S(1)}, u32[]{:S(2)}, u32[]{:S(2)}) collective-permute-start(f32[24]{0:T(128)S(1)} %add.41), channel_id=1, source_target_pairs={{0,2},{1,3},{2,0},{3,1},{4,6},{5,7},{6,4},{7,5},{8,10},{9,11},{10,... | collective-permute-start | bytes 296 | tf_op jit(solution)/shard_map/ppermute | solution.py:108
  83.7 1.0 collective-permute-done.9
  84.7 0.6 multiply_reduce_fusion
  85.3 1.4 %pad_maximum_fusion.4 = f32[2]{0:T(128)S(1)} fusion(f32[1]{0:T(128)} %bitcast.23, f32[1]{0:T(128)} %bitcast.18), kind=kLoop, calls=%fused_computation.39 | loop fusion | flops 2 | bytes 16 | tf_op jit(solution)/shard_map/stack | solution.py:157
  86.7 22.1 %all_to_all.6 = f32[64,1,2]{2,1,0:T(1,128)S(1)} all-to-all(f32[64,1,2]{2,1,0:T(1,128)S(1)} %broadcast_in_dim.27), channel_id=1, replica_groups=mesh['rows'=64,'cols'=4] {'rows'}, dimensions={0} | all-to-all | bytes 1024 | tf_op jit(solution)/shard_map/all_to_all | solution.py:158
  108.8 0.1 reduce_sum.39
  108.9 0.6 fusion.29
  110.1 0.5 divide_bitcast_fusion.1
  111.4 0.5 divide_bitcast_fusion
  (13 shorter events, 0.1 us)
Async XLA Ops:
  0.6 15.6 %copy-start = (bf16[8,360,128]{2,1,0:T(8,128)(2,1)S(1)}, bf16[8,360,128]{2,1,0:T(8,128)(2,1)}, u32[]{:S(2)}) copy-start(bf16[8,360,128]{2,1,0:T(8,128)(2,1)} %param.4) | copy-start | bytes 2211844
  1.9 11.5 %collective-permute-start = (bf16[4,360,128]{2,1,0:T(8,128)(2,1)S(1)}, bf16[4,360,128]{2,1,0:T(8,128)(2,1)S(1)}, u32[]{:S(2)}, u32[]{:S(2)}) collective-permute-start(bf16[4,360,128]{2,1,0:T(8,128)(2,1)S(1)} %get-tuple-element.13), channel_id=1, source_target_pairs={{4,0},{9,1},{14,2},{19,3},{8,4},{13,5},{18,6},{23,7},{12,8},{17,9}... | collective-permute-start | bytes 1105928 | tf_op jit(solution)/shard_map/ppermute | solution.py:129
  5.8 0.7 copy-start.2
  6.5 0.7 copy-start.1
  7.2 9.2 %collective-permute-start.2 = (f32[33]{0:T(128)S(1)}, f32[33]{0:T(128)S(1)}, u32[]{:S(2)}, u32[]{:S(2)}) collective-permute-start(f32[33]{0:T(128)S(1)} %pad_maximum_fusion.3), channel_id=1, source_target_pairs={{4,0},{9,1},{14,2},{19,3},{8,4},{13,5},{18,6},{23,7},{12,8},{17,9}... | collective-permute-start | bytes 404 | tf_op jit(solution)/shard_map/ppermute | solution.py:129
  13.3 17.3 %collective-permute-start.1 = (bf16[4,360,128]{2,1,0:T(8,128)(2,1)S(1)}, bf16[4,360,128]{2,1,0:T(8,128)(2,1)S(1)}, u32[]{:S(2)}, u32[]{:S(2)}) collective-permute-start(bf16[4,360,128]{2,1,0:T(8,128)(2,1)S(1)} %get-tuple-element.5), channel_id=1, source_target_pairs={{4,0},{9,1},{14,2},{19,3},{8,4},{13,5},{18,6},{23,7},{12,8},{17,9}... | collective-permute-start | bytes 1105928 | tf_op jit(solution)/shard_map/ppermute | solution.py:129
  47.1 5.9 %collective-permute-start.3 = (f32[24]{0:T(128)S(1)}, f32[24]{0:T(128)S(1)}, u32[]{:S(2)}, u32[]{:S(2)}) collective-permute-start(f32[24]{0:T(128)S(1)} %fusion.3), channel_id=1, source_target_pairs={{0,4},{1,9},{2,14},{3,19},{4,8},{5,13},{6,18},{7,23},{8,12},{9,17}... | collective-permute-start | bytes 296 | tf_op jit(solution)/shard_map/ppermute | solution.py:152
  53.8 9.4 %collective-permute-start.4 = (f32[24]{0:T(128)S(1)}, f32[24]{0:T(128)S(1)}, u32[]{:S(2)}, u32[]{:S(2)}) collective-permute-start(f32[24]{0:T(128)S(1)} %fusion.2), channel_id=1, source_target_pairs={{0,1},{1,0},{2,3},{3,2},{4,5},{5,4},{6,7},{7,6},{8,9},{9,8},{10,11... | collective-permute-start | bytes 296 | tf_op jit(solution)/shard_map/ppermute | solution.py:108
  63.2 6.6 %collective-permute-start.5 = (f32[24]{0:T(128)S(1)}, f32[24]{0:T(128)S(1)}, u32[]{:S(2)}, u32[]{:S(2)}) collective-permute-start(f32[24]{0:T(128)S(1)} %add.38), channel_id=1, source_target_pairs={{0,2},{1,3},{2,0},{3,1},{4,6},{5,7},{6,4},{7,5},{8,10},{9,11},{10,... | collective-permute-start | bytes 296 | tf_op jit(solution)/shard_map/ppermute | solution.py:108
  71.2 3.3 %collective-permute-start.7 = (f32[24]{0:T(128)S(1)}, f32[24]{0:T(128)S(1)}, u32[]{:S(2)}, u32[]{:S(2)}) collective-permute-start(f32[24]{0:T(128)S(1)} %fusion.6), channel_id=1, source_target_pairs={{0,4},{1,9},{2,14},{3,19},{4,8},{5,13},{6,18},{7,23},{8,12},{9,17}... | collective-permute-start | bytes 296 | tf_op jit(solution)/shard_map/ppermute | solution.py:152
  73.8 3.0 %collective-permute-start.6 = (f32[24]{0:T(128)S(1)}, f32[24]{0:T(128)S(1)}, u32[]{:S(2)}, u32[]{:S(2)}) collective-permute-start(f32[24]{0:T(128)S(1)} %get-tuple-element.7), channel_id=1, source_target_pairs={{4,0},{9,1},{14,2},{19,3},{8,4},{13,5},{18,6},{23,7},{12,8},{17,9}... | collective-permute-start | bytes 296 | tf_op jit(solution)/shard_map/ppermute | solution.py:129
  77.6 2.4 %collective-permute-start.8 = (f32[24]{0:T(128)S(1)}, f32[24]{0:T(128)S(1)}, u32[]{:S(2)}, u32[]{:S(2)}) collective-permute-start(f32[24]{0:T(128)S(1)} %fusion.5), channel_id=1, source_target_pairs={{0,1},{1,0},{2,3},{3,2},{4,5},{5,4},{6,7},{7,6},{8,9},{9,8},{10,11... | collective-permute-start | bytes 296 | tf_op jit(solution)/shard_map/ppermute | solution.py:108
  80.0 4.7 %collective-permute-start.9 = (f32[24]{0:T(128)S(1)}, f32[24]{0:T(128)S(1)}, u32[]{:S(2)}, u32[]{:S(2)}) collective-permute-start(f32[24]{0:T(128)S(1)} %add.41), channel_id=1, source_target_pairs={{0,2},{1,3},{2,0},{3,1},{4,6},{5,7},{6,4},{7,5},{8,10},{9,11},{10,... | collective-permute-start | bytes 296 | tf_op jit(solution)/shard_map/ppermute | solution.py:108

commit v8 on v7

--- a/solution.py
+++ b/solution.py
@@ -126,11 +126,15 @@
         for c in range(ncols):
             route.append((((i + c + 1) % nblk) * ncols + c, i * ncols + c))
     back = [(dst, src) for src, dst in route]
+    mirror = []
+    for i in range(nblk):
+        for c in range(ncols):
+            mirror.append((((i + c + 1) % nblk) * ncols + (ncols - 1 - c), i * ncols + c))
     fetch = lambda v: lax.ppermute(v, axes, route)
     half = count // 2
     first_half = fetch(images[:half])
     second_src, first_half = lax.optimization_barrier((images[half:], first_half))
-    others = [first_half, fetch(second_src)]
+    others = [first_half, lax.ppermute(second_src, axes, mirror)]
     packed = jnp.concatenate(
         [partners[0].astype(jnp.float32), counts.astype(jnp.float32), start[0]]
     )

time: 113 us -> 113 us (level)
  waiting for transfers between devices: 13.5 us -> 8.91 us
  starting transfers between devices: 32.6 us -> 36.9 us
    ppermute x0 -> x1, starting transfers between devices: none -> 12.9 us  [body(): others = [first_half, lax.ppermute(second_src, axes, mirror)]]
    ppermute x4, starting transfers between devices: 17.8 us -> 7.94 us  [butterfly_sum(): value = value + lax.ppermute(value, axes, route)]
    ppermute x2, waiting for transfers between devices: 5.97 us -> 0.68 us  [apply(): part = forward + lax.ppermute(backward, axes, back)]
    ppermute x4, waiting for transfers between devices: 5.3 us -> 7.99 us  [butterfly_sum(): value = value + lax.ppermute(value, axes, route)]
    ppermute x4 -> x3, waiting for transfers between devices: 2.28 us -> 0.23 us  [body(): fetch = lambda v: lax.ppermute(v, axes, route)]
    ppermute x4 -> x3, starting transfers between devices: 12.2 us -> 12.5 us  [body(): fetch = lambda v: lax.ppermute(v, axes, route)]
where the time goes in v8:
time: 113 us
  starting transfers between devices  36.9 us (33%)
  Pallas kernels  24.3 us (22%)
  blocking collectives  23.1 us (20%)
  waiting for transfers between devices  8.91 us (8%)
  other arithmetic  6.6 us (6%)
  matrix products  5.92 us (5%)
  local copies, waits for them, and re-layouts  4.09 us (4%)
  between operations  2.83 us (3%)
    pallas_call x2, Pallas kernels, pair_stats(): pl.pallas_call(tile_kernel, out_shape=jax.ShapeDtypeStruct((count, part,...  24.3 us
    all_to_all x1, blocking collectives, body(): lax.all_to_all(jnp.broadcast_to(squares, (nblk, 2)), 'rows', 0, 0, tiled=...  23.1 us
    ppermute x1, starting transfers between devices, body(): others = [first_half, lax.ppermute(second_src, axes, mirror)]  12.9 us
    ppermute x3, starting transfers between devices, body(): fetch = lambda v: lax.ppermute(v, axes, route)  12.5 us
    ppermute x4, waiting for transfers between devices, butterfly_sum(): value = value + lax.ppermute(value, axes, route)  7.99 us
    ppermute x4, starting transfers between devices, butterfly_sum(): value = value + lax.ppermute(value, axes, route)  7.94 us
    ppermute x2, starting transfers between devices, apply(): part = forward + lax.ppermute(backward, axes, back)  3.59 us
    dot_general x1, matrix products, pair_tile(): rel = jnp.einsum('lp,abql->abpq', table, sums, precision=HIGH)  2.68 us
  transfers between devices with their start and end apart: 10, of which 7 were waited for; matrix products, arithmetic and copies ran while one was open for 3% of the time, Pallas kernels for 11%

profile of v8, /device:TPU:1, one launch (start us, length us, event | category | flops | bytes accessed | tf_op | source)
XLA Modules:
  0.0 112.6 jit_solution(7036288501283692429)
XLA Ops:
  0.6 1.2 %fusion.28 = (bf16[4,360,128]{2,1,0:T(8,128)(2,1)S(1)}, bf16[4,360,128]{2,1,0:T(8,128)(2,1)S(1)}) fusion(bf16[8,360,128]{2,1,0:T(8,128)(2,1)} %param.4), kind=kLoop, calls=%fused_computation.52 | loop fusion | bytes 1474560 | tf_op jit(solution)/shard_map/slice | solution.py:135
  1.9 3.3 %collective-permute-start = (bf16[4,360,128]{2,1,0:T(8,128)(2,1)S(1)}, bf16[4,360,128]{2,1,0:T(8,128)(2,1)S(1)}, u32[]{:S(2)}, u32[]{:S(2)}) collective-permute-start(bf16[4,360,128]{2,1,0:T(8,128)(2,1)S(1)} %get-tuple-element.13), channel_id=1, source_target_pairs={{4,0},{9,1},{14,2},{19,3},{8,4},{13,5},{18,6},{23,7},{12,8},{17,9}... | collective-permute-start | bytes 1105928 | tf_op jit(solution)/shard_map/ppermute | solution.py:133
  5.8 0.6 copy-done.2
  6.5 0.7 copy-done.1
  7.1 0.1 pad_maximum_fusion.3
  7.2 6.1 %collective-permute-start.2 = (f32[33]{0:T(128)S(1)}, f32[33]{0:T(128)S(1)}, u32[]{:S(2)}, u32[]{:S(2)}) collective-permute-start(f32[33]{0:T(128)S(1)} %pad_maximum_fusion.3), channel_id=1, source_target_pairs={{4,0},{9,1},{14,2},{19,3},{8,4},{13,5},{18,6},{23,7},{12,8},{17,9}... | collective-permute-start | bytes 404 | tf_op jit(solution)/shard_map/ppermute | solution.py:133
  13.2 0.1 multiply_cosine_fusion
  13.3 12.9 %collective-permute-start.1 = (bf16[4,360,128]{2,1,0:T(8,128)(2,1)S(1)}, bf16[4,360,128]{2,1,0:T(8,128)(2,1)S(1)}, u32[]{:S(2)}, u32[]{:S(2)}) collective-permute-start(bf16[4,360,128]{2,1,0:T(8,128)(2,1)S(1)} %get-tuple-element.5), channel_id=1, source_target_pairs={{7,0},{10,1},{13,2},{16,3},{11,4},{14,5},{17,6},{20,7},{15,8},{18,... | collective-permute-start | bytes 1105928 | tf_op jit(solution)/shard_map/ppermute | solution.py:137
  26.2 0.1 fusion.19
  26.3 0.1 pad.4.a_ref
  26.4 0.6 slice.41
  27.0 1.4 %and_reduce_fusion = pred[]{:T(512)} fusion(f32[33]{0:T(128)S(1)} %collective-permute-done.2, f32[]{:T(128)} %bitcast.14, f32[]{:T(128)S(6)} %convert_element_type.43), kind=kLoop, calls=%fused_computation.33 | loop fusion | flops 39 | bytes 41 | tf_op jit(solution)/shard_map/reduce_or | solution.py:150
  28.4 0.2 broadcast_in_dim.25.w_ref
  28.6 12.1 %shard_map.59 = f32[8,4,8,384]{3,2,1,0:T(8,128)S(1)} custom-call(bf16[8,384,128]{2,1,0:T(8,128)(2,1)S(1)} %pad.4.a_ref, bf16[1440,128]{1,0:T(8,128)(2,1)S(1)} %bitcast.80, f32[3,360,128]{2,1,0:T(8,128)S(1)} %broadcast_in_dim.25.w_ref), custom_call_target="tpu_custom_call" | custom-call | flops 1185546240 | bytes 2097152 | tf_op jit(solution)/shard_map/pallas_call | solution.py:75
  40.7 12.1 %shard_map.60 = f32[8,4,8,384]{3,2,1,0:T(8,128)S(1)} custom-call(bf16[8,384,128]{2,1,0:T(8,128)(2,1)S(1)} %pad.4.a_ref, bf16[1440,128]{1,0:T(8,128)(2,1)S(1)} %bitcast.81, f32[3,360,128]{2,1,0:T(8,128)S(1)} %broadcast_in_dim.25.w_ref), custom_call_target="tpu_custom_call" | custom-call | flops 1185546240 | bytes 2097152 | tf_op jit(solution)/shard_map/pallas_call | solution.py:75
  52.9 0.3 fusion.26
  53.1 0.1 exponential_bitcast_fusion
  53.2 0.2 fusion.11
  53.4 0.1 fusion.8
  53.5 2.7 %fusion = f32[3,8,3,8]{3,0,2,1:T(4,128)S(1)} fusion(f32[8,8,3,360]{3,2,1,0:T(4,128)S(1)} %fusion.8, f32[8,8]{1,0:T(8,128)S(1)} %fusion.11, f32[360,1]{0,1:T(1,128)S(1)} %get-tuple-element.17, f32[360,1]{0,1:T(1,128)S(1)} %get-tuple-element.18, f32[360,1]{0,1:T(1,128)S(1)} %fusion.19), kind=kOutput, calls=%fused_computation.1 | convolution fusion | flops 2491056 | bytes 283360 | tf_op jit(solution)/shard_map/lp,abql->abpq/dot_general | solution.py:100
  56.2 0.1 reshape.54
  56.3 0.8 fusion.3
  57.2 2.0 %collective-permute-start.3 = (f32[24]{0:T(128)S(1)}, f32[24]{0:T(128)S(1)}, u32[]{:S(2)}, u32[]{:S(2)}) collective-permute-start(f32[24]{0:T(128)S(1)} %fusion.3), channel_id=1, source_target_pairs={{0,4},{1,9},{2,14},{3,19},{4,8},{5,13},{6,18},{7,23},{8,12},{9,17}... | collective-permute-start | bytes 296 | tf_op jit(solution)/shard_map/ppermute | solution.py:156
  59.2 0.6 fusion.17
  59.8 0.1 collective-permute-done.3
  59.9 0.8 fusion.2
  60.7 4.5 %collective-permute-start.4 = (f32[24]{0:T(128)S(1)}, f32[24]{0:T(128)S(1)}, u32[]{:S(2)}, u32[]{:S(2)}) collective-permute-start(f32[24]{0:T(128)S(1)} %fusion.2), channel_id=1, source_target_pairs={{0,1},{1,0},{2,3},{3,2},{4,5},{5,4},{6,7},{7,6},{8,9},{9,8},{10,11... | collective-permute-start | bytes 296 | tf_op jit(solution)/shard_map/ppermute | solution.py:108
  65.2 1.0 collective-permute-done.4
  66.2 0.6 collective-permute-start.5
  66.8 3.3 %collective-permute-done.5 = f32[24]{0:T(128)S(1)} collective-permute-done((f32[24]{0:T(128)S(1)}, f32[24]{0:T(128)S(1)}, u32[]{:S(2)}, u32[]{:S(2)}) %collective-permute-start.5) | collective-permute-done | bytes 128 | tf_op jit(solution)/shard_map/ppermute | solution.py:108
  70.1 0.6 multiply_reduce_fusion.1
  70.7 0.8 fusion.6
  71.5 1.6 %collective-permute-start.7 = (f32[24]{0:T(128)S(1)}, f32[24]{0:T(128)S(1)}, u32[]{:S(2)}, u32[]{:S(2)}) collective-permute-start(f32[24]{0:T(128)S(1)} %fusion.6), channel_id=1, source_target_pairs={{0,4},{1,9},{2,14},{3,19},{4,8},{5,13},{6,18},{7,23},{8,12},{9,17}... | collective-permute-start | bytes 296 | tf_op jit(solution)/shard_map/ppermute | solution.py:156
  73.1 3.2 %collective-permute-start.6 = (f32[24]{0:T(128)S(1)}, f32[24]{0:T(128)S(1)}, u32[]{:S(2)}, u32[]{:S(2)}) collective-permute-start(f32[24]{0:T(128)S(1)} %get-tuple-element.7), channel_id=1, source_target_pairs={{4,0},{9,1},{14,2},{19,3},{8,4},{13,5},{18,6},{23,7},{12,8},{17,9}... | collective-permute-start | bytes 296 | tf_op jit(solution)/shard_map/ppermute | solution.py:133
  76.3 0.6 collective-permute-done.7
  76.9 0.2 collective-permute-done.6
  77.1 0.8 fusion.5
  77.9 1.7 %collective-permute-start.8 = (f32[24]{0:T(128)S(1)}, f32[24]{0:T(128)S(1)}, u32[]{:S(2)}, u32[]{:S(2)}) collective-permute-start(f32[24]{0:T(128)S(1)} %fusion.5), channel_id=1, source_target_pairs={{0,1},{1,0},{2,3},{3,2},{4,5},{5,4},{6,7},{7,6},{8,9},{9,8},{10,11... | collective-permute-start | bytes 296 | tf_op jit(solution)/shard_map/ppermute | solution.py:108
  79.6 1.0 collective-permute-done.8
  80.5 1.2 %collective-permute-start.9 = (f32[24]{0:T(128)S(1)}, f32[24]{0:T(128)S(1)}, u32[]{:S(2)}, u32[]{:S(2)}) collective-permute-start(f32[24]{0:T(128)S(1)} %add.41), channel_id=1, source_target_pairs={{0,2},{1,3},{2,0},{3,1},{4,6},{5,7},{6,4},{7,5},{8,10},{9,11},{10,... | collective-permute-start | bytes 296 | tf_op jit(solution)/shard_map/ppermute | solution.py:108
  81.7 2.8 %collective-permute-done.9 = f32[24]{0:T(128)S(1)} collective-permute-done((f32[24]{0:T(128)S(1)}, f32[24]{0:T(128)S(1)}, u32[]{:S(2)}, u32[]{:S(2)}) %collective-permute-start.9) | collective-permute-done | bytes 128 | tf_op jit(solution)/shard_map/ppermute | solution.py:108
  84.4 0.6 multiply_reduce_fusion
  85.0 1.4 %pad_maximum_fusion.4 = f32[2]{0:T(128)S(1)} fusion(f32[1]{0:T(128)} %bitcast.23, f32[1]{0:T(128)} %bitcast.18), kind=kLoop, calls=%fused_computation.39 | loop fusion | flops 2 | bytes 16 | tf_op jit(solution)/shard_map/stack | solution.py:161
  86.4 23.1 %all_to_all.6 = f32[64,1,2]{2,1,0:T(1,128)S(1)} all-to-all(f32[64,1,2]{2,1,0:T(1,128)S(1)} %broadcast_in_dim.27), channel_id=1, replica_groups=mesh['rows'=64,'cols'=4] {'rows'}, dimensions={0} | all-to-all | bytes 1024 | tf_op jit(solution)/shard_map/all_to_all | solution.py:162
  109.5 0.1 reduce_sum.39
  109.6 0.6 fusion.29
  110.9 0.5 divide_bitcast_fusion.1
  112.1 0.5 divide_bitcast_fusion
  (13 shorter events, 0.1 us)
Async XLA Ops:
  0.6 25.7 %copy-start = (bf16[8,360,128]{2,1,0:T(8,128)(2,1)S(1)}, bf16[8,360,128]{2,1,0:T(8,128)(2,1)}, u32[]{:S(2)}) copy-start(bf16[8,360,128]{2,1,0:T(8,128)(2,1)} %param.4) | copy-start | bytes 2211844
  1.9 11.5 %collective-permute-start = (bf16[4,360,128]{2,1,0:T(8,128)(2,1)S(1)}, bf16[4,360,128]{2,1,0:T(8,128)(2,1)S(1)}, u32[]{:S(2)}, u32[]{:S(2)}) collective-permute-start(bf16[4,360,128]{2,1,0:T(8,128)(2,1)S(1)} %get-tuple-element.13), channel_id=1, source_target_pairs={{4,0},{9,1},{14,2},{19,3},{8,4},{13,5},{18,6},{23,7},{12,8},{17,9}... | collective-permute-start | bytes 1105928 | tf_op jit(solution)/shard_map/ppermute | solution.py:133
  5.8 0.7 copy-start.2
  6.5 0.7 copy-start.1
  7.2 19.2 %collective-permute-start.2 = (f32[33]{0:T(128)S(1)}, f32[33]{0:T(128)S(1)}, u32[]{:S(2)}, u32[]{:S(2)}) collective-permute-start(f32[33]{0:T(128)S(1)} %pad_maximum_fusion.3), channel_id=1, source_target_pairs={{4,0},{9,1},{14,2},{19,3},{8,4},{13,5},{18,6},{23,7},{12,8},{17,9}... | collective-permute-start | bytes 404 | tf_op jit(solution)/shard_map/ppermute | solution.py:133
  13.3 27.4 %collective-permute-start.1 = (bf16[4,360,128]{2,1,0:T(8,128)(2,1)S(1)}, bf16[4,360,128]{2,1,0:T(8,128)(2,1)S(1)}, u32[]{:S(2)}, u32[]{:S(2)}) collective-permute-start(bf16[4,360,128]{2,1,0:T(8,128)(2,1)S(1)} %get-tuple-element.5), channel_id=1, source_target_pairs={{7,0},{10,1},{13,2},{16,3},{11,4},{14,5},{17,6},{20,7},{15,8},{18,... | collective-permute-start | bytes 1105928 | tf_op jit(solution)/shard_map/ppermute | solution.py:137
  57.2 2.8 %collective-permute-start.3 = (f32[24]{0:T(128)S(1)}, f32[24]{0:T(128)S(1)}, u32[]{:S(2)}, u32[]{:S(2)}) collective-permute-start(f32[24]{0:T(128)S(1)} %fusion.3), channel_id=1, source_target_pairs={{0,4},{1,9},{2,14},{3,19},{4,8},{5,13},{6,18},{7,23},{8,12},{9,17}... | collective-permute-start | bytes 296 | tf_op jit(solution)/shard_map/ppermute | solution.py:156
  60.7 5.5 %collective-permute-start.4 = (f32[24]{0:T(128)S(1)}, f32[24]{0:T(128)S(1)}, u32[]{:S(2)}, u32[]{:S(2)}) collective-permute-start(f32[24]{0:T(128)S(1)} %fusion.2), channel_id=1, source_target_pairs={{0,1},{1,0},{2,3},{3,2},{4,5},{5,4},{6,7},{7,6},{8,9},{9,8},{10,11... | collective-permute-start | bytes 296 | tf_op jit(solution)/shard_map/ppermute | solution.py:108
  66.2 3.9 %collective-permute-start.5 = (f32[24]{0:T(128)S(1)}, f32[24]{0:T(128)S(1)}, u32[]{:S(2)}, u32[]{:S(2)}) collective-permute-start(f32[24]{0:T(128)S(1)} %add.38), channel_id=1, source_target_pairs={{0,2},{1,3},{2,0},{3,1},{4,6},{5,7},{6,4},{7,5},{8,10},{9,11},{10,... | collective-permute-start | bytes 296 | tf_op jit(solution)/shard_map/ppermute | solution.py:108
  71.5 5.3 %collective-permute-start.7 = (f32[24]{0:T(128)S(1)}, f32[24]{0:T(128)S(1)}, u32[]{:S(2)}, u32[]{:S(2)}) collective-permute-start(f32[24]{0:T(128)S(1)} %fusion.6), channel_id=1, source_target_pairs={{0,4},{1,9},{2,14},{3,19},{4,8},{5,13},{6,18},{7,23},{8,12},{9,17}... | collective-permute-start | bytes 296 | tf_op jit(solution)/shard_map/ppermute | solution.py:156
  73.1 4.0 %collective-permute-start.6 = (f32[24]{0:T(128)S(1)}, f32[24]{0:T(128)S(1)}, u32[]{:S(2)}, u32[]{:S(2)}) collective-permute-start(f32[24]{0:T(128)S(1)} %get-tuple-element.7), channel_id=1, source_target_pairs={{4,0},{9,1},{14,2},{19,3},{8,4},{13,5},{18,6},{23,7},{12,8},{17,9}... | collective-permute-start | bytes 296 | tf_op jit(solution)/shard_map/ppermute | solution.py:133
  77.9 2.6 %collective-permute-start.8 = (f32[24]{0:T(128)S(1)}, f32[24]{0:T(128)S(1)}, u32[]{:S(2)}, u32[]{:S(2)}) collective-permute-start(f32[24]{0:T(128)S(1)} %fusion.5), channel_id=1, source_target_pairs={{0,1},{1,0},{2,3},{3,2},{4,5},{5,4},{6,7},{7,6},{8,9},{9,8},{10,11... | collective-permute-start | bytes 296 | tf_op jit(solution)/shard_map/ppermute | solution.py:108
  80.5 3.9 %collective-permute-start.9 = (f32[24]{0:T(128)S(1)}, f32[24]{0:T(128)S(1)}, u32[]{:S(2)}, u32[]{:S(2)}) collective-permute-start(f32[24]{0:T(128)S(1)} %add.41), channel_id=1, source_target_pairs={{0,2},{1,3},{2,0},{3,1},{4,6},{5,7},{6,4},{7,5},{8,10},{9,11},{10,... | collective-permute-start | bytes 296 | tf_op jit(solution)/shard_map/ppermute | solution.py:108

commit v9 on v8

--- a/solution.py
+++ b/solution.py
@@ -132,9 +132,7 @@
             mirror.append((((i + c + 1) % nblk) * ncols + (ncols - 1 - c), i * ncols + c))
     fetch = lambda v: lax.ppermute(v, axes, route)
     half = count // 2
-    first_half = fetch(images[:half])
-    second_src, first_half = lax.optimization_barrier((images[half:], first_half))
-    others = [first_half, lax.ppermute(second_src, axes, mirror)]
+    others = [fetch(images[:half]), lax.ppermute(images[half:], axes, mirror)]
     packed = jnp.concatenate(
         [partners[0].astype(jnp.float32), counts.astype(jnp.float32), start[0]]
     )

time: 113 us -> 117 us (1.035)
  waiting for transfers between devices: 8.91 us -> 12.9 us
    ppermute x4, starting transfers between devices: 7.94 us -> 18 us  [butterfly_sum(): value = value + lax.ppermute(value, axes, route)]
    ppermute x3, starting transfers between devices: 12.5 us -> 3.19 us  [body(): fetch = lambda v: lax.ppermute(v, axes, route)]
    ppermute x2, waiting for transfers between devices: 0.68 us -> 4.98 us  [apply(): part = forward + lax.ppermute(backward, axes, back)]
    ppermute x4, waiting for transfers between devices: 7.99 us -> 3.95 us  [butterfly_sum(): value = value + lax.ppermute(value, axes, route)]
    ppermute x3, waiting for transfers between devices: 0.23 us -> 3.93 us  [body(): fetch = lambda v: lax.ppermute(v, axes, route)]
    ppermute x1, starting transfers between devices: 12.9 us -> 11.3 us  [body(): others = [fetch(images[:half]), lax.ppermute(images[half:], axes, mirror)]]
    ppermute x2, starting transfers between devices: 3.59 us -> 4.83 us  [apply(): part = forward + lax.ppermute(backward, axes, back)]
  transfers between devices with their start and end apart: 10 -> 10, of which waited for: 7 -> 8; matrix products, arithmetic and copies ran while one was open for 3% -> 3% of each run, Pallas kernels for 11% -> 10%
where the time goes in v9:
time: 117 us; the launch traced here: 116 us
  starting transfers between devices  37.3 us (32%)
  Pallas kernels  24.3 us (21%)
  blocking collectives  22.4 us (19%)
  waiting for transfers between devices  12.9 us (11%)
  other arithmetic  6.6 us (6%)
  matrix products  5.92 us (5%)
  local copies, waits for them, and re-layouts  4.09 us (3%)
  between operations  2.82 us (2%)
    pallas_call x2, Pallas kernels, pair_stats(): pl.pallas_call(tile_kernel, out_shape=jax.ShapeDtypeStruct((count, part,...  24.3 us
    all_to_all x1, blocking collectives, body(): lax.all_to_all(jnp.broadcast_to(squares, (nblk, 2)), 'rows', 0, 0, tiled=...  22.4 us
    ppermute x4, starting transfers between devices, butterfly_sum(): value = value + lax.ppermute(value, axes, route)  18 us
    ppermute x1, starting transfers between devices, body(): others = [fetch(images[:half]), lax.ppermute(images[half:], axes, mirror)]  11.3 us
    ppermute x2, waiting for transfers between devices, apply(): part = forward + lax.ppermute(backward, axes, back)  4.98 us
    ppermute x2, starting transfers between devices, apply(): part = forward + lax.ppermute(backward, axes, back)  4.83 us
    ppermute x4, waiting for transfers between devices, butterfly_sum(): value = value + lax.ppermute(value, axes, route)  3.95 us
    ppermute x3, waiting for transfers between devices, body(): fetch = lambda v: lax.ppermute(v, axes, route)  3.93 us
  transfers between devices with their start and end apart: 10, of which 8 were waited for; matrix products, arithmetic and copies ran while one was open for 3% of the time, Pallas kernels for 10%

profile of v9, /device:TPU:1, one launch (start us, length us, event | category | flops | bytes accessed | tf_op | source)
XLA Modules:
  0.0 116.3 jit_solution(9477630722123282918)
XLA Ops:
  0.6 1.2 %fusion.28 = (bf16[4,360,128]{2,1,0:T(8,128)(2,1)S(1)}, bf16[4,360,128]{2,1,0:T(8,128)(2,1)S(1)}) fusion(bf16[8,360,128]{2,1,0:T(8,128)(2,1)} %param.4), kind=kLoop, calls=%fused_computation.52 | loop fusion | bytes 1474560 | tf_op jit(solution)/shard_map/slice | solution.py:135
  1.9 11.3 %collective-permute-start.1 = (bf16[4,360,128]{2,1,0:T(8,128)(2,1)S(1)}, bf16[4,360,128]{2,1,0:T(8,128)(2,1)S(1)}, u32[]{:S(2)}, u32[]{:S(2)}) collective-permute-start(bf16[4,360,128]{2,1,0:T(8,128)(2,1)S(1)} %get-tuple-element.9), channel_id=1, source_target_pairs={{7,0},{10,1},{13,2},{16,3},{11,4},{14,5},{17,6},{20,7},{15,8},{18,... | collective-permute-start | bytes 1105928 | tf_op jit(solution)/shard_map/ppermute | solution.py:135
  13.2 1.0 collective-permute-start
  14.8 0.6 copy-done.2
  15.4 0.7 copy-done.1
  16.1 0.1 pad_maximum_fusion.3
  16.2 0.2 collective-permute-start.2
  16.4 0.1 multiply_cosine_fusion
  16.5 0.1 fusion.19
  16.7 3.5 %collective-permute-done.2 = f32[33]{0:T(128)S(1)} collective-permute-done((f32[33]{0:T(128)S(1)}, f32[33]{0:T(128)S(1)}, u32[]{:S(2)}, u32[]{:S(2)}) %collective-permute-start.2) | collective-permute-done | bytes 164 | tf_op jit(solution)/shard_map/ppermute | solution.py:133
  20.2 0.6 slice.41
  20.8 1.4 %and_reduce_fusion = pred[]{:T(512)} fusion(f32[33]{0:T(128)S(1)} %collective-permute-done.2, f32[]{:T(128)} %bitcast.14, f32[]{:T(128)S(6)} %convert_element_type.43), kind=kLoop, calls=%fused_computation.33 | loop fusion | flops 39 | bytes 41 | tf_op jit(solution)/shard_map/reduce_or | solution.py:148
  22.1 0.2 broadcast_in_dim.25.w_ref
  22.3 12.1 %shard_map.60 = f32[8,4,8,384]{3,2,1,0:T(8,128)S(1)} custom-call(bf16[8,384,128]{2,1,0:T(8,128)(2,1)S(1)} %pad.4.a_ref, bf16[1440,128]{1,0:T(8,128)(2,1)S(1)} %bitcast.81, f32[3,360,128]{2,1,0:T(8,128)S(1)} %broadcast_in_dim.25.w_ref), custom_call_target="tpu_custom_call" | custom-call | flops 1185546240 | bytes 2097152 | tf_op jit(solution)/shard_map/pallas_call | solution.py:75
  34.5 12.1 %shard_map.59 = f32[8,4,8,384]{3,2,1,0:T(8,128)S(1)} custom-call(bf16[8,384,128]{2,1,0:T(8,128)(2,1)S(1)} %pad.4.a_ref, bf16[1440,128]{1,0:T(8,128)(2,1)S(1)} %bitcast.80, f32[3,360,128]{2,1,0:T(8,128)S(1)} %broadcast_in_dim.25.w_ref), custom_call_target="tpu_custom_call" | custom-call | flops 1185546240 | bytes 2097152 | tf_op jit(solution)/shard_map/pallas_call | solution.py:75
  46.6 0.3 fusion.26
  46.9 0.1 exponential_bitcast_fusion
  47.0 0.2 fusion.11
  47.2 0.1 fusion.8
  47.3 2.7 %fusion = f32[3,8,3,8]{3,0,2,1:T(4,128)S(1)} fusion(f32[8,8,3,360]{3,2,1,0:T(4,128)S(1)} %fusion.8, f32[8,8]{1,0:T(8,128)S(1)} %fusion.11, f32[360,1]{0,1:T(1,128)S(1)} %get-tuple-element.13, f32[360,1]{0,1:T(1,128)S(1)} %get-tuple-element.14, f32[360,1]{0,1:T(1,128)S(1)} %fusion.19), kind=kOutput, calls=%fused_computation.1 | convolution fusion | flops 2491056 | bytes 283360 | tf_op jit(solution)/shard_map/lp,abql->abpq/dot_general | solution.py:100
  50.0 0.1 reshape.54
  50.1 0.8 fusion.3
  50.9 3.2 %collective-permute-start.3 = (f32[24]{0:T(128)S(1)}, f32[24]{0:T(128)S(1)}, u32[]{:S(2)}, u32[]{:S(2)}) collective-permute-start(f32[24]{0:T(128)S(1)} %fusion.3), channel_id=1, source_target_pairs={{0,4},{1,9},{2,14},{3,19},{4,8},{5,13},{6,18},{7,23},{8,12},{9,17}... | collective-permute-start | bytes 296 | tf_op jit(solution)/shard_map/ppermute | solution.py:154
  54.1 0.6 fusion.17
  54.8 4.4 %collective-permute-done.3 = f32[24]{0:T(128)S(1)} collective-permute-done((f32[24]{0:T(128)S(1)}, f32[24]{0:T(128)S(1)}, u32[]{:S(2)}, u32[]{:S(2)}) %collective-permute-start.3) | collective-permute-done | bytes 128 | tf_op jit(solution)/shard_map/ppermute | solution.py:154
  59.2 0.8 fusion.2
  60.0 8.6 %collective-permute-start.4 = (f32[24]{0:T(128)S(1)}, f32[24]{0:T(128)S(1)}, u32[]{:S(2)}, u32[]{:S(2)}) collective-permute-start(f32[24]{0:T(128)S(1)} %fusion.2), channel_id=1, source_target_pairs={{0,1},{1,0},{2,3},{3,2},{4,5},{5,4},{6,7},{7,6},{8,9},{9,8},{10,11... | collective-permute-start | bytes 296 | tf_op jit(solution)/shard_map/ppermute | solution.py:108
  68.6 1.0 collective-permute-done.4
  69.6 2.8 %collective-permute-start.5 = (f32[24]{0:T(128)S(1)}, f32[24]{0:T(128)S(1)}, u32[]{:S(2)}, u32[]{:S(2)}) collective-permute-start(f32[24]{0:T(128)S(1)} %add.38), channel_id=1, source_target_pairs={{0,2},{1,3},{2,0},{3,1},{4,6},{5,7},{6,4},{7,5},{8,10},{9,11},{10,... | collective-permute-start | bytes 296 | tf_op jit(solution)/shard_map/ppermute | solution.py:108
  72.4 1.1 collective-permute-done.5
  73.5 0.6 multiply_reduce_fusion.1
  74.1 0.8 fusion.6
  74.9 1.6 %collective-permute-start.7 = (f32[24]{0:T(128)S(1)}, f32[24]{0:T(128)S(1)}, u32[]{:S(2)}, u32[]{:S(2)}) collective-permute-start(f32[24]{0:T(128)S(1)} %fusion.6), channel_id=1, source_target_pairs={{0,4},{1,9},{2,14},{3,19},{4,8},{5,13},{6,18},{7,23},{8,12},{9,17}... | collective-permute-start | bytes 296 | tf_op jit(solution)/shard_map/ppermute | solution.py:154
  76.5 2.0 %collective-permute-start.6 = (f32[24]{0:T(128)S(1)}, f32[24]{0:T(128)S(1)}, u32[]{:S(2)}, u32[]{:S(2)}) collective-permute-start(f32[24]{0:T(128)S(1)} %get-tuple-element.3), channel_id=1, source_target_pairs={{4,0},{9,1},{14,2},{19,3},{8,4},{13,5},{18,6},{23,7},{12,8},{17,9}... | collective-permute-start | bytes 296 | tf_op jit(solution)/shard_map/ppermute | solution.py:133
  78.5 0.6 collective-permute-done.7
  79.1 0.4 collective-permute-done.6
  79.5 0.8 fusion.5
  80.3 2.6 %collective-permute-start.8 = (f32[24]{0:T(128)S(1)}, f32[24]{0:T(128)S(1)}, u32[]{:S(2)}, u32[]{:S(2)}) collective-permute-start(f32[24]{0:T(128)S(1)} %fusion.5), channel_id=1, source_target_pairs={{0,1},{1,0},{2,3},{3,2},{4,5},{5,4},{6,7},{7,6},{8,9},{9,8},{10,11... | collective-permute-start | bytes 296 | tf_op jit(solution)/shard_map/ppermute | solution.py:108
  82.9 1.0 collective-permute-done.8
  83.9 3.9 %collective-permute-start.9 = (f32[24]{0:T(128)S(1)}, f32[24]{0:T(128)S(1)}, u32[]{:S(2)}, u32[]{:S(2)}) collective-permute-start(f32[24]{0:T(128)S(1)} %add.41), channel_id=1, source_target_pairs={{0,2},{1,3},{2,0},{3,1},{4,6},{5,7},{6,4},{7,5},{8,10},{9,11},{10,... | collective-permute-start | bytes 296 | tf_op jit(solution)/shard_map/ppermute | solution.py:108
  87.8 1.0 collective-permute-done.9
  88.7 0.6 multiply_reduce_fusion
  89.3 1.4 %pad_maximum_fusion.4 = f32[2]{0:T(128)S(1)} fusion(f32[1]{0:T(128)} %bitcast.23, f32[1]{0:T(128)} %bitcast.18), kind=kLoop, calls=%fused_computation.39 | loop fusion | flops 2 | bytes 16 | tf_op jit(solution)/shard_map/stack | solution.py:159
  90.7 22.4 %all_to_all.6 = f32[64,1,2]{2,1,0:T(1,128)S(1)} all-to-all(f32[64,1,2]{2,1,0:T(1,128)S(1)} %broadcast_in_dim.27), channel_id=1, replica_groups=mesh['rows'=64,'cols'=4] {'rows'}, dimensions={0} | all-to-all | bytes 1024 | tf_op jit(solution)/shard_map/all_to_all | solution.py:160
  113.2 0.1 reduce_sum.39
  113.3 0.6 fusion.29
  114.5 0.5 divide_bitcast_fusion.1
  115.8 0.5 divide_bitcast_fusion
  (13 shorter events, 0.2 us)
Async XLA Ops:
  0.6 15.9 %copy-start = (bf16[8,360,128]{2,1,0:T(8,128)(2,1)S(1)}, bf16[8,360,128]{2,1,0:T(8,128)(2,1)}, u32[]{:S(2)}) copy-start(bf16[8,360,128]{2,1,0:T(8,128)(2,1)} %param.4) | copy-start | bytes 2211844
  1.9 20.3 %collective-permute-start.1 = (bf16[4,360,128]{2,1,0:T(8,128)(2,1)S(1)}, bf16[4,360,128]{2,1,0:T(8,128)(2,1)S(1)}, u32[]{:S(2)}, u32[]{:S(2)}) collective-permute-start(bf16[4,360,128]{2,1,0:T(8,128)(2,1)S(1)} %get-tuple-element.9), channel_id=1, source_target_pairs={{7,0},{10,1},{13,2},{16,3},{11,4},{14,5},{17,6},{20,7},{15,8},{18,... | collective-permute-start | bytes 1105928 | tf_op jit(solution)/shard_map/ppermute | solution.py:135
  13.2 21.3 %collective-permute-start = (bf16[4,360,128]{2,1,0:T(8,128)(2,1)S(1)}, bf16[4,360,128]{2,1,0:T(8,128)(2,1)S(1)}, u32[]{:S(2)}, u32[]{:S(2)}) collective-permute-start(bf16[4,360,128]{2,1,0:T(8,128)(2,1)S(1)} %get-tuple-element.10), channel_id=1, source_target_pairs={{4,0},{9,1},{14,2},{19,3},{8,4},{13,5},{18,6},{23,7},{12,8},{17,9}... | collective-permute-start | bytes 1105928 | tf_op jit(solution)/shard_map/ppermute | solution.py:133
  14.8 0.7 copy-start.2
  15.4 0.7 copy-start.1
  16.2 4.0 %collective-permute-start.2 = (f32[33]{0:T(128)S(1)}, f32[33]{0:T(128)S(1)}, u32[]{:S(2)}, u32[]{:S(2)}) collective-permute-start(f32[33]{0:T(128)S(1)} %pad_maximum_fusion.3), channel_id=1, source_target_pairs={{4,0},{9,1},{14,2},{19,3},{8,4},{13,5},{18,6},{23,7},{12,8},{17,9}... | collective-permute-start | bytes 404 | tf_op jit(solution)/shard_map/ppermute | solution.py:133
  50.9 8.2 %collective-permute-start.3 = (f32[24]{0:T(128)S(1)}, f32[24]{0:T(128)S(1)}, u32[]{:S(2)}, u32[]{:S(2)}) collective-permute-start(f32[24]{0:T(128)S(1)} %fusion.3), channel_id=1, source_target_pairs={{0,4},{1,9},{2,14},{3,19},{4,8},{5,13},{6,18},{7,23},{8,12},{9,17}... | collective-permute-start | bytes 296 | tf_op jit(solution)/shard_map/ppermute | solution.py:154
  60.0 9.6 %collective-permute-start.4 = (f32[24]{0:T(128)S(1)}, f32[24]{0:T(128)S(1)}, u32[]{:S(2)}, u32[]{:S(2)}) collective-permute-start(f32[24]{0:T(128)S(1)} %fusion.2), channel_id=1, source_target_pairs={{0,1},{1,0},{2,3},{3,2},{4,5},{5,4},{6,7},{7,6},{8,9},{9,8},{10,11... | collective-permute-start | bytes 296 | tf_op jit(solution)/shard_map/ppermute | solution.py:108
  69.6 3.9 %collective-permute-start.5 = (f32[24]{0:T(128)S(1)}, f32[24]{0:T(128)S(1)}, u32[]{:S(2)}, u32[]{:S(2)}) collective-permute-start(f32[24]{0:T(128)S(1)} %add.38), channel_id=1, source_target_pairs={{0,2},{1,3},{2,0},{3,1},{4,6},{5,7},{6,4},{7,5},{8,10},{9,11},{10,... | collective-permute-start | bytes 296 | tf_op jit(solution)/shard_map/ppermute | solution.py:108
  74.9 4.2 %collective-permute-start.7 = (f32[24]{0:T(128)S(1)}, f32[24]{0:T(128)S(1)}, u32[]{:S(2)}, u32[]{:S(2)}) collective-permute-start(f32[24]{0:T(128)S(1)} %fusion.6), channel_id=1, source_target_pairs={{0,4},{1,9},{2,14},{3,19},{4,8},{5,13},{6,18},{7,23},{8,12},{9,17}... | collective-permute-start | bytes 296 | tf_op jit(solution)/shard_map/ppermute | solution.py:154
  76.5 3.0 %collective-permute-start.6 = (f32[24]{0:T(128)S(1)}, f32[24]{0:T(128)S(1)}, u32[]{:S(2)}, u32[]{:S(2)}) collective-permute-start(f32[24]{0:T(128)S(1)} %get-tuple-element.3), channel_id=1, source_target_pairs={{4,0},{9,1},{14,2},{19,3},{8,4},{13,5},{18,6},{23,7},{12,8},{17,9}... | collective-permute-start | bytes 296 | tf_op jit(solution)/shard_map/ppermute | solution.py:133
  80.3 3.6 %collective-permute-start.8 = (f32[24]{0:T(128)S(1)}, f32[24]{0:T(128)S(1)}, u32[]{:S(2)}, u32[]{:S(2)}) collective-permute-start(f32[24]{0:T(128)S(1)} %fusion.5), channel_id=1, source_target_pairs={{0,1},{1,0},{2,3},{3,2},{4,5},{5,4},{6,7},{7,6},{8,9},{9,8},{10,11... | collective-permute-start | bytes 296 | tf_op jit(solution)/shard_map/ppermute | solution.py:108
  83.9 4.9 %collective-permute-start.9 = (f32[24]{0:T(128)S(1)}, f32[24]{0:T(128)S(1)}, u32[]{:S(2)}, u32[]{:S(2)}) collective-permute-start(f32[24]{0:T(128)S(1)} %add.41), channel_id=1, source_target_pairs={{0,2},{1,3},{2,0},{3,1},{4,6},{5,7},{6,4},{7,5},{8,10},{9,11},{10,... | collective-permute-start | bytes 296 | tf_op jit(solution)/shard_map/ppermute | solution.py:108

commit v10 on v7

--- a/solution.py
+++ b/solution.py
@@ -10,6 +10,7 @@
 score_gain = 0.4
 norm_eps = 1e-06
 HIGH = lax.Precision.HIGHEST
+LOG2E = 1.4426950408889634
 
 
 def line_table(lines):
@@ -30,7 +31,7 @@
             lax.dot_general(
                 b_ref[...], a_ref[a], (((1,), (1,)), ((), ())), preferred_element_type=jnp.float32
             )
-            * score_gain
+            * (score_gain * LOG2E)
         )
 
         def per_partner(b, carry2):
@@ -46,7 +47,7 @@
 
             def accumulate(r, acc):
                 start = pl.multiple_of(base + r * 8, 8)
-                e = jnp.exp(s_ref[pl.ds(start, 8), :] - top8)
+                e = jnp.exp2(s_ref[pl.ds(start, 8), :] - top8)
                 row = pl.multiple_of(r * 8, 8)
                 out = [acc[0] + e]
                 for q in range(3):
@@ -94,7 +95,7 @@
     stats = stats[:, :, :, :lines]
     top = stats[:, :, 0, :]
     peak = jnp.max(top, axis=2, keepdims=True)
-    scale = jnp.exp(top - peak)
+    scale = jnp.exp2(top - peak)
     total = jnp.sum(scale * stats[:, :, 1, :], axis=2)
     sums = stats[:, :, 2:5, :] * scale[:, :, None, :]
     rel = jnp.einsum("lp,abql->abpq", table, sums, precision=HIGH)
@@ -146,21 +147,28 @@
     minus = jnp.any((other_partners == (halo - step).astype(jnp.float32)) & (slot_ids < other_counts))
     col_bits = [1 << b for b in range(ncols.bit_length() - 1)]
 
-    def apply(x_own, x_other):
+    def partial(x_own, x_other):
         forward = jnp.where(plus, jnp.dot(tile, x_other, precision=HIGH), 0.0)
         backward = jnp.where(minus, jnp.dot(tile.T, x_own, precision=HIGH), 0.0)
-        part = forward + lax.ppermute(backward, axes, back)
-        return butterfly_sum(part, axes, size, col_bits)
+        return forward + lax.ppermute(backward, axes, back)
 
-    y1 = apply(start[0], other_start)
-    z = apply(y1, fetch(y1))
-    squares = jnp.stack([jnp.sum(y1 * y1), jnp.sum(z * z)])
-    squares = jnp.sum(lax.all_to_all(jnp.broadcast_to(squares, (nblk, 2)), "rows", 0, 0, tiled=True), axis=0)
+    y1 = butterfly_sum(partial(start[0], other_start), axes, size, col_bits)
+    z_part = partial(y1, fetch(y1))
+    own_square = jnp.where(lax.axis_index("cols") == 0, jnp.sum(y1 * y1), 0.0)
+    packet = jnp.concatenate([z_part, own_square[None]])
+    gathered = lax.all_to_all(jnp.broadcast_to(packet, (size, width + 1)), axes, 0, 0, tiled=True)
+    gathered = gathered.reshape(nblk, ncols, width + 1)
+    z_all = gathered[:, 0, :width]
+    for c in range(1, ncols):
+        z_all = z_all + gathered[:, c, :width]
+    sum_y1 = jnp.sum(gathered[:, :, width])
+    sum_z = jnp.sum(z_all * z_all)
+    z = lax.dynamic_index_in_dim(z_all, lax.axis_index("rows"), 0, keepdims=False)
     entries = float(width * nblk)
-    s1 = jnp.sqrt(squares[0] / entries + norm_eps)
+    s1 = jnp.sqrt(sum_y1 / entries + norm_eps)
     first_vec = y1 / s1
     second_raw = z / s1
-    s2 = jnp.sqrt(squares[1] / (s1 * s1) / entries + norm_eps)
+    s2 = jnp.sqrt(sum_z / (s1 * s1) / entries + norm_eps)
     return (first_vec[None, :], (second_raw / s2)[None, :])
 
 

time: 113 us -> 106 us (0.938); the launches traced: 112 us -> 106 us
  blocking collectives: 22.1 us -> 0 us
  starting transfers between devices: 32.6 us -> 42.3 us
  waiting for transfers between devices: 13.5 us -> 20.5 us
    all_to_all x1 -> x0, blocking collectives: 22.1 us -> none  [body(): lax.all_to_all(jnp.broadcast_to(squares, (nblk, 2)), 'rows', 0, 0, tiled=...]
    all_to_all x0 -> x1, starting transfers between devices: none -> 13.4 us  [body(): lax.all_to_all(jnp.broadcast_to(packet, (size, width + 1)), axes, 0, 0, t...]
    all_to_all x0 -> x1, waiting for transfers between devices: none -> 12.8 us  [body(): lax.all_to_all(jnp.broadcast_to(packet, (size, width + 1)), axes, 0, 0, t...]
    ppermute x4 -> x2, starting transfers between devices: 17.8 us -> 14.1 us  [butterfly_sum(): value = value + lax.ppermute(value, axes, route)]
    ppermute x4 -> x2, waiting for transfers between devices: 5.3 us -> 1.91 us  [butterfly_sum(): value = value + lax.ppermute(value, axes, route)]
    ppermute x4, starting transfers between devices: 12.2 us -> 14.6 us  [body(): fetch = lambda v: lax.ppermute(v, axes, route)]
    ppermute x2, starting transfers between devices: 2.6 us -> 0.23 us  [partial(): return forward + lax.ppermute(backward, axes, back)]
    ppermute x4, waiting for transfers between devices: 2.28 us -> 0.26 us  [body(): fetch = lambda v: lax.ppermute(v, axes, route)]
  transfers between devices with their start and end apart: 10 -> 9, of which waited for: 7 -> 6; matrix products, arithmetic and copies ran while one was open for 3% -> 3% of each run, Pallas kernels for 11% -> 11%
where the time goes in v10:
time: 106 us
  starting transfers between devices  42.3 us (40%)
  Pallas kernels  23.4 us (22%)
  waiting for transfers between devices  20.5 us (19%)
  other arithmetic  6.16 us (6%)
  matrix products  5.92 us (6%)
  local copies, waits for them, and re-layouts  4.2 us (4%)
  between operations  3.53 us (3%)
    pallas_call x2, Pallas kernels, pair_stats(): pl.pallas_call(tile_kernel, out_shape=jax.ShapeDtypeStruct((count, part,...  23.4 us
    ppermute x4, starting transfers between devices, body(): fetch = lambda v: lax.ppermute(v, axes, route)  14.6 us
    ppermute x2, starting transfers between devices, butterfly_sum(): value = value + lax.ppermute(value, axes, route)  14.1 us
    all_to_all x1, starting transfers between devices, body(): lax.all_to_all(jnp.broadcast_to(packet, (size, width + 1)), axes, 0, 0, t...  13.4 us
    all_to_all x1, waiting for transfers between devices, body(): lax.all_to_all(jnp.broadcast_to(packet, (size, width + 1)), axes, 0, 0, t...  12.8 us
    ppermute x2, waiting for transfers between devices, partial(): return forward + lax.ppermute(backward, axes, back)  5.52 us
    dot_general x1, matrix products, pair_tile(): rel = jnp.einsum('lp,abql->abpq', table, sums, precision=HIGH)  2.68 us
  transfers between devices with their start and end apart: 9, of which 6 were waited for; matrix products, arithmetic and copies ran while one was open for 3% of the time, Pallas kernels for 11%

profile of v10, /device:TPU:1, one launch (start us, length us, event | category | flops | bytes accessed | tf_op | source)
XLA Modules:
  0.0 106.0 jit_solution(9360558502857305513)
XLA Ops:
  0.6 1.2 %fusion.29 = (bf16[4,360,128]{2,1,0:T(8,128)(2,1)S(1)}, bf16[4,360,128]{2,1,0:T(8,128)(2,1)S(1)}) fusion(bf16[8,360,128]{2,1,0:T(8,128)(2,1)} %param.4), kind=kLoop, calls=%fused_computation.57 | loop fusion | bytes 1474560 | tf_op jit(solution)/shard_map/slice | solution.py:132
  1.9 3.3 %collective-permute-start = (bf16[4,360,128]{2,1,0:T(8,128)(2,1)S(1)}, bf16[4,360,128]{2,1,0:T(8,128)(2,1)S(1)}, u32[]{:S(2)}, u32[]{:S(2)}) collective-permute-start(bf16[4,360,128]{2,1,0:T(8,128)(2,1)S(1)} %get-tuple-element.13), channel_id=1, source_target_pairs={{4,0},{9,1},{14,2},{19,3},{8,4},{13,5},{18,6},{23,7},{12,8},{17,9}... | collective-permute-start | bytes 1105928 | tf_op jit(solution)/shard_map/ppermute | solution.py:130
  5.8 0.0 copy-start.2
  5.8 0.6 copy-done.2
  6.5 0.7 copy-done.1
  7.1 0.1 pad_maximum_fusion.3
  7.2 6.1 %collective-permute-start.2 = (f32[33]{0:T(128)S(1)}, f32[33]{0:T(128)S(1)}, u32[]{:S(2)}, u32[]{:S(2)}) collective-permute-start(f32[33]{0:T(128)S(1)} %pad_maximum_fusion.3), channel_id=1, source_target_pairs={{4,0},{9,1},{14,2},{19,3},{8,4},{13,5},{18,6},{23,7},{12,8},{17,9}... | collective-permute-start | bytes 404 | tf_op jit(solution)/shard_map/ppermute | solution.py:130
  13.2 0.1 multiply_cosine_fusion
  13.3 0.0 collective-permute-done
  13.3 2.9 %collective-permute-start.1 = (bf16[4,360,128]{2,1,0:T(8,128)(2,1)S(1)}, bf16[4,360,128]{2,1,0:T(8,128)(2,1)S(1)}, u32[]{:S(2)}, u32[]{:S(2)}) collective-permute-start(bf16[4,360,128]{2,1,0:T(8,128)(2,1)S(1)} %get-tuple-element.5), channel_id=1, source_target_pairs={{4,0},{9,1},{14,2},{19,3},{8,4},{13,5},{18,6},{23,7},{12,8},{17,9}... | collective-permute-start | bytes 1105928 | tf_op jit(solution)/shard_map/ppermute | solution.py:130
  16.2 0.1 fusion.20
  16.3 0.1 pad.4.a_ref
  16.4 0.0 collective-permute-done.2
  16.4 0.6 slice.50
  17.0 1.4 %and_reduce_fusion = pred[]{:T(512)} fusion(f32[33]{0:T(128)S(1)} %collective-permute-done.2, f32[]{:T(128)} %bitcast.14, f32[]{:T(128)S(6)} %convert_element_type.43), kind=kLoop, calls=%fused_computation.39 | loop fusion | flops 39 | bytes 41 | tf_op jit(solution)/shard_map/reduce_or | solution.py:147
  18.3 0.2 broadcast_in_dim.26.w_ref
  18.5 11.7 %shard_map.59 = f32[8,4,8,384]{3,2,1,0:T(8,128)S(1)} custom-call(bf16[8,384,128]{2,1,0:T(8,128)(2,1)S(1)} %pad.4.a_ref, bf16[1440,128]{1,0:T(8,128)(2,1)S(1)} %bitcast.80, f32[3,360,128]{2,1,0:T(8,128)S(1)} %broadcast_in_dim.26.w_ref), custom_call_target="tpu_custom_call" | custom-call | flops 1185546240 | bytes 2097152 | tf_op jit(solution)/shard_map/pallas_call | solution.py:76
  30.2 11.7 %shard_map.60 = f32[8,4,8,384]{3,2,1,0:T(8,128)S(1)} custom-call(bf16[8,384,128]{2,1,0:T(8,128)(2,1)S(1)} %pad.4.a_ref, bf16[1440,128]{1,0:T(8,128)(2,1)S(1)} %bitcast.81, f32[3,360,128]{2,1,0:T(8,128)S(1)} %broadcast_in_dim.26.w_ref), custom_call_target="tpu_custom_call" | custom-call | flops 1185546240 | bytes 2097152 | tf_op jit(solution)/shard_map/pallas_call | solution.py:76
  42.0 0.3 fusion.27
  42.2 0.1 exponential_bitcast_fusion
  42.3 0.2 fusion.11
  42.5 0.1 fusion.8
  42.6 2.7 %fusion = f32[3,8,3,8]{3,0,2,1:T(4,128)S(1)} fusion(f32[8,8,3,360]{3,2,1,0:T(4,128)S(1)} %fusion.8, f32[8,8]{1,0:T(8,128)S(1)} %fusion.11, f32[360,1]{0,1:T(1,128)S(1)} %get-tuple-element.15, f32[360,1]{0,1:T(1,128)S(1)} %get-tuple-element.16, f32[360,1]{0,1:T(1,128)S(1)} %fusion.20), kind=kOutput, calls=%fused_computation.1 | convolution fusion | flops 2491056 | bytes 283360 | tf_op jit(solution)/shard_map/lp,abql->abpq/dot_general | solution.py:101
  45.3 0.1 reshape.60
  45.4 0.8 fusion.3
  46.2 0.0 collective-permute-start.3
  46.3 0.6 fusion.18
  46.9 5.2 %collective-permute-done.3 = f32[24]{0:T(128)S(1)} collective-permute-done((f32[24]{0:T(128)S(1)}, f32[24]{0:T(128)S(1)}, u32[]{:S(2)}, u32[]{:S(2)}) %collective-permute-start.3) | collective-permute-done | bytes 128 | tf_op jit(solution)/shard_map/ppermute | solution.py:153
  52.1 0.8 fusion.2
  53.0 8.5 %collective-permute-start.4 = (f32[24]{0:T(128)S(1)}, f32[24]{0:T(128)S(1)}, u32[]{:S(2)}, u32[]{:S(2)}) collective-permute-start(f32[24]{0:T(128)S(1)} %fusion.2), channel_id=1, source_target_pairs={{0,1},{1,0},{2,3},{3,2},{4,5},{5,4},{6,7},{7,6},{8,9},{9,8},{10,11... | collective-permute-start | bytes 296 | tf_op jit(solution)/shard_map/ppermute | solution.py:109
  61.4 1.0 collective-permute-done.4
  62.4 5.7 %collective-permute-start.5 = (f32[24]{0:T(128)S(1)}, f32[24]{0:T(128)S(1)}, u32[]{:S(2)}, u32[]{:S(2)}) collective-permute-start(f32[24]{0:T(128)S(1)} %add.47), channel_id=1, source_target_pairs={{0,2},{1,3},{2,0},{3,1},{4,6},{5,7},{6,4},{7,5},{8,10},{9,11},{10,... | collective-permute-start | bytes 296 | tf_op jit(solution)/shard_map/ppermute | solution.py:109
  68.0 1.0 collective-permute-done.5
  69.0 0.6 multiply_reduce_fusion.1
  69.6 0.8 fusion.6
  70.4 2.4 %collective-permute-start.6 = (f32[24]{0:T(128)S(1)}, f32[24]{0:T(128)S(1)}, u32[]{:S(2)}, u32[]{:S(2)}) collective-permute-start(f32[24]{0:T(128)S(1)} %get-tuple-element.9), channel_id=1, source_target_pairs={{4,0},{9,1},{14,2},{19,3},{8,4},{13,5},{18,6},{23,7},{12,8},{17,9}... | collective-permute-start | bytes 296 | tf_op jit(solution)/shard_map/ppermute | solution.py:130
  72.8 0.2 collective-permute-start.7
  73.7 0.3 collective-permute-done.7
  74.0 0.3 collective-permute-done.6
  74.2 0.8 fusion.5
  75.0 0.1 pad_maximum_fusion.4
  75.1 0.7 broadcast_in_dim.29
  75.8 13.4 %all-to-all-start = ((f32[256,1,25]{2,1,0:T(1,128)}), f32[256,1,25]{2,1,0:T(1,128)S(1)}, u32[]{:S(2)}, u32[]{:S(2)}) async-start(f32[256,1,25]{2,1,0:T(1,128)} %broadcast_in_dim.29), calls=%async_computation | async-start | bytes 262144 | tf_op jit(solution)/shard_map/all_to_all | solution.py:159
  89.2 12.8 %all-to-all-done = f32[256,1,25]{2,1,0:T(1,128)S(1)} async-done(((f32[256,1,25]{2,1,0:T(1,128)}), f32[256,1,25]{2,1,0:T(1,128)S(1)}, u32[]{:S(2)}, u32[]{:S(2)}) %all-to-all-start) | async-done | bytes 25632 | tf_op jit(solution)/shard_map/all_to_all | solution.py:159
  102.0 0.8 multiply_reduce_fusion
  102.8 0.7 slice_reduce_fusion
  104.2 0.5 divide_bitcast_fusion.1
  105.5 0.5 divide_bitcast_fusion
  (8 shorter events, 0.1 us)
Async XLA Ops:
  0.6 15.6 %copy-start = (bf16[8,360,128]{2,1,0:T(8,128)(2,1)S(1)}, bf16[8,360,128]{2,1,0:T(8,128)(2,1)}, u32[]{:S(2)}) copy-start(bf16[8,360,128]{2,1,0:T(8,128)(2,1)} %param.4) | copy-start | bytes 2211844
  1.9 11.5 %collective-permute-start = (bf16[4,360,128]{2,1,0:T(8,128)(2,1)S(1)}, bf16[4,360,128]{2,1,0:T(8,128)(2,1)S(1)}, u32[]{:S(2)}, u32[]{:S(2)}) collective-permute-start(bf16[4,360,128]{2,1,0:T(8,128)(2,1)S(1)} %get-tuple-element.13), channel_id=1, source_target_pairs={{4,0},{9,1},{14,2},{19,3},{8,4},{13,5},{18,6},{23,7},{12,8},{17,9}... | collective-permute-start | bytes 1105928 | tf_op jit(solution)/shard_map/ppermute | solution.py:130
  5.8 0.7 copy-start.2
  6.5 0.7 copy-start.1
  7.2 9.2 %collective-permute-start.2 = (f32[33]{0:T(128)S(1)}, f32[33]{0:T(128)S(1)}, u32[]{:S(2)}, u32[]{:S(2)}) collective-permute-start(f32[33]{0:T(128)S(1)} %pad_maximum_fusion.3), channel_id=1, source_target_pairs={{4,0},{9,1},{14,2},{19,3},{8,4},{13,5},{18,6},{23,7},{12,8},{17,9}... | collective-permute-start | bytes 404 | tf_op jit(solution)/shard_map/ppermute | solution.py:130
  13.3 16.9 %collective-permute-start.1 = (bf16[4,360,128]{2,1,0:T(8,128)(2,1)S(1)}, bf16[4,360,128]{2,1,0:T(8,128)(2,1)S(1)}, u32[]{:S(2)}, u32[]{:S(2)}) collective-permute-start(bf16[4,360,128]{2,1,0:T(8,128)(2,1)S(1)} %get-tuple-element.5), channel_id=1, source_target_pairs={{4,0},{9,1},{14,2},{19,3},{8,4},{13,5},{18,6},{23,7},{12,8},{17,9}... | collective-permute-start | bytes 1105928 | tf_op jit(solution)/shard_map/ppermute | solution.py:130
  46.2 5.9 %collective-permute-start.3 = (f32[24]{0:T(128)S(1)}, f32[24]{0:T(128)S(1)}, u32[]{:S(2)}, u32[]{:S(2)}) collective-permute-start(f32[24]{0:T(128)S(1)} %fusion.3), channel_id=1, source_target_pairs={{0,4},{1,9},{2,14},{3,19},{4,8},{5,13},{6,18},{7,23},{8,12},{9,17}... | collective-permute-start | bytes 296 | tf_op jit(solution)/shard_map/ppermute | solution.py:153
  53.0 9.4 %collective-permute-start.4 = (f32[24]{0:T(128)S(1)}, f32[24]{0:T(128)S(1)}, u32[]{:S(2)}, u32[]{:S(2)}) collective-permute-start(f32[24]{0:T(128)S(1)} %fusion.2), channel_id=1, source_target_pairs={{0,1},{1,0},{2,3},{3,2},{4,5},{5,4},{6,7},{7,6},{8,9},{9,8},{10,11... | collective-permute-start | bytes 296 | tf_op jit(solution)/shard_map/ppermute | solution.py:109
  62.4 6.6 %collective-permute-start.5 = (f32[24]{0:T(128)S(1)}, f32[24]{0:T(128)S(1)}, u32[]{:S(2)}, u32[]{:S(2)}) collective-permute-start(f32[24]{0:T(128)S(1)} %add.47), channel_id=1, source_target_pairs={{0,2},{1,3},{2,0},{3,1},{4,6},{5,7},{6,4},{7,5},{8,10},{9,11},{10,... | collective-permute-start | bytes 296 | tf_op jit(solution)/shard_map/ppermute | solution.py:109
  70.4 3.8 %collective-permute-start.6 = (f32[24]{0:T(128)S(1)}, f32[24]{0:T(128)S(1)}, u32[]{:S(2)}, u32[]{:S(2)}) collective-permute-start(f32[24]{0:T(128)S(1)} %get-tuple-element.9), channel_id=1, source_target_pairs={{4,0},{9,1},{14,2},{19,3},{8,4},{13,5},{18,6},{23,7},{12,8},{17,9}... | collective-permute-start | bytes 296 | tf_op jit(solution)/shard_map/ppermute | solution.py:130
  72.8 1.2 %collective-permute-start.7 = (f32[24]{0:T(128)S(1)}, f32[24]{0:T(128)S(1)}, u32[]{:S(2)}, u32[]{:S(2)}) collective-permute-start(f32[24]{0:T(128)S(1)} %fusion.6), channel_id=1, source_target_pairs={{0,4},{1,9},{2,14},{3,19},{4,8},{5,13},{6,18},{7,23},{8,12},{9,17}... | collective-permute-start | bytes 296 | tf_op jit(solution)/shard_map/ppermute | solution.py:153
  75.8 26.2 %all-to-all-start = ((f32[256,1,25]{2,1,0:T(1,128)}), f32[256,1,25]{2,1,0:T(1,128)S(1)}, u32[]{:S(2)}, u32[]{:S(2)}) async-start(f32[256,1,25]{2,1,0:T(1,128)} %broadcast_in_dim.29), calls=%async_computation | async-start | bytes 262144 | tf_op jit(solution)/shard_map/all_to_all | solution.py:159

commit v11 on v10

--- a/solution.py
+++ b/solution.py
@@ -98,7 +98,7 @@
     scale = jnp.exp2(top - peak)
     total = jnp.sum(scale * stats[:, :, 1, :], axis=2)
     sums = stats[:, :, 2:5, :] * scale[:, :, None, :]
-    rel = jnp.einsum("lp,abql->abpq", table, sums, precision=HIGH)
+    rel = jnp.sum(jnp.transpose(table)[None, None, :, None, :] * sums[:, :, None, :, :], axis=-1)
     rel = rel / total[:, :, None, None]
     return jnp.transpose(rel, (2, 0, 3, 1)).reshape(3 * count, 3 * count)
 
@@ -132,19 +132,16 @@
     first_half = fetch(images[:half])
     second_src, first_half = lax.optimization_barrier((images[half:], first_half))
     others = [first_half, fetch(second_src)]
-    packed = jnp.concatenate(
-        [partners[0].astype(jnp.float32), counts.astype(jnp.float32), start[0]]
-    )
+    slot_ids = jnp.arange(slots)
+    plus = jnp.any((partners[0] == step + halo - 1) & (slot_ids < counts[0]))
+    own_minus = jnp.any((partners[0] == halo - step) & (slot_ids < counts[0]))
+    packed = jnp.concatenate([start[0], own_minus.astype(jnp.float32)[None]])
     other_packed = fetch(packed)
-    other_partners = other_packed[:slots]
-    other_counts = other_packed[slots]
-    other_start = other_packed[slots + 1 :]
+    minus = other_packed[width] > 0.5
+    other_start = other_packed[:width]
 
     tile = pair_tile(images, others, table)
 
-    slot_ids = jnp.arange(slots)
-    plus = jnp.any((partners[0] == step + halo - 1) & (slot_ids < counts[0]))
-    minus = jnp.any((other_partners == (halo - step).astype(jnp.float32)) & (slot_ids < other_counts))
     col_bits = [1 << b for b in range(ncols.bit_length() - 1)]
 
     def partial(x_own, x_other):

time: 106 us -> 102 us (0.962)
  matrix products: 5.92 us -> 1.82 us
  between operations: 3.53 us -> 4.88 us
  starting transfers between devices: 42.3 us -> 41.1 us
  other arithmetic: 6.16 us -> 5.07 us
    dot_general x1 -> x0, matrix products: 2.68 us -> none  [pair_tile(): rel = jnp.einsum('lp,abql->abpq', table, sums, precision=HIGH)]
    dot_general x2, matrix products: 1.63 us -> 0.26 us  [partial(): backward = jnp.where(minus, jnp.dot(tile.T, x_own, precision=HIGH), 0.0)]
    reduce_or x1 -> x0, other arithmetic: 1.36 us -> none  [body(): jnp.any((other_partners == (halo - step).astype(jnp.float32)) & (slot_ids...]
    ppermute x4, starting transfers between devices: 14.6 us -> 13.3 us  [body(): fetch = lambda v: lax.ppermute(v, axes, route)]
  transfers between devices with their start and end apart: 9 -> 9, of which waited for: 6 -> 6; matrix products, arithmetic and copies ran while one was open for 3% -> 2% of each run, Pallas kernels for 11% -> 12%
where the time goes in v11:
time: 102 us; the launch traced here: 101 us
  starting transfers between devices  41.1 us (40%)
  Pallas kernels  23.5 us (23%)
  waiting for transfers between devices  20.9 us (20%)
  other arithmetic  5.07 us (5%)
  between operations  4.88 us (5%)
  local copies, waits for them, and re-layouts  4.2 us (4%)
  matrix products  1.82 us (2%)
    pallas_call x2, Pallas kernels, pair_stats(): pl.pallas_call(tile_kernel, out_shape=jax.ShapeDtypeStruct((count, part,...  23.5 us
    ppermute x2, starting transfers between devices, butterfly_sum(): value = value + lax.ppermute(value, axes, route)  14.1 us
    all_to_all x1, starting transfers between devices, body(): lax.all_to_all(jnp.broadcast_to(packet, (size, width + 1)), axes, 0, 0, t...  13.4 us
    ppermute x4, starting transfers between devices, body(): fetch = lambda v: lax.ppermute(v, axes, route)  13.3 us
    all_to_all x1, waiting for transfers between devices, body(): lax.all_to_all(jnp.broadcast_to(packet, (size, width + 1)), axes, 0, 0, t...  12.8 us
    ppermute x2, waiting for transfers between devices, partial(): return forward + lax.ppermute(backward, axes, back)  5.92 us
  transfers between devices with their start and end apart: 9, of which 6 were waited for; matrix products, arithmetic and copies ran while one was open for 2% of the time, Pallas kernels for 12%

profile of v11, /device:TPU:1, one launch (start us, length us, event | category | flops | bytes accessed | tf_op | source)
XLA Modules:
  0.0 101.5 jit_solution(34875311474128441)
XLA Ops:
  0.6 1.2 %fusion.25 = (bf16[4,360,128]{2,1,0:T(8,128)(2,1)S(1)}, bf16[4,360,128]{2,1,0:T(8,128)(2,1)S(1)}) fusion(bf16[8,360,128]{2,1,0:T(8,128)(2,1)} %param.4), kind=kLoop, calls=%fused_computation.53 | loop fusion | bytes 1474560 | tf_op jit(solution)/shard_map/slice | solution.py:132
  1.9 3.3 %collective-permute-start = (bf16[4,360,128]{2,1,0:T(8,128)(2,1)S(1)}, bf16[4,360,128]{2,1,0:T(8,128)(2,1)S(1)}, u32[]{:S(2)}, u32[]{:S(2)}) collective-permute-start(bf16[4,360,128]{2,1,0:T(8,128)(2,1)S(1)} %get-tuple-element.15), channel_id=1, source_target_pairs={{4,0},{9,1},{14,2},{19,3},{8,4},{13,5},{18,6},{23,7},{12,8},{17,9}... | collective-permute-start | bytes 1105928 | tf_op jit(solution)/shard_map/ppermute | solution.py:130
  5.8 0.0 copy-start.2
  5.8 0.6 copy-done.2
  6.4 0.7 fusion.15
  7.9 0.0 copy-start.1
  7.9 0.6 copy-done.1
  8.5 0.1 pad_maximum_fusion.1
  8.6 6.0 %collective-permute-start.2 = (f32[25]{0:T(128)S(1)}, f32[25]{0:T(128)S(1)}, u32[]{:S(2)}, u32[]{:S(2)}) collective-permute-start(f32[25]{0:T(128)S(1)} %pad_maximum_fusion.1), channel_id=1, source_target_pairs={{4,0},{9,1},{14,2},{19,3},{8,4},{13,5},{18,6},{23,7},{12,8},{17,9}... | collective-permute-start | bytes 308 | tf_op jit(solution)/shard_map/ppermute | solution.py:130
  14.6 0.0 collective-permute-done
  14.6 1.6 %collective-permute-start.1 = (bf16[4,360,128]{2,1,0:T(8,128)(2,1)S(1)}, bf16[4,360,128]{2,1,0:T(8,128)(2,1)S(1)}, u32[]{:S(2)}, u32[]{:S(2)}) collective-permute-start(bf16[4,360,128]{2,1,0:T(8,128)(2,1)S(1)} %get-tuple-element.5), channel_id=1, source_target_pairs={{4,0},{9,1},{14,2},{19,3},{8,4},{13,5},{18,6},{23,7},{12,8},{17,9}... | collective-permute-start | bytes 1105928 | tf_op jit(solution)/shard_map/ppermute | solution.py:130
  16.2 0.1 fusion.17
  16.3 0.1 multiply_cosine_fusion
  16.4 0.1 pad.4.a_ref
  16.5 0.0 collective-permute-done.2
  16.5 0.6 slice.46
  17.7 0.2 broadcast_in_dim.34.w_ref
  17.9 11.7 %shard_map.59 = f32[8,4,8,384]{3,2,1,0:T(8,128)S(1)} custom-call(bf16[8,384,128]{2,1,0:T(8,128)(2,1)S(1)} %pad.4.a_ref, bf16[1440,128]{1,0:T(8,128)(2,1)S(1)} %bitcast.78, f32[3,360,128]{2,1,0:T(8,128)S(1)} %broadcast_in_dim.34.w_ref), custom_call_target="tpu_custom_call" | custom-call | flops 1185546240 | bytes 2097152 | tf_op jit(solution)/shard_map/pallas_call | solution.py:76
  29.7 11.7 %shard_map.60 = f32[8,4,8,384]{3,2,1,0:T(8,128)S(1)} custom-call(bf16[8,384,128]{2,1,0:T(8,128)(2,1)S(1)} %pad.4.a_ref, bf16[1440,128]{1,0:T(8,128)(2,1)S(1)} %bitcast.79, f32[3,360,128]{2,1,0:T(8,128)S(1)} %broadcast_in_dim.34.w_ref), custom_call_target="tpu_custom_call" | custom-call | flops 1185546240 | bytes 2097152 | tf_op jit(solution)/shard_map/pallas_call | solution.py:76
  41.4 0.3 fusion.23
  41.7 0.1 exponential_bitcast_fusion
  41.8 0.1 fusion.7
  41.9 0.2 multiply_reduce_fusion
  42.1 0.2 fusion.9
  42.3 0.1 reshape.65
  42.4 0.1 fusion.2
  42.5 0.2 collective-permute-start.3
  42.7 5.7 %collective-permute-done.3 = f32[24]{0:T(128)S(1)} collective-permute-done((f32[24]{0:T(128)S(1)}, f32[24]{0:T(128)S(1)}, u32[]{:S(2)}, u32[]{:S(2)}) %collective-permute-start.3) | collective-permute-done | bytes 128 | tf_op jit(solution)/shard_map/ppermute | solution.py:150
  48.4 0.8 fusion.1
  49.2 8.5 %collective-permute-start.4 = (f32[24]{0:T(128)S(1)}, f32[24]{0:T(128)S(1)}, u32[]{:S(2)}, u32[]{:S(2)}) collective-permute-start(f32[24]{0:T(128)S(1)} %fusion.1), channel_id=1, source_target_pairs={{0,1},{1,0},{2,3},{3,2},{4,5},{5,4},{6,7},{7,6},{8,9},{9,8},{10,11... | collective-permute-start | bytes 296 | tf_op jit(solution)/shard_map/ppermute | solution.py:109
  57.7 1.0 collective-permute-done.4
  58.6 5.6 %collective-permute-start.5 = (f32[24]{0:T(128)S(1)}, f32[24]{0:T(128)S(1)}, u32[]{:S(2)}, u32[]{:S(2)}) collective-permute-start(f32[24]{0:T(128)S(1)} %add.47), channel_id=1, source_target_pairs={{0,2},{1,3},{2,0},{3,1},{4,6},{5,7},{6,4},{7,5},{8,10},{9,11},{10,... | collective-permute-start | bytes 296 | tf_op jit(solution)/shard_map/ppermute | solution.py:109
  64.2 1.0 collective-permute-done.5
  65.2 0.6 multiply_reduce_fusion.2
  65.8 0.1 fusion.5
  65.9 2.4 %collective-permute-start.6 = (f32[24]{0:T(128)S(1)}, f32[24]{0:T(128)S(1)}, u32[]{:S(2)}, u32[]{:S(2)}) collective-permute-start(f32[24]{0:T(128)S(1)} %get-tuple-element.11), channel_id=1, source_target_pairs={{4,0},{9,1},{14,2},{19,3},{8,4},{13,5},{18,6},{23,7},{12,8},{17,9}... | collective-permute-start | bytes 296 | tf_op jit(solution)/shard_map/ppermute | solution.py:130
  68.3 0.3 collective-permute-start.7
  69.2 0.2 collective-permute-done.7
  69.4 0.3 collective-permute-done.6
  69.8 0.8 fusion.4
  70.5 0.1 pad_maximum_fusion.2
  70.6 0.7 broadcast_in_dim.39
  71.3 13.4 %all-to-all-start = ((f32[256,1,25]{2,1,0:T(1,128)}), f32[256,1,25]{2,1,0:T(1,128)S(1)}, u32[]{:S(2)}, u32[]{:S(2)}) async-start(f32[256,1,25]{2,1,0:T(1,128)} %broadcast_in_dim.39), calls=%async_computation | async-start | bytes 262144 | tf_op jit(solution)/shard_map/all_to_all | solution.py:156
  84.7 12.8 %all-to-all-done = f32[256,1,25]{2,1,0:T(1,128)S(1)} async-done(((f32[256,1,25]{2,1,0:T(1,128)}), f32[256,1,25]{2,1,0:T(1,128)S(1)}, u32[]{:S(2)}, u32[]{:S(2)}) %all-to-all-start) | async-done | bytes 25632 | tf_op jit(solution)/shard_map/all_to_all | solution.py:156
  97.5 0.8 multiply_reduce_fusion.1
  98.3 0.7 slice_reduce_fusion
  99.7 0.5 divide_bitcast_fusion.2
  101.0 0.5 divide_bitcast_fusion.1
  (8 shorter events, 0.1 us)
Async XLA Ops:
  0.6 15.8 %copy-start = (bf16[8,360,128]{2,1,0:T(8,128)(2,1)S(1)}, bf16[8,360,128]{2,1,0:T(8,128)(2,1)}, u32[]{:S(2)}) copy-start(bf16[8,360,128]{2,1,0:T(8,128)(2,1)} %param.4) | copy-start | bytes 2211844
  1.9 12.8 %collective-permute-start = (bf16[4,360,128]{2,1,0:T(8,128)(2,1)S(1)}, bf16[4,360,128]{2,1,0:T(8,128)(2,1)S(1)}, u32[]{:S(2)}, u32[]{:S(2)}) collective-permute-start(bf16[4,360,128]{2,1,0:T(8,128)(2,1)S(1)} %get-tuple-element.15), channel_id=1, source_target_pairs={{4,0},{9,1},{14,2},{19,3},{8,4},{13,5},{18,6},{23,7},{12,8},{17,9}... | collective-permute-start | bytes 1105928 | tf_op jit(solution)/shard_map/ppermute | solution.py:130
  5.8 0.7 copy-start.2
  7.9 0.7 copy-start.1
  8.6 7.9 %collective-permute-start.2 = (f32[25]{0:T(128)S(1)}, f32[25]{0:T(128)S(1)}, u32[]{:S(2)}, u32[]{:S(2)}) collective-permute-start(f32[25]{0:T(128)S(1)} %pad_maximum_fusion.1), channel_id=1, source_target_pairs={{4,0},{9,1},{14,2},{19,3},{8,4},{13,5},{18,6},{23,7},{12,8},{17,9}... | collective-permute-start | bytes 308 | tf_op jit(solution)/shard_map/ppermute | solution.py:130
  14.6 15.0 %collective-permute-start.1 = (bf16[4,360,128]{2,1,0:T(8,128)(2,1)S(1)}, bf16[4,360,128]{2,1,0:T(8,128)(2,1)S(1)}, u32[]{:S(2)}, u32[]{:S(2)}) collective-permute-start(bf16[4,360,128]{2,1,0:T(8,128)(2,1)S(1)} %get-tuple-element.5), channel_id=1, source_target_pairs={{4,0},{9,1},{14,2},{19,3},{8,4},{13,5},{18,6},{23,7},{12,8},{17,9}... | collective-permute-start | bytes 1105928 | tf_op jit(solution)/shard_map/ppermute | solution.py:130
  42.5 5.9 %collective-permute-start.3 = (f32[24]{0:T(128)S(1)}, f32[24]{0:T(128)S(1)}, u32[]{:S(2)}, u32[]{:S(2)}) collective-permute-start(f32[24]{0:T(128)S(1)} %fusion.2), channel_id=1, source_target_pairs={{0,4},{1,9},{2,14},{3,19},{4,8},{5,13},{6,18},{7,23},{8,12},{9,17}... | collective-permute-start | bytes 296 | tf_op jit(solution)/shard_map/ppermute | solution.py:150
  49.2 9.4 %collective-permute-start.4 = (f32[24]{0:T(128)S(1)}, f32[24]{0:T(128)S(1)}, u32[]{:S(2)}, u32[]{:S(2)}) collective-permute-start(f32[24]{0:T(128)S(1)} %fusion.1), channel_id=1, source_target_pairs={{0,1},{1,0},{2,3},{3,2},{4,5},{5,4},{6,7},{7,6},{8,9},{9,8},{10,11... | collective-permute-start | bytes 296 | tf_op jit(solution)/shard_map/ppermute | solution.py:109
  58.6 6.6 %collective-permute-start.5 = (f32[24]{0:T(128)S(1)}, f32[24]{0:T(128)S(1)}, u32[]{:S(2)}, u32[]{:S(2)}) collective-permute-start(f32[24]{0:T(128)S(1)} %add.47), channel_id=1, source_target_pairs={{0,2},{1,3},{2,0},{3,1},{4,6},{5,7},{6,4},{7,5},{8,10},{9,11},{10,... | collective-permute-start | bytes 296 | tf_op jit(solution)/shard_map/ppermute | solution.py:109
  65.9 3.8 %collective-permute-start.6 = (f32[24]{0:T(128)S(1)}, f32[24]{0:T(128)S(1)}, u32[]{:S(2)}, u32[]{:S(2)}) collective-permute-start(f32[24]{0:T(128)S(1)} %get-tuple-element.11), channel_id=1, source_target_pairs={{4,0},{9,1},{14,2},{19,3},{8,4},{13,5},{18,6},{23,7},{12,8},{17,9}... | collective-permute-start | bytes 296 | tf_op jit(solution)/shard_map/ppermute | solution.py:130
  68.3 1.2 %collective-permute-start.7 = (f32[24]{0:T(128)S(1)}, f32[24]{0:T(128)S(1)}, u32[]{:S(2)}, u32[]{:S(2)}) collective-permute-start(f32[24]{0:T(128)S(1)} %fusion.5), channel_id=1, source_target_pairs={{0,4},{1,9},{2,14},{3,19},{4,8},{5,13},{6,18},{7,23},{8,12},{9,17}... | collective-permute-start | bytes 296 | tf_op jit(solution)/shard_map/ppermute | solution.py:150
  71.3 26.1 %all-to-all-start = ((f32[256,1,25]{2,1,0:T(1,128)}), f32[256,1,25]{2,1,0:T(1,128)S(1)}, u32[]{:S(2)}, u32[]{:S(2)}) async-start(f32[256,1,25]{2,1,0:T(1,128)} %broadcast_in_dim.39), calls=%async_computation | async-start | bytes 262144 | tf_op jit(solution)/shard_map/all_to_all | solution.py:156

commit v12 on v11

--- a/solution.py
+++ b/solution.py
@@ -144,21 +144,25 @@
 
     col_bits = [1 << b for b in range(ncols.bit_length() - 1)]
 
-    def partial(x_own, x_other):
-        forward = jnp.where(plus, jnp.dot(tile, x_other, precision=HIGH), 0.0)
-        backward = jnp.where(minus, jnp.dot(tile.T, x_own, precision=HIGH), 0.0)
-        return forward + lax.ppermute(backward, axes, back)
-
-    y1 = butterfly_sum(partial(start[0], other_start), axes, size, col_bits)
-    z_part = partial(y1, fetch(y1))
+    forward = jnp.where(plus, jnp.dot(tile, other_start, precision=HIGH), 0.0)
+    backward = jnp.where(minus, jnp.dot(tile.T, start[0], precision=HIGH), 0.0)
+    sent = jnp.concatenate([backward, tile.reshape(width * width), plus.astype(jnp.float32)[None]])
+    got = lax.ppermute(sent, axes, back)
+    y1 = butterfly_sum(forward + got[:width], axes, size, col_bits)
+    tile_below = got[width : width + width * width].reshape(width, width)
+    plus_below = got[width + width * width] > 0.5
+    up = jnp.where(minus, jnp.dot(tile.T, y1, precision=HIGH), 0.0)
+    down = jnp.where(plus_below, jnp.dot(tile_below, y1, precision=HIGH), 0.0)
     own_square = jnp.where(lax.axis_index("cols") == 0, jnp.sum(y1 * y1), 0.0)
-    packet = jnp.concatenate([z_part, own_square[None]])
-    gathered = lax.all_to_all(jnp.broadcast_to(packet, (size, width + 1)), axes, 0, 0, tiled=True)
-    gathered = gathered.reshape(nblk, ncols, width + 1)
-    z_all = gathered[:, 0, :width]
+    packet = jnp.concatenate([up, down, own_square[None]])
+    gathered = lax.all_to_all(jnp.broadcast_to(packet, (size, 2 * width + 1)), axes, 0, 0, tiled=True)
+    gathered = gathered.reshape(nblk, ncols, 2 * width + 1)
+    z_all = jnp.roll(gathered[:, 0, :width], 1, axis=0)
     for c in range(1, ncols):
-        z_all = z_all + gathered[:, c, :width]
-    sum_y1 = jnp.sum(gathered[:, :, width])
+        z_all = z_all + jnp.roll(gathered[:, c, :width], c + 1, axis=0)
+    for c in range(ncols):
+        z_all = z_all + jnp.roll(gathered[:, c, width : 2 * width], -(c + 1), axis=0)
+    sum_y1 = jnp.sum(gathered[:, :, 2 * width])
     sum_z = jnp.sum(z_all * z_all)
     z = lax.dynamic_index_in_dim(z_all, lax.axis_index("rows"), 0, keepdims=False)
     entries = float(width * nblk)

time: 102 us -> 96.8 us (0.949)
  starting transfers between devices: 41.1 us -> 34.5 us
  local copies, waits for them, and re-layouts: 4.2 us -> 7.68 us
  waiting for transfers between devices: 20.9 us -> 19.1 us
  between operations: 4.88 us -> 6.14 us
    all_to_all x1, starting transfers between devices: 13.4 us -> 9.31 us  [body(): lax.all_to_all(jnp.broadcast_to(packet, (size, 2 * width + 1)), axes, 0,...]
    slice x0 -> x26, local copies, waits for them, and re-layouts: none -> 2.74 us  [the longest x12 1.1 us: body(): z_all = z_all + jnp.roll(gathered[:, c, :width], c + 1, axis=0)]
    ppermute x4 -> x3, starting transfers between devices: 13.3 us -> 11 us  [body(): fetch = lambda v: lax.ppermute(v, axes, route)]
    ppermute x2, waiting for transfers between devices: 1.91 us -> 0.52 us  [butterfly_sum(): value = value + lax.ppermute(value, axes, route)]
    ppermute x2 -> x1, waiting for transfers between devices: 5.92 us -> 5.8 us  [body(): got = lax.ppermute(sent, axes, back)]
  transfers between devices with their start and end apart: 9 -> 7, of which waited for: 6 -> 4; matrix products, arithmetic and copies ran while one was open for 2% -> 3% of each run, Pallas kernels for 12% -> 12%
where the time goes in v12:
time: 96.8 us; the launch traced here: 96.5 us
  starting transfers between devices  34.5 us (36%)
  Pallas kernels  23.4 us (24%)
  waiting for transfers between devices  19.1 us (20%)
  local copies, waits for them, and re-layouts  7.68 us (8%)
  between operations  6.14 us (6%)
  other arithmetic  4.57 us (5%)
  matrix products  1.16 us (1%)
    pallas_call x2, Pallas kernels, pair_stats(): pl.pallas_call(tile_kernel, out_shape=jax.ShapeDtypeStruct((count, part,...  23.4 us
    ppermute x2, starting transfers between devices, butterfly_sum(): value = value + lax.ppermute(value, axes, route)  14 us
    all_to_all x1, waiting for transfers between devices, body(): lax.all_to_all(jnp.broadcast_to(packet, (size, 2 * width + 1)), axes, 0,...  12.8 us
    ppermute x3, starting transfers between devices, body(): fetch = lambda v: lax.ppermute(v, axes, route)  11 us
    all_to_all x1, starting transfers between devices, body(): lax.all_to_all(jnp.broadcast_to(packet, (size, 2 * width + 1)), axes, 0,...  9.31 us
    ppermute x1, waiting for transfers between devices, body(): got = lax.ppermute(sent, axes, back)  5.8 us
  transfers between devices with their start and end apart: 7, of which 4 were waited for; matrix products, arithmetic and copies ran while one was open for 3% of the time, Pallas kernels for 12%

profile of v12, /device:TPU:1, one launch (start us, length us, event | category | flops | bytes accessed | tf_op | source)
XLA Modules:
  0.0 96.5 jit_solution(8396805670954479202)
XLA Ops:
  0.6 1.2 %fusion.32 = (bf16[4,360,128]{2,1,0:T(8,128)(2,1)S(1)}, bf16[4,360,128]{2,1,0:T(8,128)(2,1)S(1)}) fusion(bf16[8,360,128]{2,1,0:T(8,128)(2,1)} %param.4), kind=kLoop, calls=%fused_computation.59 | loop fusion | bytes 1474560 | tf_op jit(solution)/shard_map/slice | solution.py:132
  1.9 3.3 %collective-permute-start = (bf16[4,360,128]{2,1,0:T(8,128)(2,1)S(1)}, bf16[4,360,128]{2,1,0:T(8,128)(2,1)S(1)}, u32[]{:S(2)}, u32[]{:S(2)}) collective-permute-start(bf16[4,360,128]{2,1,0:T(8,128)(2,1)S(1)} %get-tuple-element.21), channel_id=1, source_target_pairs={{4,0},{9,1},{14,2},{19,3},{8,4},{13,5},{18,6},{23,7},{12,8},{17,9}... | collective-permute-start | bytes 1105928 | tf_op jit(solution)/shard_map/ppermute | solution.py:130
  5.8 0.6 copy-done.2
  6.4 0.7 fusion.18
  7.8 0.6 copy-done.1
  8.5 6.0 %collective-permute-start.2 = (f32[25]{0:T(128)S(1)}, f32[25]{0:T(128)S(1)}, u32[]{:S(2)}, u32[]{:S(2)}) collective-permute-start(f32[25]{0:T(128)S(1)} %pad_maximum_fusion.2), channel_id=1, source_target_pairs={{4,0},{9,1},{14,2},{19,3},{8,4},{13,5},{18,6},{23,7},{12,8},{17,9}... | collective-permute-start | bytes 308 | tf_op jit(solution)/shard_map/ppermute | solution.py:130
  14.5 1.7 %collective-permute-start.1 = (bf16[4,360,128]{2,1,0:T(8,128)(2,1)S(1)}, bf16[4,360,128]{2,1,0:T(8,128)(2,1)S(1)}, u32[]{:S(2)}, u32[]{:S(2)}) collective-permute-start(bf16[4,360,128]{2,1,0:T(8,128)(2,1)S(1)} %get-tuple-element.5), channel_id=1, source_target_pairs={{4,0},{9,1},{14,2},{19,3},{8,4},{13,5},{18,6},{23,7},{12,8},{17,9}... | collective-permute-start | bytes 1105928 | tf_op jit(solution)/shard_map/ppermute | solution.py:130
  16.3 0.1 multiply_cosine_fusion
  17.1 0.6 slice.179
  18.4 0.2 broadcast_in_dim.40.w_ref
  18.6 11.7 %shard_map.59 = f32[8,4,8,384]{3,2,1,0:T(8,128)S(1)} custom-call(bf16[8,384,128]{2,1,0:T(8,128)(2,1)S(1)} %pad.4.a_ref, bf16[1440,128]{1,0:T(8,128)(2,1)S(1)} %bitcast.96, f32[3,360,128]{2,1,0:T(8,128)S(1)} %broadcast_in_dim.40.w_ref), custom_call_target="tpu_custom_call" | custom-call | flops 1185546240 | bytes 2097152 | tf_op jit(solution)/shard_map/pallas_call | solution.py:76
  30.3 11.7 %shard_map.60 = f32[8,4,8,384]{3,2,1,0:T(8,128)S(1)} custom-call(bf16[8,384,128]{2,1,0:T(8,128)(2,1)S(1)} %pad.4.a_ref, bf16[1440,128]{1,0:T(8,128)(2,1)S(1)} %bitcast.97, f32[3,360,128]{2,1,0:T(8,128)S(1)} %broadcast_in_dim.40.w_ref), custom_call_target="tpu_custom_call" | custom-call | flops 1185546240 | bytes 2097152 | tf_op jit(solution)/shard_map/pallas_call | solution.py:76
  42.0 0.3 fusion.30
  42.3 0.1 exponential_bitcast_fusion
  42.4 0.1 fusion.5
  42.5 0.2 multiply_reduce_fusion
  42.7 0.2 fusion.7
  42.9 0.1 reshape.79
  43.0 0.1 reshape_reshape.3
  43.1 0.1 fusion.2
  43.3 0.1 collective-permute-start.3
  43.4 5.8 %collective-permute-done.3 = f32[601]{0:T(1024)S(1)} collective-permute-done((f32[601]{0:T(1024)S(1)}, f32[601]{0:T(1024)S(1)}, u32[]{:S(2)}, u32[]{:S(2)}) %collective-permute-start.3) | collective-permute-done | bytes 2436 | tf_op jit(solution)/shard_map/ppermute | solution.py:150
  49.2 0.8 fusion.1
  50.0 8.5 %collective-permute-start.4 = (f32[24]{0:T(128)S(1)}, f32[24]{0:T(128)S(1)}, u32[]{:S(2)}, u32[]{:S(2)}) collective-permute-start(f32[24]{0:T(128)S(1)} %fusion.1), channel_id=1, source_target_pairs={{0,1},{1,0},{2,3},{3,2},{4,5},{5,4},{6,7},{7,6},{8,9},{9,8},{10,11... | collective-permute-start | bytes 296 | tf_op jit(solution)/shard_map/ppermute | solution.py:109
  58.6 0.6 slice.181
  59.2 0.2 collective-permute-done.4
  59.4 5.6 %collective-permute-start.5 = (f32[24]{0:T(128)S(1)}, f32[24]{0:T(128)S(1)}, u32[]{:S(2)}, u32[]{:S(2)}) collective-permute-start(f32[24]{0:T(128)S(1)} %add.53), channel_id=1, source_target_pairs={{0,2},{1,3},{2,0},{3,1},{4,6},{5,7},{6,4},{7,5},{8,10},{9,11},{10,... | collective-permute-start | bytes 296 | tf_op jit(solution)/shard_map/ppermute | solution.py:109
  65.7 0.3 collective-permute-done.5
  66.0 0.6 multiply_reduce_fusion.2
  66.6 0.1 fusion.3
  66.7 0.1 broadcast_select_fusion
  67.6 0.7 broadcast_in_dim.47
  68.3 9.3 %all-to-all-start = ((f32[256,1,49]{2,1,0:T(1,128)}), f32[256,1,49]{2,1,0:T(1,128)S(1)}, u32[]{:S(2)}, u32[]{:S(2)}) async-start(f32[256,1,49]{2,1,0:T(1,128)} %broadcast_in_dim.47), calls=%async_computation | async-start | bytes 262144 | tf_op jit(solution)/shard_map/all_to_all | solution.py:158
  77.6 12.8 %all-to-all-done = f32[256,1,49]{2,1,0:T(1,128)S(1)} async-done(((f32[256,1,49]{2,1,0:T(1,128)}), f32[256,1,49]{2,1,0:T(1,128)S(1)}, u32[]{:S(2)}, u32[]{:S(2)}) %all-to-all-start) | async-done | bytes 50208 | tf_op jit(solution)/shard_map/all_to_all | solution.py:158
  90.4 0.1 fusion.33
  90.5 0.1 fusion.35
  90.7 0.1 fusion.37
  90.8 0.1 fusion.39
  91.2 0.7 slice_reduce_fusion
  92.7 0.5 divide_bitcast_fusion.1
  93.9 0.1 copy.154
  93.9 0.1 copy.156
  94.0 0.1 copy.157
  94.1 0.1 copy.142
  94.2 0.1 copy.150
  94.4 0.1 copy.148
  94.5 0.7 multiply_reduce_fusion.1
  96.0 0.6 copy.155
  (34 shorter events, 1.7 us)
Async XLA Ops:
  0.6 15.6 %copy-start = (bf16[8,360,128]{2,1,0:T(8,128)(2,1)S(1)}, bf16[8,360,128]{2,1,0:T(8,128)(2,1)}, u32[]{:S(2)}) copy-start(bf16[8,360,128]{2,1,0:T(8,128)(2,1)} %param.4) | copy-start | bytes 2211844
  1.9 12.7 %collective-permute-start = (bf16[4,360,128]{2,1,0:T(8,128)(2,1)S(1)}, bf16[4,360,128]{2,1,0:T(8,128)(2,1)S(1)}, u32[]{:S(2)}, u32[]{:S(2)}) collective-permute-start(bf16[4,360,128]{2,1,0:T(8,128)(2,1)S(1)} %get-tuple-element.21), channel_id=1, source_target_pairs={{4,0},{9,1},{14,2},{19,3},{8,4},{13,5},{18,6},{23,7},{12,8},{17,9}... | collective-permute-start | bytes 1105928 | tf_op jit(solution)/shard_map/ppermute | solution.py:130
  5.8 0.7 copy-start.2
  7.8 0.7 copy-start.1
  8.5 8.6 %collective-permute-start.2 = (f32[25]{0:T(128)S(1)}, f32[25]{0:T(128)S(1)}, u32[]{:S(2)}, u32[]{:S(2)}) collective-permute-start(f32[25]{0:T(128)S(1)} %pad_maximum_fusion.2), channel_id=1, source_target_pairs={{4,0},{9,1},{14,2},{19,3},{8,4},{13,5},{18,6},{23,7},{12,8},{17,9}... | collective-permute-start | bytes 308 | tf_op jit(solution)/shard_map/ppermute | solution.py:130
  14.5 15.7 %collective-permute-start.1 = (bf16[4,360,128]{2,1,0:T(8,128)(2,1)S(1)}, bf16[4,360,128]{2,1,0:T(8,128)(2,1)S(1)}, u32[]{:S(2)}, u32[]{:S(2)}) collective-permute-start(bf16[4,360,128]{2,1,0:T(8,128)(2,1)S(1)} %get-tuple-element.5), channel_id=1, source_target_pairs={{4,0},{9,1},{14,2},{19,3},{8,4},{13,5},{18,6},{23,7},{12,8},{17,9}... | collective-permute-start | bytes 1105928 | tf_op jit(solution)/shard_map/ppermute | solution.py:130
  43.3 5.9 %collective-permute-start.3 = (f32[601]{0:T(1024)S(1)}, f32[601]{0:T(1024)S(1)}, u32[]{:S(2)}, u32[]{:S(2)}) collective-permute-start(f32[601]{0:T(1024)S(1)} %pad_maximum_fusion.1), channel_id=1, source_target_pairs={{0,4},{1,9},{2,14},{3,19},{4,8},{5,13},{6,18},{7,23},{8,12},{9,17}... | collective-permute-start | bytes 7220 | tf_op jit(solution)/shard_map/ppermute | solution.py:150
  50.0 9.4 %collective-permute-start.4 = (f32[24]{0:T(128)S(1)}, f32[24]{0:T(128)S(1)}, u32[]{:S(2)}, u32[]{:S(2)}) collective-permute-start(f32[24]{0:T(128)S(1)} %fusion.1), channel_id=1, source_target_pairs={{0,1},{1,0},{2,3},{3,2},{4,5},{5,4},{6,7},{7,6},{8,9},{9,8},{10,11... | collective-permute-start | bytes 296 | tf_op jit(solution)/shard_map/ppermute | solution.py:109
  59.4 6.5 %collective-permute-start.5 = (f32[24]{0:T(128)S(1)}, f32[24]{0:T(128)S(1)}, u32[]{:S(2)}, u32[]{:S(2)}) collective-permute-start(f32[24]{0:T(128)S(1)} %add.53), channel_id=1, source_target_pairs={{0,2},{1,3},{2,0},{3,1},{4,6},{5,7},{6,4},{7,5},{8,10},{9,11},{10,... | collective-permute-start | bytes 296 | tf_op jit(solution)/shard_map/ppermute | solution.py:109
  68.3 22.1 %all-to-all-start = ((f32[256,1,49]{2,1,0:T(1,128)}), f32[256,1,49]{2,1,0:T(1,128)S(1)}, u32[]{:S(2)}, u32[]{:S(2)}) async-start(f32[256,1,49]{2,1,0:T(1,128)} %broadcast_in_dim.47), calls=%async_computation | async-start | bytes 262144 | tf_op jit(solution)/shard_map/all_to_all | solution.py:158

commit v13 on v12

--- a/solution.py
+++ b/solution.py
@@ -128,10 +128,7 @@
             route.append((((i + c + 1) % nblk) * ncols + c, i * ncols + c))
     back = [(dst, src) for src, dst in route]
     fetch = lambda v: lax.ppermute(v, axes, route)
-    half = count // 2
-    first_half = fetch(images[:half])
-    second_src, first_half = lax.optimization_barrier((images[half:], first_half))
-    others = [first_half, fetch(second_src)]
+    others = [fetch(images)]
     slot_ids = jnp.arange(slots)
     plus = jnp.any((partners[0] == step + halo - 1) & (slot_ids < counts[0]))
     own_minus = jnp.any((partners[0] == halo - step) & (slot_ids < counts[0]))

time: 96.8 us -> 98.6 us (1.019)
  starting transfers between devices: 34.5 us -> 38.9 us
  Pallas kernels: 23.4 us -> 22 us
  waiting for transfers between devices: 19.1 us -> 17.8 us
    ppermute x2, starting transfers between devices: 14 us -> 18.2 us  [butterfly_sum(): value = value + lax.ppermute(value, axes, route)]
    all_to_all x1, starting transfers between devices: 9.31 us -> 11.4 us  [body(): lax.all_to_all(jnp.broadcast_to(packet, (size, 2 * width + 1)), axes, 0,...]
    ppermute x3 -> x2, starting transfers between devices: 11 us -> 9.32 us  [body(): fetch = lambda v: lax.ppermute(v, axes, route)]
    pallas_call x2 -> x1, Pallas kernels: 23.4 us -> 22 us  [pair_stats(): pl.pallas_call(tile_kernel, out_shape=jax.ShapeDtypeStruct((count, part,...]
    ppermute x1, waiting for transfers between devices: 5.8 us -> 4.45 us  [body(): got = lax.ppermute(sent, axes, back)]
    slice x1 -> x0, local copies, waits for them, and re-layouts: 1.22 us -> none  [body(): first_half = fetch(images[:half])]
    pad x1, local copies, waits for them, and re-layouts: 0.06 us -> 1.17 us  [pair_tile(): own_p = jnp.pad(own, ((0, 0), (0, padded - lines), (0, 0)))]
  transfers between devices with their start and end apart: 7 -> 6, of which waited for: 4 -> 4; matrix products, arithmetic and copies ran while one was open for 3% -> 4% of each run, Pallas kernels for 12% -> 0%
where the time goes in v13:
time: 98.6 us; the launch traced here: 98.3 us
  starting transfers between devices  38.9 us (39%)
  Pallas kernels  22 us (22%)
  waiting for transfers between devices  17.8 us (18%)
  local copies, waits for them, and re-layouts  7.57 us (8%)
  between operations  6.18 us (6%)
  other arithmetic  4.61 us (5%)
  matrix products  1.22 us (1%)
    pallas_call x1, Pallas kernels, pair_stats(): pl.pallas_call(tile_kernel, out_shape=jax.ShapeDtypeStruct((count, part,...  22 us
    ppermute x2, starting transfers between devices, butterfly_sum(): value = value + lax.ppermute(value, axes, route)  18.2 us
    all_to_all x1, waiting for transfers between devices, body(): lax.all_to_all(jnp.broadcast_to(packet, (size, 2 * width + 1)), axes, 0,...  12.8 us
    all_to_all x1, starting transfers between devices, body(): lax.all_to_all(jnp.broadcast_to(packet, (size, 2 * width + 1)), axes, 0,...  11.4 us
    ppermute x2, starting transfers between devices, body(): fetch = lambda v: lax.ppermute(v, axes, route)  9.32 us
    ppermute x1, waiting for transfers between devices, body(): got = lax.ppermute(sent, axes, back)  4.45 us
  transfers between devices with their start and end apart: 6, of which 4 were waited for; matrix products, arithmetic and copies ran while one was open for 4% of the time, Pallas kernels for 0%

profile of v13, /device:TPU:1, one launch (start us, length us, event | category | flops | bytes accessed | tf_op | source)
XLA Modules:
  0.0 98.3 jit_solution(14795329647266728006)
XLA Ops:
  0.6 3.3 %collective-permute-start = (bf16[8,360,128]{2,1,0:T(8,128)(2,1)}, bf16[8,360,128]{2,1,0:T(8,128)(2,1)S(1)}, u32[]{:S(2)}, u32[]{:S(2)}) collective-permute-start(bf16[8,360,128]{2,1,0:T(8,128)(2,1)} %param.4), channel_id=1, source_target_pairs={{4,0},{9,1},{14,2},{19,3},{8,4},{13,5},{18,6},{23,7},{12,8},{17,9}... | collective-permute-start | bytes 2211848 | tf_op jit(solution)/shard_map/ppermute | solution.py:130
  4.6 0.6 copy-done.1
  5.2 0.7 fusion.15
  6.6 0.6 copy-done
  7.3 6.0 %collective-permute-start.1 = (f32[25]{0:T(128)S(1)}, f32[25]{0:T(128)S(1)}, u32[]{:S(2)}, u32[]{:S(2)}) collective-permute-start(f32[25]{0:T(128)S(1)} %pad_maximum_fusion.1), channel_id=1, source_target_pairs={{4,0},{9,1},{14,2},{19,3},{8,4},{13,5},{18,6},{23,7},{12,8},{17,9}... | collective-permute-start | bytes 308 | tf_op jit(solution)/shard_map/ppermute | solution.py:130
  13.4 1.2 %pad.4.a_ref = bf16[8,384,128]{2,1,0:T(8,128)(2,1)S(1)} pad(bf16[8,360,128]{2,1,0:T(8,128)(2,1)} %param.4, bf16[]{:T(256)} %constant.39.clone.1), padding=0_0x0_24x0_0 | pad | bytes 1523714 | tf_op jit(solution)/shard_map/jit(_pad)/pad | solution.py:92
  14.6 0.1 multiply_cosine_fusion
  15.4 0.6 slice.171
  16.7 0.2 broadcast_in_dim.40.w_ref
  16.9 22.0 %shard_map.59 = f32[8,8,8,384]{3,2,1,0:T(8,128)S(1)} custom-call(bf16[8,384,128]{2,1,0:T(8,128)(2,1)S(1)} %pad.4.a_ref, bf16[2880,128]{1,0:T(8,128)(2,1)S(1)} %bitcast.95, f32[3,360,128]{2,1,0:T(8,128)S(1)} %broadcast_in_dim.40.w_ref), custom_call_target="tpu_custom_call" | custom-call | flops 2371092480 | bytes 2097152 | tf_op jit(solution)/shard_map/pallas_call | solution.py:76
  38.9 0.3 fusion.27
  39.2 0.1 exponential_bitcast_fusion
  39.3 0.1 slice_multiply_fusion
  39.4 0.2 multiply_reduce_fusion
  39.6 0.2 fusion.4
  39.8 0.1 reshape.75
  39.9 0.1 reshape_reshape.3
  40.0 0.1 fusion.2
  40.1 0.1 pad_maximum_fusion
  40.3 4.5 %collective-permute-done.2 = f32[601]{0:T(1024)S(1)} collective-permute-done((f32[601]{0:T(1024)S(1)}, f32[601]{0:T(1024)S(1)}, u32[]{:S(2)}, u32[]{:S(2)}) %collective-permute-start.2) | collective-permute-done | bytes 2436 | tf_op jit(solution)/shard_map/ppermute | solution.py:147
  44.7 0.8 fusion.1
  45.5 12.8 %collective-permute-start.3 = (f32[24]{0:T(128)S(1)}, f32[24]{0:T(128)S(1)}, u32[]{:S(2)}, u32[]{:S(2)}) collective-permute-start(f32[24]{0:T(128)S(1)} %fusion.1), channel_id=1, source_target_pairs={{0,1},{1,0},{2,3},{3,2},{4,5},{5,4},{6,7},{7,6},{8,9},{9,8},{10,11... | collective-permute-start | bytes 296 | tf_op jit(solution)/shard_map/ppermute | solution.py:109
  58.5 0.6 slice.173
  59.1 0.2 collective-permute-done.3
  59.3 5.5 %collective-permute-start.4 = (f32[24]{0:T(128)S(1)}, f32[24]{0:T(128)S(1)}, u32[]{:S(2)}, u32[]{:S(2)}) collective-permute-start(f32[24]{0:T(128)S(1)} %add.53), channel_id=1, source_target_pairs={{0,2},{1,3},{2,0},{3,1},{4,6},{5,7},{6,4},{7,5},{8,10},{9,11},{10,... | collective-permute-start | bytes 296 | tf_op jit(solution)/shard_map/ppermute | solution.py:109
  65.4 0.3 collective-permute-done.4
  65.7 0.6 multiply_reduce_fusion.2
  66.3 0.1 fusion.3
  66.4 0.1 broadcast_select_fusion
  67.3 0.7 broadcast_in_dim.47
  68.0 11.4 %all-to-all-start = ((f32[256,1,49]{2,1,0:T(1,128)}), f32[256,1,49]{2,1,0:T(1,128)S(1)}, u32[]{:S(2)}, u32[]{:S(2)}) async-start(f32[256,1,49]{2,1,0:T(1,128)} %broadcast_in_dim.47), calls=%async_computation | async-start | bytes 262144 | tf_op jit(solution)/shard_map/all_to_all | solution.py:155
  79.4 12.8 %all-to-all-done = f32[256,1,49]{2,1,0:T(1,128)S(1)} async-done(((f32[256,1,49]{2,1,0:T(1,128)}), f32[256,1,49]{2,1,0:T(1,128)S(1)}, u32[]{:S(2)}, u32[]{:S(2)}) %all-to-all-start) | async-done | bytes 50208 | tf_op jit(solution)/shard_map/all_to_all | solution.py:155
  92.2 0.1 fusion.28
  92.3 0.1 fusion.30
  92.4 0.1 fusion.32
  92.6 0.1 fusion.34
  93.0 0.7 slice_reduce_fusion
  94.4 0.5 divide_bitcast_fusion.1
  95.5 0.1 copy.146
  95.6 0.1 copy.154
  95.7 0.1 copy.156
  95.8 0.1 copy.157
  95.9 0.1 copy.142
  96.0 0.1 copy.150
  96.1 0.1 copy.140
  96.1 0.1 copy.148
  96.2 0.7 multiply_reduce_fusion.1
  97.7 0.6 copy.155
  (28 shorter events, 1.4 us)
Async XLA Ops:
  0.6 16.0 %collective-permute-start = (bf16[8,360,128]{2,1,0:T(8,128)(2,1)}, bf16[8,360,128]{2,1,0:T(8,128)(2,1)S(1)}, u32[]{:S(2)}, u32[]{:S(2)}) collective-permute-start(bf16[8,360,128]{2,1,0:T(8,128)(2,1)} %param.4), channel_id=1, source_target_pairs={{4,0},{9,1},{14,2},{19,3},{8,4},{13,5},{18,6},{23,7},{12,8},{17,9}... | collective-permute-start | bytes 2211848 | tf_op jit(solution)/shard_map/ppermute | solution.py:130
  4.6 0.7 copy-start.1
  6.6 0.7 copy-start
  7.3 8.1 %collective-permute-start.1 = (f32[25]{0:T(128)S(1)}, f32[25]{0:T(128)S(1)}, u32[]{:S(2)}, u32[]{:S(2)}) collective-permute-start(f32[25]{0:T(128)S(1)} %pad_maximum_fusion.1), channel_id=1, source_target_pairs={{4,0},{9,1},{14,2},{19,3},{8,4},{13,5},{18,6},{23,7},{12,8},{17,9}... | collective-permute-start | bytes 308 | tf_op jit(solution)/shard_map/ppermute | solution.py:130
  40.2 4.5 %collective-permute-start.2 = (f32[601]{0:T(1024)S(1)}, f32[601]{0:T(1024)S(1)}, u32[]{:S(2)}, u32[]{:S(2)}) collective-permute-start(f32[601]{0:T(1024)S(1)} %pad_maximum_fusion), channel_id=1, source_target_pairs={{0,4},{1,9},{2,14},{3,19},{4,8},{5,13},{6,18},{7,23},{8,12},{9,17}... | collective-permute-start | bytes 7220 | tf_op jit(solution)/shard_map/ppermute | solution.py:147
  45.5 13.7 %collective-permute-start.3 = (f32[24]{0:T(128)S(1)}, f32[24]{0:T(128)S(1)}, u32[]{:S(2)}, u32[]{:S(2)}) collective-permute-start(f32[24]{0:T(128)S(1)} %fusion.1), channel_id=1, source_target_pairs={{0,1},{1,0},{2,3},{3,2},{4,5},{5,4},{6,7},{7,6},{8,9},{9,8},{10,11... | collective-permute-start | bytes 296 | tf_op jit(solution)/shard_map/ppermute | solution.py:109
  59.3 6.4 %collective-permute-start.4 = (f32[24]{0:T(128)S(1)}, f32[24]{0:T(128)S(1)}, u32[]{:S(2)}, u32[]{:S(2)}) collective-permute-start(f32[24]{0:T(128)S(1)} %add.53), channel_id=1, source_target_pairs={{0,2},{1,3},{2,0},{3,1},{4,6},{5,7},{6,4},{7,5},{8,10},{9,11},{10,... | collective-permute-start | bytes 296 | tf_op jit(solution)/shard_map/ppermute | solution.py:109
  68.0 24.1 %all-to-all-start = ((f32[256,1,49]{2,1,0:T(1,128)}), f32[256,1,49]{2,1,0:T(1,128)S(1)}, u32[]{:S(2)}, u32[]{:S(2)}) async-start(f32[256,1,49]{2,1,0:T(1,128)} %broadcast_in_dim.47), calls=%async_computation | async-start | bytes 262144 | tf_op jit(solution)/shard_map/all_to_all | solution.py:155

commit v14 on v12

--- a/solution.py
+++ b/solution.py
@@ -148,7 +148,10 @@
     backward = jnp.where(minus, jnp.dot(tile.T, start[0], precision=HIGH), 0.0)
     sent = jnp.concatenate([backward, tile.reshape(width * width), plus.astype(jnp.float32)[None]])
     got = lax.ppermute(sent, axes, back)
-    y1 = butterfly_sum(forward + got[:width], axes, size, col_bits)
+    parts = lax.all_to_all(jnp.broadcast_to(forward + got[:width], (ncols, width)), "cols", 0, 0, tiled=True)
+    y1 = parts[0]
+    for c in range(1, ncols):
+        y1 = y1 + parts[c]
     tile_below = got[width : width + width * width].reshape(width, width)
     plus_below = got[width + width * width] > 0.5
     up = jnp.where(minus, jnp.dot(tile.T, y1, precision=HIGH), 0.0)

time: 96.8 us -> 97.6 us (level)
  waiting for transfers between devices: 19.1 us -> 21.3 us
  starting transfers between devices: 34.5 us -> 32.4 us
    ppermute x2 -> x0, starting transfers between devices: 14 us -> none  [butterfly_sum(): value = value + lax.ppermute(value, axes, route)]
    all_to_all x0 -> x1, starting transfers between devices: none -> 13.8 us  [body(): lax.all_to_all(jnp.broadcast_to(forward + got[:width], (ncols, width)), '...]
    all_to_all x0 -> x1, waiting for transfers between devices: none -> 2.59 us  [body(): lax.all_to_all(jnp.broadcast_to(forward + got[:width], (ncols, width)), '...]
    all_to_all x1, starting transfers between devices: 9.31 us -> 7.46 us  [body(): lax.all_to_all(jnp.broadcast_to(packet, (size, 2 * width + 1)), axes, 0,...]
  transfers between devices with their start and end apart: 7 -> 6, of which waited for: 4 -> 3; matrix products, arithmetic and copies ran while one was open for 3% -> 3% of each run, Pallas kernels for 12% -> 12%
where the time goes in v14:
time: 97.6 us; the launch traced here: 97.3 us
  starting transfers between devices  32.4 us (33%)
  Pallas kernels  23.4 us (24%)
  waiting for transfers between devices  21.3 us (22%)
  local copies, waits for them, and re-layouts  8.26 us (8%)
  between operations  6.14 us (6%)
  other arithmetic  4.57 us (5%)
  matrix products  1.16 us (1%)
    pallas_call x2, Pallas kernels, pair_stats(): pl.pallas_call(tile_kernel, out_shape=jax.ShapeDtypeStruct((count, part,...  23.4 us
    all_to_all x1, starting transfers between devices, body(): lax.all_to_all(jnp.broadcast_to(forward + got[:width], (ncols, width)), '...  13.8 us
    all_to_all x1, waiting for transfers between devices, body(): lax.all_to_all(jnp.broadcast_to(packet, (size, 2 * width + 1)), axes, 0,...  12.9 us
    ppermute x3, starting transfers between devices, body(): fetch = lambda v: lax.ppermute(v, axes, route)  11 us
    all_to_all x1, starting transfers between devices, body(): lax.all_to_all(jnp.broadcast_to(packet, (size, 2 * width + 1)), axes, 0,...  7.46 us
    ppermute x1, waiting for transfers between devices, body(): got = lax.ppermute(sent, axes, back)  5.8 us
    all_to_all x1, waiting for transfers between devices, body(): lax.all_to_all(jnp.broadcast_to(forward + got[:width], (ncols, width)), '...  2.59 us
  transfers between devices with their start and end apart: 6, of which 3 were waited for; matrix products, arithmetic and copies ran while one was open for 3% of the time, Pallas kernels for 12%

profile of v14, /device:TPU:1, one launch (start us, length us, event | category | flops | bytes accessed | tf_op | source)
XLA Modules:
  0.0 97.3 jit_solution(4024685438520958454)
XLA Ops:
  0.6 1.2 %fusion.33 = (bf16[4,360,128]{2,1,0:T(8,128)(2,1)S(1)}, bf16[4,360,128]{2,1,0:T(8,128)(2,1)S(1)}) fusion(bf16[8,360,128]{2,1,0:T(8,128)(2,1)} %param.4), kind=kLoop, calls=%fused_computation.63 | loop fusion | bytes 1474560 | tf_op jit(solution)/shard_map/slice | solution.py:132
  1.9 3.3 %collective-permute-start = (bf16[4,360,128]{2,1,0:T(8,128)(2,1)S(1)}, bf16[4,360,128]{2,1,0:T(8,128)(2,1)S(1)}, u32[]{:S(2)}, u32[]{:S(2)}) collective-permute-start(bf16[4,360,128]{2,1,0:T(8,128)(2,1)S(1)} %get-tuple-element.21), channel_id=1, source_target_pairs={{4,0},{9,1},{14,2},{19,3},{8,4},{13,5},{18,6},{23,7},{12,8},{17,9}... | collective-permute-start | bytes 1105928 | tf_op jit(solution)/shard_map/ppermute | solution.py:130
  5.8 0.6 copy-done.2
  6.4 0.7 fusion.18
  7.8 0.6 copy-done.1
  8.5 6.0 %collective-permute-start.2 = (f32[25]{0:T(128)S(1)}, f32[25]{0:T(128)S(1)}, u32[]{:S(2)}, u32[]{:S(2)}) collective-permute-start(f32[25]{0:T(128)S(1)} %pad_maximum_fusion.2), channel_id=1, source_target_pairs={{4,0},{9,1},{14,2},{19,3},{8,4},{13,5},{18,6},{23,7},{12,8},{17,9}... | collective-permute-start | bytes 308 | tf_op jit(solution)/shard_map/ppermute | solution.py:130
  14.5 1.7 %collective-permute-start.1 = (bf16[4,360,128]{2,1,0:T(8,128)(2,1)S(1)}, bf16[4,360,128]{2,1,0:T(8,128)(2,1)S(1)}, u32[]{:S(2)}, u32[]{:S(2)}) collective-permute-start(bf16[4,360,128]{2,1,0:T(8,128)(2,1)S(1)} %get-tuple-element.5), channel_id=1, source_target_pairs={{4,0},{9,1},{14,2},{19,3},{8,4},{13,5},{18,6},{23,7},{12,8},{17,9}... | collective-permute-start | bytes 1105928 | tf_op jit(solution)/shard_map/ppermute | solution.py:130
  16.3 0.1 multiply_cosine_fusion
  17.1 0.6 slice.195
  18.4 0.2 broadcast_in_dim.41.w_ref
  18.6 11.7 %shard_map.59 = f32[8,4,8,384]{3,2,1,0:T(8,128)S(1)} custom-call(bf16[8,384,128]{2,1,0:T(8,128)(2,1)S(1)} %pad.4.a_ref, bf16[1440,128]{1,0:T(8,128)(2,1)S(1)} %bitcast.101, f32[3,360,128]{2,1,0:T(8,128)S(1)} %broadcast_in_dim.41.w_ref), custom_call_target="tpu_custom_call" | custom-call | flops 1185546240 | bytes 2097152 | tf_op jit(solution)/shard_map/pallas_call | solution.py:76
  30.3 11.7 %shard_map.60 = f32[8,4,8,384]{3,2,1,0:T(8,128)S(1)} custom-call(bf16[8,384,128]{2,1,0:T(8,128)(2,1)S(1)} %pad.4.a_ref, bf16[1440,128]{1,0:T(8,128)(2,1)S(1)} %bitcast.102, f32[3,360,128]{2,1,0:T(8,128)S(1)} %broadcast_in_dim.41.w_ref), custom_call_target="tpu_custom_call" | custom-call | flops 1185546240 | bytes 2097152 | tf_op jit(solution)/shard_map/pallas_call | solution.py:76
  42.0 0.3 fusion.31
  42.3 0.1 exponential_bitcast_fusion
  42.4 0.1 fusion.5
  42.5 0.2 multiply_reduce_fusion
  42.7 0.2 fusion.7
  42.9 0.1 reshape.145
  43.0 0.1 reshape_reshape.3
  43.1 0.1 fusion.2
  43.3 0.1 collective-permute-start.3
  43.4 5.8 %collective-permute-done.3 = f32[601]{0:T(1024)S(1)} collective-permute-done((f32[601]{0:T(1024)S(1)}, f32[601]{0:T(1024)S(1)}, u32[]{:S(2)}, u32[]{:S(2)}) %collective-permute-start.3) | collective-permute-done | bytes 2436 | tf_op jit(solution)/shard_map/ppermute | solution.py:150
  49.2 0.8 fusion.1
  50.0 0.6 broadcast_in_dim.47
  50.6 13.8 %all-to-all-start = ((f32[4,1,24]{2,1,0:T(1,128)}), f32[4,1,24]{2,1,0:T(1,128)S(1)}, u32[]{:S(2)}, u32[]{:S(2)}) async-start(f32[4,1,24]{2,1,0:T(1,128)} %broadcast_in_dim.47), calls=%async_computation | async-start | bytes 4096 | tf_op jit(solution)/shard_map/all_to_all | solution.py:151
  64.6 0.6 slice.201
  65.8 2.6 %all-to-all-done = f32[4,1,24]{2,1,0:T(1,128)S(1)} async-done(((f32[4,1,24]{2,1,0:T(1,128)}), f32[4,1,24]{2,1,0:T(1,128)S(1)}, u32[]{:S(2)}, u32[]{:S(2)}) %all-to-all-start) | async-done | bytes 416 | tf_op jit(solution)/shard_map/all_to_all | solution.py:151
  68.4 0.6 fusion.26
  69.0 0.1 fusion.3
  69.1 0.1 broadcast_select_fusion
  70.0 0.7 broadcast_in_dim.49
  70.7 7.5 %all-to-all-start.1 = ((f32[256,1,49]{2,1,0:T(1,128)}), f32[256,1,49]{2,1,0:T(1,128)S(1)}, u32[]{:S(2)}, u32[]{:S(2)}) async-start(f32[256,1,49]{2,1,0:T(1,128)} %broadcast_in_dim.49), calls=%async_computation.1 | async-start | bytes 262144 | tf_op jit(solution)/shard_map/all_to_all | solution.py:161
  78.2 12.9 %all-to-all-done.1 = f32[256,1,49]{2,1,0:T(1,128)S(1)} async-done(((f32[256,1,49]{2,1,0:T(1,128)}), f32[256,1,49]{2,1,0:T(1,128)S(1)}, u32[]{:S(2)}, u32[]{:S(2)}) %all-to-all-start.1) | async-done | bytes 50208 | tf_op jit(solution)/shard_map/all_to_all | solution.py:161
  91.1 0.1 fusion.34
  91.2 0.1 fusion.36
  91.4 0.1 fusion.38
  91.5 0.1 fusion.40
  92.0 0.7 slice_reduce_fusion
  93.4 0.5 divide_bitcast_fusion.1
  94.5 0.1 copy.146
  94.6 0.1 copy.154
  94.7 0.1 copy.156
  94.8 0.1 copy.157
  94.8 0.1 copy.142
  95.0 0.1 copy.140
  95.1 0.1 copy.148
  95.2 0.7 multiply_reduce_fusion.1
  96.7 0.6 copy.155
  (32 shorter events, 1.6 us)
Async XLA Ops:
  0.6 15.6 %copy-start = (bf16[8,360,128]{2,1,0:T(8,128)(2,1)S(1)}, bf16[8,360,128]{2,1,0:T(8,128)(2,1)}, u32[]{:S(2)}) copy-start(bf16[8,360,128]{2,1,0:T(8,128)(2,1)} %param.4) | copy-start | bytes 2211844
  1.9 12.7 %collective-permute-start = (bf16[4,360,128]{2,1,0:T(8,128)(2,1)S(1)}, bf16[4,360,128]{2,1,0:T(8,128)(2,1)S(1)}, u32[]{:S(2)}, u32[]{:S(2)}) collective-permute-start(bf16[4,360,128]{2,1,0:T(8,128)(2,1)S(1)} %get-tuple-element.21), channel_id=1, source_target_pairs={{4,0},{9,1},{14,2},{19,3},{8,4},{13,5},{18,6},{23,7},{12,8},{17,9}... | collective-permute-start | bytes 1105928 | tf_op jit(solution)/shard_map/ppermute | solution.py:130
  5.8 0.7 copy-start.2
  7.8 0.7 copy-start.1
  8.5 8.6 %collective-permute-start.2 = (f32[25]{0:T(128)S(1)}, f32[25]{0:T(128)S(1)}, u32[]{:S(2)}, u32[]{:S(2)}) collective-permute-start(f32[25]{0:T(128)S(1)} %pad_maximum_fusion.2), channel_id=1, source_target_pairs={{4,0},{9,1},{14,2},{19,3},{8,4},{13,5},{18,6},{23,7},{12,8},{17,9}... | collective-permute-start | bytes 308 | tf_op jit(solution)/shard_map/ppermute | solution.py:130
  14.5 15.7 %collective-permute-start.1 = (bf16[4,360,128]{2,1,0:T(8,128)(2,1)S(1)}, bf16[4,360,128]{2,1,0:T(8,128)(2,1)S(1)}, u32[]{:S(2)}, u32[]{:S(2)}) collective-permute-start(bf16[4,360,128]{2,1,0:T(8,128)(2,1)S(1)} %get-tuple-element.5), channel_id=1, source_target_pairs={{4,0},{9,1},{14,2},{19,3},{8,4},{13,5},{18,6},{23,7},{12,8},{17,9}... | collective-permute-start | bytes 1105928 | tf_op jit(solution)/shard_map/ppermute | solution.py:130
  43.3 5.9 %collective-permute-start.3 = (f32[601]{0:T(1024)S(1)}, f32[601]{0:T(1024)S(1)}, u32[]{:S(2)}, u32[]{:S(2)}) collective-permute-start(f32[601]{0:T(1024)S(1)} %pad_maximum_fusion.1), channel_id=1, source_target_pairs={{0,4},{1,9},{2,14},{3,19},{4,8},{5,13},{6,18},{7,23},{8,12},{9,17}... | collective-permute-start | bytes 7220 | tf_op jit(solution)/shard_map/ppermute | solution.py:150
  50.6 17.8 %all-to-all-start = ((f32[4,1,24]{2,1,0:T(1,128)}), f32[4,1,24]{2,1,0:T(1,128)S(1)}, u32[]{:S(2)}, u32[]{:S(2)}) async-start(f32[4,1,24]{2,1,0:T(1,128)} %broadcast_in_dim.47), calls=%async_computation | async-start | bytes 4096 | tf_op jit(solution)/shard_map/all_to_all | solution.py:151
  70.7 20.4 %all-to-all-start.1 = ((f32[256,1,49]{2,1,0:T(1,128)}), f32[256,1,49]{2,1,0:T(1,128)S(1)}, u32[]{:S(2)}, u32[]{:S(2)}) async-start(f32[256,1,49]{2,1,0:T(1,128)} %broadcast_in_dim.49), calls=%async_computation.1 | async-start | bytes 262144 | tf_op jit(solution)/shard_map/all_to_all | solution.py:161
